TPU v7x, 256 devices: a whole 4x4x8 slice. The times are simulated.
256 devices in a mesh: seq: 64 (over x, z_lo, y, core), mp: 4 (over z_hi).
Axes of the slice: x: 4, y: 4, z: 8 (z_hi: 4, z_lo: 2; z = z_hi * 2 + z_lo), core: 2. Of those that a mesh axis runs over, the one named last changes fastest.
Arguments:
- tokens: bfloat16 [8192, 4096], P('seq', 'mp'), may hold values from -6 to 6
- w_proj: bfloat16 [4096, 3, 2048], P('seq', None, 'mp'), may hold values from -0.09375 to 0.09375
- short_filter: float32 [3, 3, 2048], P(None, None, 'mp'), may hold values from -3.5 to 3.5
- long_filter: float32 [2048, 8192], P(('mp', 'seq')), may hold values from -0.0625 to 0.0625
- skip_gain: float32 [2048], P('mp'), may hold values from -4 to 4
Outputs:
- gated: bfloat16 [8192, 2048], P('seq', 'mp')
All inputs are finite; a program needn't handle non-finite values.
Results may differ from a plain program's by a relative error of at most 0.012.
Values may be sent and summed in bfloat16 or wider, within the bound.
No kernel may reach another device: no remote copies, remote signals or barrier semaphores. Data moves between devices by JAX's collectives and lax.ppermute only.
A program may use at most 64 MiB of HBM per device.

v0:
```python
import math

import jax
import jax.numpy as jnp
from jax import lax
from jax.sharding import PartitionSpec as P


def shifted(value, axis, steps):
    count = lax.axis_size(axis)
    leading, last = (max(0, -steps), min(count, count - steps))
    return lax.ppermute(value, axis, [(source, source + steps) for source in range(leading, last)])


def transform(real_part, imag_part, orient, filled):
    length = real_part.shape[-1]
    first = math.gcd(length, 64)
    highest = lax.Precision.HIGHEST
    if length <= 64 or first == 1:
        counter = jnp.arange(length, dtype=jnp.int32)
        angles = (
            2.0
            * math.pi
            / length
            * (counter[:, None] * counter[None, :] % length).astype(jnp.float32)
        )
        cosine = jnp.cos(angles)
        sine = jnp.sin(angles)
        new_real = jnp.dot(real_part, cosine, precision=highest) - orient * jnp.dot(
            imag_part, sine, precision=highest
        )
        new_imag = jnp.dot(imag_part, cosine, precision=highest) + orient * jnp.dot(
            real_part, sine, precision=highest
        )
        return (new_real, new_imag)
    second = length // first
    outer = real_part.shape[:-1]
    live = first
    if filled > 0 and filled % second == 0:
        live = filled // second
    real_grid = real_part.reshape(outer + (first, second))[..., :live, :]
    imag_grid = imag_part.reshape(outer + (first, second))[..., :live, :]
    counter = jnp.arange(first, dtype=jnp.int32)
    angles = (
        2.0 * math.pi / first * (counter[:, None] * counter[None, :] % first).astype(jnp.float32)
    )
    cosine = jnp.cos(angles)[:live]
    sine = jnp.sin(angles)[:live]
    section_real = jnp.einsum(
        "...ab,ak->...kb", real_grid, cosine, precision=highest
    ) - orient * jnp.einsum("...ab,ak->...kb", imag_grid, sine, precision=highest)
    section_imag = jnp.einsum(
        "...ab,ak->...kb", imag_grid, cosine, precision=highest
    ) + orient * jnp.einsum("...ab,ak->...kb", real_grid, sine, precision=highest)
    freq_rows = jnp.arange(first, dtype=jnp.int32)[:, None]
    time_cols = jnp.arange(second, dtype=jnp.int32)[None, :]
    twiddle = 2.0 * math.pi / length * (freq_rows * time_cols).astype(jnp.float32)
    twist_cos = jnp.cos(twiddle)
    twist_sin = jnp.sin(twiddle)
    turned_real = section_real * twist_cos - orient * section_imag * twist_sin
    turned_imag = section_imag * twist_cos + orient * section_real * twist_sin
    inner_real, inner_imag = transform(turned_real, turned_imag, orient, 0)
    final_real = jnp.swapaxes(inner_real, -1, -2).reshape(outer + (length,))
    final_imag = jnp.swapaxes(inner_imag, -1, -2).reshape(outer + (length,))
    return (final_real, final_imag)


def mirrored(values):
    return jnp.concatenate([values[:, :1], values[:, :0:-1]], axis=1)


def long_conv(signal, kernel):
    seq_len = signal.shape[-1]
    padded_signal = jnp.pad(signal.astype(jnp.float32), ((0, 0), (0, seq_len)))
    padded_kernel = jnp.pad(kernel, ((0, 0), (0, seq_len)))
    joint_real, joint_imag = transform(padded_signal, padded_kernel, -1.0, seq_len)
    mirror_real = mirrored(joint_real)
    mirror_imag = mirrored(joint_imag)
    signal_real = 0.5 * (joint_real + mirror_real)
    signal_imag = 0.5 * (joint_imag - mirror_imag)
    kernel_real = 0.5 * (joint_imag + mirror_imag)
    kernel_imag = -0.5 * (joint_real - mirror_real)
    prod_real = signal_real * kernel_real - signal_imag * kernel_imag
    prod_imag = signal_real * kernel_imag + signal_imag * kernel_real
    back_real, back_imag = transform(prod_real, prod_imag, 1.0, 0)
    return back_real[:, :seq_len] / (2.0 * seq_len)


def on_device(tokens, w_proj, short_filter, long_filter, skip_gain):
    rows_dev = tokens.shape[0]
    margin = short_filter.shape[1] - 1
    width = w_proj.shape[2]
    source = lax.all_gather(tokens, "mp", axis=1, tiled=True)
    projected = jnp.einsum(
        "td,dpc->tpc",
        source,
        lax.all_gather(w_proj, "seq", axis=0, tiled=True),
        preferred_element_type=jnp.float32,
    ).astype(jnp.bfloat16)
    tail = shifted(projected[rows_dev - margin :], "seq", 1)
    extended = jnp.concatenate([tail, projected], axis=0).astype(jnp.float32)
    mixed = jnp.zeros((rows_dev, 3, width), jnp.float32)
    for offset in range(margin + 1):
        mixed = (
            mixed
            + short_filter[:, offset, :][None]
            * extended[margin - offset : margin - offset + rows_dev]
        )
    query_rows = mixed[:, 0]
    product = (mixed[:, 1] * mixed[:, 2]).astype(jnp.bfloat16)
    groups = lax.axis_size("seq")
    channel_count = width // groups
    outgoing = product.reshape(rows_dev, groups, channel_count).transpose(1, 2, 0)
    arrived = lax.all_to_all(outgoing, "seq", split_axis=0, concat_axis=2, tiled=True)[0]
    convolved = long_conv(arrived, long_filter).astype(jnp.bfloat16)[None]
    returned = lax.all_to_all(convolved, "seq", split_axis=2, concat_axis=0, tiled=True)
    back_rows = returned.transpose(2, 0, 1).reshape(rows_dev, width)
    result = query_rows * (
        back_rows.astype(jnp.float32) + skip_gain[None, :] * product.astype(jnp.float32)
    )
    return result.astype(jnp.bfloat16)


def solution(mesh):
    return jax.shard_map(
        on_device,
        mesh=mesh,
        in_specs=(
            P("seq", "mp"),
            P("seq", None, "mp"),
            P(None, None, "mp"),
            P(("mp", "seq"), None),
            P("mp"),
        ),
        out_specs=P("seq", "mp"),
        check_vma=False,
    )
```

profile of v0, /device:TPU:1, one launch (start us, length us, event | category | flops | bytes accessed | tf_op | source)
XLA Modules:
  0.0 374.8 jit_solution(6726618726081883636)
XLA Ops:
  6.5 0.7 all-gather.3.cloned.1.call-update
  7.3 0.7 all-gather.5.cloned.1.call-update
  8.8 0.9 fusion.158
  9.7 37.3 %all-gather.3.cloned.1.call-done = bf16[128,4096]{1,0:T(8,128)(2,1)} async-done(((bf16[128,1024]{1,0:T(8,128)(2,1)}), bf16[128,4096]{1,0:T(8,128)(2,1)}) %all-gather.3.cloned.1.call-update) | async-done | bytes 1048592 | tf_op jit(solution)/shard_map/all_gather | solution.py:93
  47.0 120.2 %all-gather.5.cloned.1.call-done = bf16[4096,3,512]{2,0,1:T(8,128)(2,1)} async-done(((bf16[64,3,512]{2,0,1:T(8,128)(2,1)}), bf16[4096,3,512]{2,0,1:T(8,128)(2,1)}) %all-gather.5.cloned.1.call-update) | async-done | bytes 12582928 | tf_op jit(solution)/shard_map/all_gather | solution.py:97
  167.2 6.7 %convolution_convert_fusion = bf16[128,3,512]{2,0,1:T(8,128)(2,1)S(1)} fusion(bf16[4096,3,512]{2,0,1:T(8,128)(2,1)} %all-gather.5.cloned.1.call-done, bf16[128,4096]{1,0:T(8,128)(2,1)} %all-gather.3.cloned.1.call-done), kind=kOutput, calls=%fused_computation.14 | convolution fusion | flops 1610809344 | bytes 14024704 | tf_op jit(solution)/shard_map/td,dpc->tpc/dot_general | solution.py:94
  173.9 2.8 collective-permute-start
  177.9 0.9 copy-done
  178.8 0.8 copy.108
  179.5 8.7 %all-to-all-start = ((bf16[64,8,128]{2,1,0:T(8,128)(2,1)}), bf16[64,8,128]{2,1,0:T(8,128)(2,1)S(1)}, u32[]{:S(2)}, u32[]{:S(2)}) async-start(bf16[64,8,128]{2,1,0:T(8,128)(2,1)} %bitcast.7), calls=%async_computation | async-start | bytes 262144 | tf_op jit(solution)/shard_map/all_to_all | solution.py:114
  189.1 7.4 %all-to-all-done = bf16[64,8,128]{2,1,0:T(8,128)(2,1)S(1)} async-done(((bf16[64,8,128]{2,1,0:T(8,128)(2,1)}), bf16[64,8,128]{2,1,0:T(8,128)(2,1)S(1)}, u32[]{:S(2)}, u32[]{:S(2)}) %all-to-all-start) | async-done | bytes 131104 | tf_op jit(solution)/shard_map/all_to_all | solution.py:114
  199.3 3.3 fusion.41
  202.6 1.4 copy.109
  203.9 1.8 copy.111
  205.7 3.3 fusion.43
  209.0 3.3 fusion.5
  212.3 4.7 %add_bitcast_fusion.1 = (f32[8,64,64,4]{1,2,3,0:T(8,128)}, f32[8,64,64,4]{1,2,3,0:T(8,128)S(1)}) fusion(f32[64,8,64,4]{2,0,3,1:T(8,128)S(1)} %fusion.5, f32[64,4]{0,1:T(4,128)S(1)} %get-tuple-element.23, f32[64,4]{0,1:T(4,128)S(1)} %get-tuple-element.22, f32[64,8,64,4]{2,0,3,1:T(8,128)S(1)} %fusion.43, f32[8,64,64,4]{2,1,3,0:T(8,128)S(1)} %copy.114), kind=kOutput, calls=%fused_computation.24 | convolution fusion | flops 101769216 | bytes 2623488 | tf_op jit(solution)/shard_map/...ab,ak->...kb/dot_general | solution.py:51
  217.3 1.9 fusion.74
  219.3 1.6 copy.120
  220.9 3.1 fusion.4
  223.9 1.5 copy.166
  225.5 1.1 reshape.129
  226.6 1.2 reshape.130
  227.8 1.3 slice.96
  229.1 1.9 fusion.72
  231.0 2.1 fusion.2
  234.4 8.9 %reverse = f32[8,16384]{1,0:T(8,128)S(1)} reverse(f32[8,16384]{1,0:T(8,128)S(1)} %bitcast.226), dimensions={1} | reverse | bytes 1048576
  243.5 9.3 %reverse.1 = f32[8,16384]{1,0:T(8,128)S(1)} reverse(f32[8,16384]{1,0:T(8,128)S(1)} %bitcast.229), dimensions={1} | reverse | bytes 1048576
  253.9 0.8 fusion.35
  254.6 0.8 fusion.37
  255.4 0.8 convolution_add_fusion.2
  256.2 0.9 subtract_bitcast_fusion.2
  258.1 3.3 fusion.39
  261.4 1.4 copy.129
  262.8 1.8 copy.131
  264.5 3.3 fusion.45
  267.8 3.3 convolution_add_fusion
  271.1 4.6 %add_bitcast_fusion = (f32[8,64,64,4]{1,2,3,0:T(8,128)S(1)}, f32[8,64,64,4]{1,2,3,0:T(8,128)}) fusion(f32[64,8,64,4]{2,0,3,1:T(8,128)S(1)} %convolution_add_fusion, f32[64,4]{0,1:T(4,128)S(1)} %fusion.76, f32[64,4]{0,1:T(4,128)S(1)} %get-tuple-element.22, f32[64,8,64,4]{2,0,3,1:T(8,128)S(1)} %fusion.45, f32[8,64,64,4]{2,1,3,0:T(8,128)S(1)} %copy.134), kind=kOutput, calls=%fused_computation.22 | convolution fusion | flops 101638144 | bytes 2623488 | tf_op jit(solution)/shard_map/...ab,ak->...kb/dot_general | solution.py:51
  275.7 1.6 copy.139
  277.4 1.9 fusion.70
  279.7 2.0 fusion
  282.4 6.8 %copy.142 = bf16[1,8,8192]{1,0,2:T(2,128)(2,1)} copy(bf16[1,8,8192]{2,1,0:T(8,128)(2,1)S(1)} %fusion.21) | data formatting | bytes 262144 | tf_op jit(solution)/shard_map/broadcast_in_dim | solution.py:115
  289.7 45.4 %reduce = bf16[8192,8]{1,0:T(8,128)(2,1)S(1)} reduce(bf16[8192,1,8]{2,1,0:T(2,128)(2,1)} %bitcast.215, bf16[]{:T(256)} %broadcast.303), dimensions={1}, to_apply=%bitcast.180.reduce_sub_computation | reduce | bytes 262146
  335.1 2.3 reshape.159
  337.4 12.7 %all_to_all.21 = bf16[64,2,512]{2,1,0:T(2,128)(2,1)S(1)} all-to-all(bf16[64,2,512]{2,1,0:T(2,128)(2,1)S(1)} %reshape.159), channel_id=1, replica_groups=mesh['seq'=64,'mp'=4] {'seq'}, dimensions={0} | all-to-all | bytes 262144 | tf_op jit(solution)/shard_map/all_to_all | solution.py:116
  350.1 8.7 %reshape.160 = bf16[8192,1,8]{2,1,0:T(2,128)(2,1)} reshape(bf16[64,2,512]{2,1,0:T(2,128)(2,1)S(1)} %all_to_all.21) | data formatting | bytes 262144
  358.8 7.8 %copy.143 = bf16[1,8,8192]{2,1,0:T(8,128)(2,1)S(1)} copy(bf16[1,8,8192]{1,0,2:T(2,128)(2,1)} %bitcast.216) | data formatting | bytes 262144 | tf_op jit(solution)/shard_map/all_to_all | solution.py:116
  367.0 0.7 fusion.17
  (58 shorter events, 11.5 us)
Async XLA Ops:
  6.5 181.7 %copy-start.3 = (f32[8,8192]{1,0:T(8,128)S(1)}, f32[8,8192]{1,0:T(8,128)}, u32[]{:S(2)}) copy-start(f32[8,8192]{1,0:T(8,128)} %param.8) | copy-start | bytes 786436
  6.5 40.4 %all-gather.3.cloned.1.call-start = ((), (), s32[]{:S(2)}) async-start(), calls=%async_computation.2 | async-start | bytes 1310720 | tf_op jit(solution)/shard_map/all_gather | solution.py:93
  7.3 159.9 %all-gather.5.cloned.1.call-start = ((), (), s32[]{:S(2)}) async-start(), calls=%async_computation.3 | async-start | bytes 12779520 | tf_op jit(solution)/shard_map/all_gather | solution.py:97
  173.9 3.6 collective-permute-start
  177.8 0.9 copy-start
  179.5 17.0 %all-to-all-start = ((bf16[64,8,128]{2,1,0:T(8,128)(2,1)}), bf16[64,8,128]{2,1,0:T(8,128)(2,1)S(1)}, u32[]{:S(2)}, u32[]{:S(2)}) async-start(bf16[64,8,128]{2,1,0:T(8,128)(2,1)} %bitcast.7), calls=%async_computation | async-start | bytes 262144 | tf_op jit(solution)/shard_map/all_to_all | solution.py:114
  227.8 25.2 %slice-start = ((f32[8,16384]{1,0:T(8,128)}), f32[8,1]{1,0:T(8,128)S(1)}, s32[]{:S(2)}) async-start(f32[8,16384]{1,0:T(8,128)} %reshape.130), calls=%async_computation.4 | async-start | bytes 8192 | tf_op jit(solution)/shard_map/slice | solution.py:69
  227.8 25.6 %copy-start.2 = (f32[8,64,256]{2,1,0:T(8,128)S(1)}, f32[8,64,256]{2,1,0:T(8,128)}, u32[]{:S(2)}) copy-start(f32[8,64,256]{2,1,0:T(8,128)} %reshape.129) | copy-start | bytes 1572868
  282.0 85.0 %copy-start.1 = (f32[128,3,512]{2,0,1:T(8,128)S(1)}, f32[128,3,512]{2,0,1:T(8,128)}, u32[]{:S(2)}) copy-start(f32[128,3,512]{2,0,1:T(8,128)} %copy-done) | copy-start | bytes 2359300
  282.0 85.0 %copy-start.4 = (f32[512]{0:T(512)S(1)}, f32[512]{0:T(512)}, u32[]{:S(2)}) copy-start(f32[512]{0:T(512)} %param.9) | copy-start | bytes 6148
Sparse Core Ops, SparseCore 0:
  9.1 37.7 all-gather.2
  48.8 118.2 all-gather.4
where the time goes:
time: 379 us; the launch traced here: 375 us
  waiting for transfers between devices  167 us (44%)
  local copies, waits for them, and re-layouts  67.2 us (18%)
  matrix products  54 us (14%)
  other arithmetic  48.3 us (13%)
  between operations  14.1 us (4%)
  blocking collectives  12.7 us (3%)
  starting transfers between devices  11.5 us (3%)
    all_gather x1, waiting for transfers between devices, on_device(): lax.all_gather(w_proj, 'seq', axis=0, tiled=True)  120 us
    unnamed x2, other arithmetic  45.4 us
    all_gather x1, waiting for transfers between devices, on_device(): source = lax.all_gather(tokens, 'mp', axis=1, tiled=True)  37.3 us
    unnamed x22, local copies, waits for them, and re-layouts  31.3 us
    all_to_all x1, blocking collectives, on_device(): lax.all_to_all(convolved, 'seq', split_axis=2, concat_axis=0, tiled=True)  12.7 us
    dot_general x4, matrix products, transform(): jnp.einsum('...ab,ak->...kb', imag_grid, sine, precision=highest)  10.8 us
    all_to_all x1, starting transfers between devices, on_device(): lax.all_to_all(outgoing, 'seq', split_axis=0, concat_axis=2, tiled=True)[0]  8.66 us
    dot_general x4, matrix products, transform(): jnp.einsum('...ab,ak->...kb', imag_grid, cosine, precision=highest)  7.92 us
  transfers between devices with their start and end apart: 4, of which 4 were waited for; matrix products, arithmetic and copies ran while one was open for 1% of the time, Pallas kernels for 0%

commit v1 on v0

v1 whole, which is shorter than its diff:
```python
import numpy as np

import jax
import jax.numpy as jnp
from jax import lax
from jax.sharding import PartitionSpec as P

HIGHEST = lax.Precision.HIGHEST


def shifted(value, axis, steps):
    count = lax.axis_size(axis)
    leading, last = (max(0, -steps), min(count, count - steps))
    return lax.ppermute(value, axis, [(source, source + steps) for source in range(leading, last)])


def tables(rows, cols):
    first = np.arange(rows)
    second = np.arange(cols)
    outer = 2.0 * np.pi * np.outer(first, first) / rows
    inner = 2.0 * np.pi * np.outer(second, second) / cols
    twist = 2.0 * np.pi * np.outer(first, second) / (rows * cols)
    f32 = lambda a: jnp.asarray(a.astype(np.float32))
    return dict(
        outer_cos=f32(np.cos(outer)),
        outer_sin=f32(np.sin(outer)),
        inner_cos=f32(np.cos(inner)),
        inner_sin=f32(np.sin(inner)),
        twist_cos=f32(np.cos(twist)),
        twist_sin=f32(np.sin(twist)),
    )


def forward(first_re, first_im, t):
    tc = t["twist_cos"][:, None, :]
    ts = t["twist_sin"][:, None, :]
    b_re = first_re * tc + first_im * ts
    b_im = first_im * tc - first_re * ts
    dot = lambda a, m: jnp.einsum("krn,nm->krm", a, m, precision=HIGHEST)
    x_re = dot(b_re, t["inner_cos"]) + dot(b_im, t["inner_sin"])
    x_im = dot(b_im, t["inner_cos"]) - dot(b_re, t["inner_sin"])
    return x_re, x_im


def long_conv(signal, kernel):
    live, channels, cols = signal.shape
    rows = 2 * live
    t = tables(rows, cols)
    oc = t["outer_cos"][:, :live]
    os_ = t["outer_sin"][:, :live]
    sig = signal.astype(jnp.float32)
    s_re = jnp.einsum("kn,nrm->krm", oc, sig, precision=HIGHEST)
    s_im = -jnp.einsum("kn,nrm->krm", os_, sig, precision=HIGHEST)
    ker = kernel.reshape(channels, live, cols)
    h_re = jnp.einsum("kn,rnm->krm", oc, ker, precision=HIGHEST)
    h_im = -jnp.einsum("kn,rnm->krm", os_, ker, precision=HIGHEST)
    su_re, su_im = forward(s_re, s_im, t)
    sh_re, sh_im = forward(h_re, h_im, t)
    z_re = su_re * sh_re - su_im * sh_im
    z_im = su_re * sh_im + su_im * sh_re
    dot = lambda a, m: jnp.einsum("krn,nm->krm", a, m, precision=HIGHEST)
    d_re = dot(z_re, t["inner_cos"]) - dot(z_im, t["inner_sin"])
    d_im = dot(z_im, t["inner_cos"]) + dot(z_re, t["inner_sin"])
    tc = t["twist_cos"][:, None, :]
    ts = t["twist_sin"][:, None, :]
    e_re = d_re * tc - d_im * ts
    e_im = d_im * tc + d_re * ts
    scale = 1.0 / (rows * cols)
    back_cos = t["outer_cos"][:live] * scale
    back_sin = t["outer_sin"][:live] * scale
    return jnp.einsum("nk,krm->nrm", back_cos, e_re, precision=HIGHEST) - jnp.einsum(
        "nk,krm->nrm", back_sin, e_im, precision=HIGHEST
    )


def on_device(tokens, w_proj, short_filter, long_filter, skip_gain):
    rows_dev = tokens.shape[0]
    margin = short_filter.shape[1] - 1
    width = w_proj.shape[2]
    source = lax.all_gather(tokens, "mp", axis=1, tiled=True)
    projected = jnp.einsum(
        "td,dpc->tpc",
        source,
        lax.all_gather(w_proj, "seq", axis=0, tiled=True),
        preferred_element_type=jnp.float32,
    ).astype(jnp.bfloat16)
    tail = shifted(projected[rows_dev - margin :], "seq", 1)
    extended = jnp.concatenate([tail, projected], axis=0).astype(jnp.float32)
    mixed = jnp.zeros((rows_dev, 3, width), jnp.float32)
    for offset in range(margin + 1):
        mixed = (
            mixed
            + short_filter[:, offset, :][None]
            * extended[margin - offset : margin - offset + rows_dev]
        )
    query_rows = mixed[:, 0]
    product = (mixed[:, 1] * mixed[:, 2]).astype(jnp.bfloat16)
    groups = lax.axis_size("seq")
    channel_count = width // groups
    outgoing = product.T.reshape(groups, channel_count, rows_dev)
    arrived = lax.all_to_all(outgoing, "seq", split_axis=0, concat_axis=0, tiled=True)
    convolved = long_conv(arrived, long_filter).astype(jnp.bfloat16)
    returned = lax.all_to_all(convolved, "seq", split_axis=0, concat_axis=0, tiled=True)
    back_rows = returned.reshape(width, rows_dev).T
    result = query_rows * (
        back_rows.astype(jnp.float32) + skip_gain[None, :] * product.astype(jnp.float32)
    )
    return result.astype(jnp.bfloat16)


def solution(mesh):
    return jax.shard_map(
        on_device,
        mesh=mesh,
        in_specs=(
            P("seq", "mp"),
            P("seq", None, "mp"),
            P(None, None, "mp"),
            P(("mp", "seq"), None),
            P("mp"),
        ),
        out_specs=P("seq", "mp"),
        check_vma=False,
    )
```

time: 379 us -> 226 us (0.60)
  local copies, waits for them, and re-layouts: 67.2 us -> 1.91 us
  other arithmetic: 48.3 us -> 1.15 us
  matrix products: 54 us -> 24.2 us
  waiting for transfers between devices: 167 us -> 160 us
    unnamed x2 -> x0, other arithmetic: 45.4 us -> none
    unnamed x22 -> x18, local copies, waits for them, and re-layouts: 31.3 us -> 0.06 us
    dot_general x22 -> x18, matrix products: 47.3 us -> 17.5 us  [the longest x8 9.21 us: forward(): dot = lambda a, m: jnp.einsum('krn,nm->krm', a, m, precision=HIGHEST)]
    reshape x12 -> x0, local copies, waits for them, and re-layouts: 10.3 us -> none  [the longest x5 4.5 us: transform(): final_real = jnp.swapaxes(inner_real, -1, -2).reshape(outer + (length,))]
    all_to_all x1 -> x0, local copies, waits for them, and re-layouts: 7.79 us -> none  [on_device(): lax.all_to_all(convolved, 'seq', split_axis=2, concat_axis=0, tiled=True)]
    broadcast_in_dim x1 -> x0, local copies, waits for them, and re-layouts: 6.75 us -> none  [on_device(): convolved = long_conv(arrived, long_filter).astype(jnp.bfloat16)[None]]
    all_gather x1, waiting for transfers between devices: 37.3 us -> 30.8 us  [on_device(): source = lax.all_gather(tokens, 'mp', axis=1, tiled=True)]
    sub x4 -> x0, local copies, waits for them, and re-layouts: 4.74 us -> none  [transform(): turned_real = section_real * twist_cos - orient * section_imag * twist_sin]
  transfers between devices with their start and end apart: 4 -> 4, of which waited for: 4 -> 4; matrix products, arithmetic and copies ran while one was open for 1% -> 4% of each run, Pallas kernels for 0% -> 0%
where the time goes in v1:
time: 226 us; the launch traced here: 225 us
  waiting for transfers between devices  160 us (71%)
  matrix products  24.2 us (11%)
  between operations  13.7 us (6%)
  blocking collectives  12.7 us (6%)
  starting transfers between devices  11.4 us (5%)
    all_gather x1, waiting for transfers between devices, on_device(): lax.all_gather(w_proj, 'seq', axis=0, tiled=True)  120 us
    all_gather x1, waiting for transfers between devices, on_device(): source = lax.all_gather(tokens, 'mp', axis=1, tiled=True)  30.8 us
    all_to_all x1, blocking collectives, on_device(): lax.all_to_all(convolved, 'seq', split_axis=0, concat_axis=0, tiled=True)  12.7 us
    dot_general x8, matrix products, forward(): dot = lambda a, m: jnp.einsum('krn,nm->krm', a, m, precision=HIGHEST)  9.21 us
    all_to_all x1, starting transfers between devices, on_device(): lax.all_to_all(outgoing, 'seq', split_axis=0, concat_axis=0, tiled=True)  8.51 us
    all_to_all x1, waiting for transfers between devices, on_device(): lax.all_to_all(outgoing, 'seq', split_axis=0, concat_axis=0, tiled=True)  7.09 us
    dot_general x1, matrix products, on_device(): jnp.einsum('td,dpc->tpc', source, lax.all_gather(w_proj, 'seq', axis=0, t...  6.71 us
  transfers between devices with their start and end apart: 4, of which 4 were waited for; matrix products, arithmetic and copies ran while one was open for 4% of the time, Pallas kernels for 0%

profile of v1, /device:TPU:1, one launch (start us, length us, event | category | flops | bytes accessed | tf_op | source)
XLA Modules:
  0.0 225.3 jit_solution(88990485449807214)
XLA Ops:
  6.5 0.0 copy-start
  6.5 0.0 all-gather.3.cloned.1.call-start
  6.5 0.7 all-gather.3.cloned.1.call-update
  7.3 0.0 all-gather.5.cloned.1.call-start
  7.3 0.7 all-gather.5.cloned.1.call-update
  8.0 0.9 fusion.29
  8.9 0.0 copy-done
  8.9 1.4 convolution_negate_fusion
  10.3 1.4 fusion.20
  11.7 1.5 fusion.25
  13.2 0.0 copy-start.1
  13.2 0.0 copy-start.2
  13.2 0.0 copy-start.4
  13.2 1.5 fusion.24
  14.7 1.5 convolution_subtract_fusion.1
  16.2 0.0 copy-start.3
  16.2 30.8 %all-gather.3.cloned.1.call-done = bf16[128,4096]{1,0:T(8,128)(2,1)} async-done(((bf16[128,1024]{1,0:T(8,128)(2,1)}), bf16[128,4096]{1,0:T(8,128)(2,1)}) %all-gather.3.cloned.1.call-update) | async-done | bytes 1048592 | tf_op jit(solution)/shard_map/all_gather | solution.py:80
  47.0 120.2 %all-gather.5.cloned.1.call-done = bf16[4096,3,512]{2,0,1:T(8,128)(2,1)} async-done(((bf16[64,3,512]{2,0,1:T(8,128)(2,1)}), bf16[4096,3,512]{2,0,1:T(8,128)(2,1)}) %all-gather.5.cloned.1.call-update) | async-done | bytes 12582928 | tf_op jit(solution)/shard_map/all_gather | solution.py:84
  167.2 6.7 %convolution_convert_fusion = bf16[128,3,512]{2,0,1:T(8,128)(2,1)S(1)} fusion(bf16[4096,3,512]{2,0,1:T(8,128)(2,1)} %all-gather.5.cloned.1.call-done, bf16[128,4096]{1,0:T(8,128)(2,1)} %all-gather.3.cloned.1.call-done), kind=kOutput, calls=%fused_computation | convolution fusion | flops 1610809344 | bytes 14024704 | tf_op jit(solution)/shard_map/td,dpc->tpc/dot_general | solution.py:81
  173.9 2.8 %collective-permute-start = (bf16[2,3,512]{2,0,1:T(2,128)(2,1)S(1)}, bf16[2,3,512]{2,0,1:T(2,128)(2,1)S(1)}, u32[]{:S(2)}, u32[]{:S(2)}) collective-permute-start(bf16[2,3,512]{2,0,1:T(2,128)(2,1)S(1)} %slice.56), channel_id=1, source_target_pairs={{0,4},{4,8},{8,12},{12,16},{16,20},{20,24},{24,28},{28,32},{32,36}... | collective-permute-start | bytes 18440 | tf_op jit(solution)/shard_map/ppermute | solution.py:14
  176.8 0.7 collective-permute-done
  177.5 0.1 maximum_convert_fusion
  177.6 0.2 fusion.3
  177.8 0.0 copy-start.7
  177.9 0.8 copy.24
  178.7 8.5 %all-to-all-start = ((bf16[64,8,128]{2,1,0:T(8,128)(2,1)}), bf16[64,8,128]{2,1,0:T(8,128)(2,1)S(1)}, u32[]{:S(2)}, u32[]{:S(2)}) async-start(bf16[64,8,128]{2,1,0:T(8,128)(2,1)} %bitcast.63), calls=%async_computation | async-start | bytes 262144 | tf_op jit(solution)/shard_map/all_to_all | solution.py:101
  187.2 0.0 copy-done.1
  187.2 0.0 copy-done.2
  187.2 0.0 copy-done.4
  187.2 1.4 convolution_add_fusion.1
  188.6 7.1 %all-to-all-done = bf16[64,8,128]{2,1,0:T(8,128)(2,1)S(1)} async-done(((bf16[64,8,128]{2,1,0:T(8,128)(2,1)}), bf16[64,8,128]{2,1,0:T(8,128)(2,1)S(1)}, u32[]{:S(2)}, u32[]{:S(2)}) %all-to-all-start) | async-done | bytes 131104 | tf_op jit(solution)/shard_map/all_to_all | solution.py:101
  195.7 1.2 fusion
  196.8 1.2 fusion.27
  198.0 0.6 fusion.23
  198.6 0.6 fusion.22
  199.2 0.6 convolution_add_fusion.2
  199.8 1.7 multiply_subtract_fusion
  201.4 0.6 fusion.30
  202.0 0.6 fusion.31
  202.6 0.6 convolution_subtract_fusion
  203.2 0.6 convolution_add_fusion
  203.7 0.5 fusion.8
  204.2 0.5 fusion.1
  204.7 0.1 copy.30
  204.8 12.7 %all_to_all.10 = bf16[64,8,128]{2,1,0:T(8,128)(2,1)S(1)} all-to-all(bf16[64,8,128]{2,1,0:T(8,128)(2,1)S(1)} %copy.30), channel_id=1, replica_groups=mesh['seq'=64,'mp'=4] {'seq'}, dimensions={0} | all-to-all | bytes 262144 | tf_op jit(solution)/shard_map/all_to_all | solution.py:103
  217.5 0.1 copy.31
  217.7 0.0 copy-done.7
  217.7 0.7 fusion.14
  (10 shorter events, 0.1 us)
Async XLA Ops:
  6.5 2.3 %copy-start = (f32[8,8192]{1,0:T(8,128)S(1)}, f32[8,8192]{1,0:T(8,128)}, u32[]{:S(2)}) copy-start(f32[8,8192]{1,0:T(8,128)} %param.14) | copy-start | bytes 786436
  6.5 40.4 %all-gather.3.cloned.1.call-start = ((), (), s32[]{:S(2)}) async-start(), calls=%async_computation.2 | async-start | bytes 1310720 | tf_op jit(solution)/shard_map/all_gather | solution.py:80
  7.3 159.9 %all-gather.5.cloned.1.call-start = ((), (), s32[]{:S(2)}) async-start(), calls=%async_computation.3 | async-start | bytes 12779520 | tf_op jit(solution)/shard_map/all_gather | solution.py:84
  13.2 174.0 %copy-start.1 = (f32[128,128]{1,0:T(8,128)S(1)}, f32[128,128]{1,0:T(8,128)}, u32[]{:S(2)}) copy-start(f32[128,128]{1,0:T(8,128)} %constant.13.clone) | copy-start | bytes 196612
  13.2 174.0 %copy-start.2 = (f32[128,128]{1,0:T(8,128)S(1)}, f32[128,128]{1,0:T(8,128)}, u32[]{:S(2)}) copy-start(f32[128,128]{1,0:T(8,128)} %constant.12.clone) | copy-start | bytes 196612
  13.2 174.0 %copy-start.4 = (f32[128,128,1]{1,0,2:T(8,128)S(1)}, f32[128,128,1]{1,0,2:T(8,128)}, u32[]{:S(2)}) copy-start(f32[128,128,1]{1,0,2:T(8,128)} %constant.25) | copy-start | bytes 196612
  16.2 181.8 %copy-start.3 = (f32[128,128,1]{1,0,2:T(8,128)S(1)}, f32[128,128,1]{1,0,2:T(8,128)}, u32[]{:S(2)}) copy-start(f32[128,128,1]{1,0,2:T(8,128)} %constant.24) | copy-start | bytes 196612
  173.9 3.6 %collective-permute-start = (bf16[2,3,512]{2,0,1:T(2,128)(2,1)S(1)}, bf16[2,3,512]{2,0,1:T(2,128)(2,1)S(1)}, u32[]{:S(2)}, u32[]{:S(2)}) collective-permute-start(bf16[2,3,512]{2,0,1:T(2,128)(2,1)S(1)} %slice.56), channel_id=1, source_target_pairs={{0,4},{4,8},{8,12},{12,16},{16,20},{20,24},{24,28},{28,32},{32,36}... | collective-permute-start | bytes 18440 | tf_op jit(solution)/shard_map/ppermute | solution.py:14
  177.8 39.8 %copy-start.7 = (f32[512]{0:T(512)S(1)}, f32[512]{0:T(512)}, u32[]{:S(2)}) copy-start(f32[512]{0:T(512)} %param.15) | copy-start | bytes 6148
  178.7 17.0 %all-to-all-start = ((bf16[64,8,128]{2,1,0:T(8,128)(2,1)}), bf16[64,8,128]{2,1,0:T(8,128)(2,1)S(1)}, u32[]{:S(2)}, u32[]{:S(2)}) async-start(bf16[64,8,128]{2,1,0:T(8,128)(2,1)} %bitcast.63), calls=%async_computation | async-start | bytes 262144 | tf_op jit(solution)/shard_map/all_to_all | solution.py:101
  188.6 15.2 %copy-start.6 = (f32[64,128,1]{1,0,2:T(8,128)S(1)}, f32[64,128,1]{1,0,2:T(8,128)}, u32[]{:S(2)}) copy-start(f32[64,128,1]{1,0,2:T(8,128)} %constant.21) | copy-start | bytes 98308
  188.6 15.6 %copy-start.5 = (f32[64,128,1]{1,0,2:T(8,128)S(1)}, f32[64,128,1]{1,0,2:T(8,128)}, u32[]{:S(2)}) copy-start(f32[64,128,1]{1,0,2:T(8,128)} %constant.26) | copy-start | bytes 98308
Sparse Core Ops, SparseCore 0:
  9.1 37.7 all-gather.2
  48.8 118.2 all-gather.4

commit v2 on v1

--- a/solution.py
+++ b/solution.py
@@ -6,6 +6,7 @@
 from jax.sharding import PartitionSpec as P
 
 HIGHEST = lax.Precision.HIGHEST
+GROUP = 8
 
 
 def shifted(value, axis, steps):
@@ -73,52 +74,65 @@
     )
 
 
+def pick(values, axis, parity):
+    shape = values.shape
+    grouped = values.reshape(shape[:axis] + (shape[axis] // (2 * GROUP), 2, GROUP) + shape[axis + 1 :])
+    taken = lax.dynamic_index_in_dim(grouped, parity, axis + 1, keepdims=False)
+    return taken.reshape(shape[:axis] + (shape[axis] // 2,) + shape[axis + 1 :])
+
+
 def on_device(tokens, w_proj, short_filter, long_filter, skip_gain):
     rows_dev = tokens.shape[0]
     margin = short_filter.shape[1] - 1
     width = w_proj.shape[2]
-    source = lax.all_gather(tokens, "mp", axis=1, tiled=True)
+    half = width // 2
+    chips = lax.axis_size("chip")
+    parity = lax.axis_index("core")
+    source = lax.all_gather(lax.all_gather(tokens, "mp", axis=1, tiled=True), "core", axis=0, tiled=True)
+    split = w_proj.reshape(w_proj.shape[0], 3, width // (2 * GROUP), 2, GROUP)
+    split = jnp.moveaxis(split, 3, 0).reshape(2, w_proj.shape[0], 3, half)
+    paired = lax.all_to_all(split, "core", split_axis=0, concat_axis=0, tiled=True)
+    weights = lax.all_gather(paired.reshape(2 * w_proj.shape[0], 3, half), "chip", axis=0, tiled=True)
     projected = jnp.einsum(
-        "td,dpc->tpc",
-        source,
-        lax.all_gather(w_proj, "seq", axis=0, tiled=True),
-        preferred_element_type=jnp.float32,
+        "td,dpc->tpc", source, weights, preferred_element_type=jnp.float32
     ).astype(jnp.bfloat16)
-    tail = shifted(projected[rows_dev - margin :], "seq", 1)
+    rows = source.shape[0]
+    tail = shifted(projected[rows - margin :], "chip", 1)
     extended = jnp.concatenate([tail, projected], axis=0).astype(jnp.float32)
-    mixed = jnp.zeros((rows_dev, 3, width), jnp.float32)
+    taps = pick(short_filter, 2, parity)
+    mixed = jnp.zeros((rows, 3, half), jnp.float32)
     for offset in range(margin + 1):
-        mixed = (
-            mixed
-            + short_filter[:, offset, :][None]
-            * extended[margin - offset : margin - offset + rows_dev]
-        )
+        mixed = mixed + taps[:, offset, :][None] * extended[margin - offset : margin - offset + rows]
     query_rows = mixed[:, 0]
     product = (mixed[:, 1] * mixed[:, 2]).astype(jnp.bfloat16)
-    groups = lax.axis_size("seq")
-    channel_count = width // groups
-    outgoing = product.T.reshape(groups, channel_count, rows_dev)
-    arrived = lax.all_to_all(outgoing, "seq", split_axis=0, concat_axis=0, tiled=True)
+    outgoing = product.T.reshape(chips, GROUP, rows)
+    arrived = lax.all_to_all(outgoing, "chip", split_axis=0, concat_axis=0, tiled=True)
     convolved = long_conv(arrived, long_filter).astype(jnp.bfloat16)
-    returned = lax.all_to_all(convolved, "seq", split_axis=0, concat_axis=0, tiled=True)
-    back_rows = returned.reshape(width, rows_dev).T
-    result = query_rows * (
-        back_rows.astype(jnp.float32) + skip_gain[None, :] * product.astype(jnp.float32)
-    )
-    return result.astype(jnp.bfloat16)
+    returned = lax.all_to_all(convolved, "chip", split_axis=0, concat_axis=0, tiled=True)
+    back_rows = returned.reshape(half, rows).T
+    gain = pick(skip_gain, 0, parity)
+    local = query_rows * (back_rows.astype(jnp.float32) + gain[None, :] * product.astype(jnp.float32))
+    local = local.astype(jnp.bfloat16).reshape(2, rows_dev, half)
+    swapped = lax.all_to_all(local, "core", split_axis=0, concat_axis=0, tiled=True)
+    swapped = swapped.reshape(2, rows_dev, half // GROUP, GROUP)
+    return jnp.transpose(swapped, (1, 2, 0, 3)).reshape(rows_dev, width)
 
 
 def solution(mesh):
+    seq_size = mesh.shape["seq"]
+    devices = mesh.devices.reshape(seq_size // 2, 2, mesh.shape["mp"])
+    inner = jax.sharding.Mesh(devices, ("chip", "core", "mp"))
+    seq = ("chip", "core")
     return jax.shard_map(
         on_device,
-        mesh=mesh,
+        mesh=inner,
         in_specs=(
-            P("seq", "mp"),
-            P("seq", None, "mp"),
+            P(seq, "mp"),
+            P(seq, None, "mp"),
             P(None, None, "mp"),
-            P(("mp", "seq"), None),
+            P(("mp",) + seq, None),
             P("mp"),
         ),
-        out_specs=P("seq", "mp"),
+        out_specs=P(seq, "mp"),
         check_vma=False,
     )

time: 226 us -> 297 us (1.31)
  waiting for transfers between devices: 160 us -> 210 us
  blocking collectives: 12.7 us -> 33.6 us
  matrix products: 24.2 us -> 17.6 us
  local copies, waits for them, and re-layouts: 1.91 us -> 6.72 us
  starting transfers between devices: 11.4 us -> 15 us
    all_gather x2 -> x3, waiting for transfers between devices: 151 us -> 194 us  [the longest x1 146 us: on_device(): lax.all_gather(paired.reshape(2 * w_proj.shape[0], 3, half), 'chip', axis...]
    all_to_all x1 -> x2, blocking collectives: 12.7 us -> 33.6 us  [the longest x1 28.4 us: on_device(): lax.all_to_all(local, 'core', split_axis=0, concat_axis=0, tiled=True)]
    all_to_all x1 -> x2, waiting for transfers between devices: 7.09 us -> 14 us  [the longest x1 7.29 us: on_device(): lax.all_to_all(convolved, 'chip', split_axis=0, concat_axis=0, tiled=True)]
    all_to_all x1 -> x2, starting transfers between devices: 8.51 us -> 12 us  [the longest x1 8.17 us: on_device(): lax.all_to_all(outgoing, 'chip', split_axis=0, concat_axis=0, tiled=True)]
  transfers between devices with their start and end apart: 4 -> 6, of which waited for: 4 -> 6; matrix products, arithmetic and copies ran while one was open for 4% -> 2% of each run, Pallas kernels for 0% -> 0%
where the time goes in v2:
time: 297 us
  waiting for transfers between devices  210 us (71%)
  blocking collectives  33.6 us (11%)
  matrix products  17.6 us (6%)
  starting transfers between devices  15 us (5%)
  between operations  13.6 us (5%)
  local copies, waits for them, and re-layouts  6.72 us (2%)
    all_gather x1, waiting for transfers between devices, on_device(): lax.all_gather(paired.reshape(2 * w_proj.shape[0], 3, half), 'chip', axis...  146 us
    all_gather x1, waiting for transfers between devices, on_device(): lax.all_gather(tokens, 'mp', axis=1, tiled=True)  39.7 us
    all_to_all x1, blocking collectives, on_device(): lax.all_to_all(local, 'core', split_axis=0, concat_axis=0, tiled=True)  28.4 us
    all_gather x1, waiting for transfers between devices, on_device(): lax.all_gather(lax.all_gather(tokens, 'mp', axis=1, tiled=True), 'core',...  8.64 us
    all_to_all x1, starting transfers between devices, on_device(): lax.all_to_all(outgoing, 'chip', split_axis=0, concat_axis=0, tiled=True)  8.17 us
    all_to_all x1, waiting for transfers between devices, on_device(): lax.all_to_all(convolved, 'chip', split_axis=0, concat_axis=0, tiled=True)  7.29 us
    all_to_all x1, waiting for transfers between devices, on_device(): lax.all_to_all(outgoing, 'chip', split_axis=0, concat_axis=0, tiled=True)  6.74 us
    dot_general x8, matrix products, forward(): dot = lambda a, m: jnp.einsum('krn,nm->krm', a, m, precision=HIGHEST)  6.64 us
  transfers between devices with their start and end apart: 6, of which 6 were waited for; matrix products, arithmetic and copies ran while one was open for 2% of the time, Pallas kernels for 0%

profile of v2, /device:TPU:1, one launch (start us, length us, event | category | flops | bytes accessed | tf_op | source)
XLA Modules:
  0.0 296.9 jit_solution(217743995064844577)
XLA Ops:
  6.5 0.7 all-gather.4.cloned.1.call-update
  7.3 39.7 %all-gather.4.cloned.1.call-done = bf16[128,4096]{1,0:T(8,128)(2,1)} async-done(((bf16[128,1024]{1,0:T(8,128)(2,1)}), bf16[128,4096]{1,0:T(8,128)(2,1)}) %all-gather.4.cloned.1.call-update) | async-done | bytes 1048592 | tf_op jit(solution)/shard_map/all_gather | solution.py:91
  47.0 1.1 copy.55
  48.2 0.1 copy.130
  48.3 0.2 copy.57
  48.4 5.2 %all_to_all.20 = bf16[2,64,3,256]{3,1,2,0:T(8,128)(2,1)S(1)} all-to-all(bf16[2,64,3,256]{3,1,2,0:T(8,128)(2,1)S(1)} %copy.57), channel_id=1, replica_groups=mesh['chip'=32,'core'=2,'mp'=4] {'core'}, dimensions={0} | all-to-all | bytes 393216 | tf_op jit(solution)/shard_map/all_to_all | solution.py:94
  53.6 0.7 copy.58
  54.3 1.2 reshape.46
  55.6 0.4 dynamic-slice_reduce_fusion
  56.0 0.1 reshape.47
  56.2 8.6 %all-gather.6.cloned.1.call-done = bf16[256,4096]{1,0:T(8,128)(2,1)} async-done(((bf16[128,4096]{1,0:T(8,128)(2,1)}), bf16[256,4096]{1,0:T(8,128)(2,1)}) %all-gather.6.cloned.1.call-update) | async-done | bytes 2097168 | tf_op jit(solution)/shard_map/all_gather | solution.py:91
  64.8 146.2 %all-gather.8.cloned.1.call-done = bf16[4096,3,256]{2,0,1:T(8,128)(2,1)} async-done(((bf16[128,3,256]{2,0,1:T(8,128)(2,1)}), bf16[4096,3,256]{2,0,1:T(8,128)(2,1)}) %all-gather.8.cloned.1.call-update) | async-done | bytes 6291472 | tf_op jit(solution)/shard_map/all_gather | solution.py:95
  211.0 5.2 %fusion.2 = bf16[256,3,256]{2,0,1:T(8,128)(2,1)S(1)} fusion(bf16[4096,3,256]{2,0,1:T(8,128)(2,1)} %all-gather.8.cloned.1.call-done, bf16[256,4096]{1,0:T(8,128)(2,1)} %all-gather.6.cloned.1.call-done), kind=kOutput, calls=%fused_computation.2 | convolution fusion | flops 1610809344 | bytes 8781824 | tf_op jit(solution)/shard_map/td,dpc->tpc/dot_general | solution.py:96
  216.2 2.9 collective-permute-start
  219.2 0.7 collective-permute-done
  219.9 0.1 maximum_convert_fusion
  220.0 0.2 fusion.7
  220.3 0.8 copy.59
  221.0 8.2 %all-to-all-start.1 = ((bf16[32,8,256]{2,1,0:T(8,128)(2,1)}), bf16[32,8,256]{2,1,0:T(8,128)(2,1)S(1)}, u32[]{:S(2)}, u32[]{:S(2)}) async-start(bf16[32,8,256]{2,1,0:T(8,128)(2,1)} %bitcast.10), calls=%async_computation.1 | async-start | bytes 262144 | tf_op jit(solution)/shard_map/all_to_all | solution.py:109
  229.2 0.6 convolution_negate_fusion
  229.8 6.7 %all-to-all-done.1 = bf16[32,8,256]{2,1,0:T(8,128)(2,1)S(1)} async-done(((bf16[32,8,256]{2,1,0:T(8,128)(2,1)}), bf16[32,8,256]{2,1,0:T(8,128)(2,1)S(1)}, u32[]{:S(2)}, u32[]{:S(2)}) %all-to-all-start.1) | async-done | bytes 131104 | tf_op jit(solution)/shard_map/all_to_all | solution.py:109
  236.6 0.4 fusion.5
  237.0 0.4 fusion.45
  237.5 0.8 multiply_subtract_fusion.1
  238.3 0.8 fusion.22
  239.1 0.8 fusion.26
  239.9 0.8 convolution_subtract_fusion.1
  240.8 0.8 convolution_add_fusion.1
  241.6 0.8 fusion.28
  242.4 0.8 fusion.32
  243.3 0.8 convolution_add_fusion.2
  244.1 0.9 multiply_subtract_fusion
  245.0 0.7 fusion.20
  245.7 0.7 fusion.16
  246.4 0.7 convolution_subtract_fusion
  247.0 0.7 convolution_add_fusion
  247.7 0.4 fusion.12
  248.2 0.5 fusion.6
  248.6 0.7 copy.76
  249.4 3.9 %all-to-all-start.2 = ((bf16[32,8,256]{2,1,0:T(8,128)(2,1)}), bf16[32,8,256]{2,1,0:T(8,128)(2,1)S(1)}, u32[]{:S(2)}, u32[]{:S(2)}) async-start(bf16[32,8,256]{2,1,0:T(8,128)(2,1)} %copy.76), calls=%async_computation.2 | async-start | bytes 262144 | tf_op jit(solution)/shard_map/all_to_all | solution.py:111
  253.2 0.1 reshape.53
  253.4 0.1 mul.171
  253.5 7.3 %all-to-all-done.2 = bf16[32,8,256]{2,1,0:T(8,128)(2,1)S(1)} async-done(((bf16[32,8,256]{2,1,0:T(8,128)(2,1)}), bf16[32,8,256]{2,1,0:T(8,128)(2,1)S(1)}, u32[]{:S(2)}, u32[]{:S(2)}) %all-to-all-start.2) | async-done | bytes 131104 | tf_op jit(solution)/shard_map/all_to_all | solution.py:111
  260.8 0.1 copy.77
  261.0 0.1 fusion.36
  261.0 0.1 copy.78
  261.2 28.4 %all_to_all.21 = bf16[2,128,256]{1,2,0:T(8,128)(2,1)S(1)} all-to-all(bf16[2,128,256]{1,2,0:T(8,128)(2,1)S(1)} %copy.78), channel_id=1, replica_groups=mesh['chip'=32,'core'=2,'mp'=4] {'core'}, dimensions={0} | all-to-all | bytes 262144 | tf_op jit(solution)/shard_map/all_to_all | solution.py:116
  289.6 0.8 copy.80
  (33 shorter events, 0.3 us)
Async XLA Ops:
  6.5 222.7 %copy-start = (f32[8,8192]{1,0:T(8,128)S(1)}, f32[8,8192]{1,0:T(8,128)}, u32[]{:S(2)}) copy-start(f32[8,8192]{1,0:T(8,128)} %param.14) | copy-start | bytes 786436
  6.5 40.4 %all-gather.4.cloned.1.call-start = ((), (), s32[]{:S(2)}) async-start(), calls=%async_computation.4 | async-start | bytes 1310720 | tf_op jit(solution)/shard_map/all_gather | solution.py:91
  7.3 57.5 %all-gather.6.cloned.1.call-start = ((), (), s32[]{:S(2)}) async-start(), calls=%async_computation.5 | async-start | bytes 3145728 | tf_op jit(solution)/shard_map/all_gather | solution.py:91
  47.0 164.0 %all-gather.8.cloned.1.call-start = ((), (), s32[]{:S(2)}) async-start(), calls=%async_computation.6 | async-start | bytes 6488064 | tf_op jit(solution)/shard_map/all_gather | solution.py:95
  56.1 173.1 %copy-start.6 = (f32[64,32,1]{0,1,2:T(8,128)S(1)}, f32[64,32,1]{0,1,2:T(8,128)}, u32[]{:S(2)}) copy-start(f32[64,32,1]{0,1,2:T(8,128)} %constant.45) | copy-start | bytes 24580
  216.2 20.8 %copy-start.5 = (f32[64,32,1]{0,1,2:T(8,128)S(1)}, f32[64,32,1]{0,1,2:T(8,128)}, u32[]{:S(2)}) copy-start(f32[64,32,1]{0,1,2:T(8,128)} %constant.44) | copy-start | bytes 24580
  216.2 21.3 %copy-start.3 = (f32[64,256]{1,0:T(8,128)S(1)}, f32[64,256]{1,0:T(8,128)}, u32[]{:S(2)}) copy-start(f32[64,256]{1,0:T(8,128)} %constant.35.clone) | copy-start | bytes 196612
  216.2 21.2 %copy-start.4 = (f32[64,256]{1,0:T(8,128)S(1)}, f32[64,256]{1,0:T(8,128)}, u32[]{:S(2)}) copy-start(f32[64,256]{1,0:T(8,128)} %constant.34.clone) | copy-start | bytes 196612
  216.2 22.1 %copy-start.1 = (f32[256,256,1]{1,0,2:T(8,128)S(1)}, f32[256,256,1]{1,0,2:T(8,128)}, u32[]{:S(2)}) copy-start(f32[256,256,1]{1,0,2:T(8,128)} %constant.46) | copy-start | bytes 786436
  216.2 3.6 %collective-permute-start = (bf16[2,3,256]{2,0,1:T(2,128)(2,1)S(1)}, bf16[2,3,256]{2,0,1:T(2,128)(2,1)S(1)}, u32[]{:S(2)}, u32[]{:S(2)}) collective-permute-start(bf16[2,3,256]{2,0,1:T(2,128)(2,1)S(1)} %slice.57), channel_id=1, source_target_pairs={{0,8},{8,16},{16,24},{24,32},{32,40},{40,48},{48,56},{56,64},{64,7... | collective-permute-start | bytes 9224 | tf_op jit(solution)/shard_map/ppermute | solution.py:15
  220.0 20.0 %copy-start.2 = (f32[256,256,1]{1,0,2:T(8,128)S(1)}, f32[256,256,1]{1,0,2:T(8,128)}, u32[]{:S(2)}) copy-start(f32[256,256,1]{1,0,2:T(8,128)} %constant.47) | copy-start | bytes 786436
  221.0 15.6 %all-to-all-start.1 = ((bf16[32,8,256]{2,1,0:T(8,128)(2,1)}), bf16[32,8,256]{2,1,0:T(8,128)(2,1)S(1)}, u32[]{:S(2)}, u32[]{:S(2)}) async-start(bf16[32,8,256]{2,1,0:T(8,128)(2,1)} %bitcast.10), calls=%async_computation.1 | async-start | bytes 262144 | tf_op jit(solution)/shard_map/all_to_all | solution.py:109
  243.3 4.4 %copy-start.8 = (f32[32,64,1]{1,0,2:T(8,128)S(1)}, f32[32,64,1]{1,0,2:T(8,128)}, u32[]{:S(2)}) copy-start(f32[32,64,1]{1,0,2:T(8,128)} %constant.43) | copy-start | bytes 24580
  244.1 4.0 %copy-start.7 = (f32[32,64,1]{1,0,2:T(8,128)S(1)}, f32[32,64,1]{1,0,2:T(8,128)}, u32[]{:S(2)}) copy-start(f32[32,64,1]{1,0,2:T(8,128)} %constant.48) | copy-start | bytes 24580
  244.1 9.1 %copy-start.9 = (f32[512]{0:T(512)S(1)}, f32[512]{0:T(512)}, u32[]{:S(2)}) copy-start(f32[512]{0:T(512)} %param.15) | copy-start | bytes 6148
  249.4 11.4 %all-to-all-start.2 = ((bf16[32,8,256]{2,1,0:T(8,128)(2,1)}), bf16[32,8,256]{2,1,0:T(8,128)(2,1)S(1)}, u32[]{:S(2)}, u32[]{:S(2)}) async-start(bf16[32,8,256]{2,1,0:T(8,128)(2,1)} %copy.76), calls=%async_computation.2 | async-start | bytes 262144 | tf_op jit(solution)/shard_map/all_to_all | solution.py:111
Sparse Core Ops, SparseCore 0:
  9.1 37.7 all-gather.3
  48.8 15.9 all-gather.5
  66.6 144.3 all-gather.7

commit v3 on v2

--- a/solution.py
+++ b/solution.py
@@ -90,9 +90,10 @@
     parity = lax.axis_index("core")
     source = lax.all_gather(lax.all_gather(tokens, "mp", axis=1, tiled=True), "core", axis=0, tiled=True)
     split = w_proj.reshape(w_proj.shape[0], 3, width // (2 * GROUP), 2, GROUP)
-    split = jnp.moveaxis(split, 3, 0).reshape(2, w_proj.shape[0], 3, half)
-    paired = lax.all_to_all(split, "core", split_axis=0, concat_axis=0, tiled=True)
-    weights = lax.all_gather(paired.reshape(2 * w_proj.shape[0], 3, half), "chip", axis=0, tiled=True)
+    split = jnp.moveaxis(split, 3, 0).reshape(1, 2, w_proj.shape[0], 3, half)
+    spread = jnp.broadcast_to(split, (chips, 2) + split.shape[2:]).reshape((2 * chips,) + split.shape[2:])
+    weights = lax.all_to_all(spread, ("chip", "core"), split_axis=0, concat_axis=0, tiled=True)
+    weights = weights.reshape(2 * chips * w_proj.shape[0], 3, half)
     projected = jnp.einsum(
         "td,dpc->tpc", source, weights, preferred_element_type=jnp.float32
     ).astype(jnp.bfloat16)

time: 297 us -> 183 us (0.62)
  waiting for transfers between devices: 210 us -> 105 us
  blocking collectives: 33.6 us -> 6.48 us
  starting transfers between devices: 15 us -> 23.8 us
  local copies, waits for them, and re-layouts: 6.72 us -> 15.2 us
    all_gather x1 -> x0, waiting for transfers between devices: 146 us -> none  [on_device(): lax.all_gather(paired.reshape(2 * w_proj.shape[0], 3, half), 'chip', axis...]
    all_to_all x0 -> x1, waiting for transfers between devices: none -> 42.5 us  [on_device(): lax.all_to_all(spread, ('chip', 'core'), split_axis=0, concat_axis=0, til...]
    all_to_all x1, blocking collectives: 28.4 us -> 6.48 us  [on_device(): lax.all_to_all(local, 'core', split_axis=0, concat_axis=0, tiled=True)]
    all_to_all x0 -> x1, starting transfers between devices: none -> 10.6 us  [on_device(): lax.all_to_all(spread, ('chip', 'core'), split_axis=0, concat_axis=0, til...]
    all_gather x1, waiting for transfers between devices: 8.64 us -> 0.01 us  [on_device(): lax.all_gather(lax.all_gather(tokens, 'mp', axis=1, tiled=True), 'core',...]
    all_gather x1, waiting for transfers between devices: 39.7 us -> 47.2 us  [on_device(): lax.all_gather(tokens, 'mp', axis=1, tiled=True)]
    all_to_all x1, local copies, waits for them, and re-layouts: 0.7 us -> 6.51 us  [on_device(): lax.all_to_all(spread, ('chip', 'core'), split_axis=0, concat_axis=0, til...]
    all_to_all x1 -> x0, blocking collectives: 5.16 us -> none  [on_device(): lax.all_to_all(split, 'core', split_axis=0, concat_axis=0, tiled=True)]
  transfers between devices with their start and end apart: 6 -> 6, of which waited for: 6 -> 5; matrix products, arithmetic and copies ran while one was open for 2% -> 5% of each run, Pallas kernels for 0% -> 0%
where the time goes in v3:
time: 183 us
  waiting for transfers between devices  105 us (57%)
  starting transfers between devices  23.8 us (13%)
  matrix products  17.6 us (10%)
  local copies, waits for them, and re-layouts  15.2 us (8%)
  between operations  13.9 us (8%)
  blocking collectives  6.48 us (4%)
    all_gather x1, waiting for transfers between devices, on_device(): lax.all_gather(tokens, 'mp', axis=1, tiled=True)  47.2 us
    all_to_all x1, waiting for transfers between devices, on_device(): lax.all_to_all(spread, ('chip', 'core'), split_axis=0, concat_axis=0, til...  42.5 us
    all_to_all x1, starting transfers between devices, on_device(): lax.all_to_all(spread, ('chip', 'core'), split_axis=0, concat_axis=0, til...  10.6 us
    all_to_all x1, starting transfers between devices, on_device(): lax.all_to_all(outgoing, 'chip', split_axis=0, concat_axis=0, tiled=True)  7.81 us
    all_to_all x1, waiting for transfers between devices, on_device(): lax.all_to_all(convolved, 'chip', split_axis=0, concat_axis=0, tiled=True)  7.29 us
    all_to_all x1, waiting for transfers between devices, on_device(): lax.all_to_all(outgoing, 'chip', split_axis=0, concat_axis=0, tiled=True)  6.74 us
    dot_general x8, matrix products, forward(): dot = lambda a, m: jnp.einsum('krn,nm->krm', a, m, precision=HIGHEST)  6.64 us
    all_to_all x1, local copies, waits for them, and re-layouts, on_device(): lax.all_to_all(spread, ('chip', 'core'), split_axis=0, concat_axis=0, til...  6.51 us
  transfers between devices with their start and end apart: 6, of which 5 were waited for; matrix products, arithmetic and copies ran while one was open for 5% of the time, Pallas kernels for 0%

profile of v3, /device:TPU:1, one launch (start us, length us, event | category | flops | bytes accessed | tf_op | source)
XLA Modules:
  0.0 182.6 jit_solution(11547071746382031340)
XLA Ops:
  6.5 1.2 copy.54
  7.7 0.1 copy.129
  7.8 0.2 copy.56
  8.0 3.4 %broadcast_in_dim.5 = bf16[32,2,64,3,256]{4,2,3,1,0:T(8,128)(2,1)} broadcast(bf16[2,64,3,256]{3,1,2,0:T(8,128)(2,1)S(1)} %copy.56), dimensions={1,2,3,4} | broadcast | bytes 6488064 | tf_op jit(solution)/shard_map/broadcast_in_dim | solution.py:94
  11.4 10.6 %all-to-all-start = ((bf16[64,64,3,256]{3,1,2,0:T(8,128)(2,1)}), bf16[64,64,3,256]{3,1,2,0:T(8,128)(2,1)}, u32[]{:S(2)}, u32[]{:S(2)}) async-start(bf16[64,64,3,256]{3,1,2,0:T(8,128)(2,1)} %bitcast.76), calls=%async_computation | async-start | bytes 12582912 | tf_op jit(solution)/shard_map/all_to_all | solution.py:95
  22.1 0.7 all-gather.3.cloned.1.call-update
  22.8 47.2 %all-gather.3.cloned.1.call-done = bf16[128,4096]{1,0:T(8,128)(2,1)} async-done(((bf16[128,1024]{1,0:T(8,128)(2,1)}), bf16[128,4096]{1,0:T(8,128)(2,1)}) %all-gather.3.cloned.1.call-update) | async-done | bytes 1048592 | tf_op jit(solution)/shard_map/all_gather | solution.py:91
  70.0 0.5 reshape.48
  70.5 0.4 dynamic-slice_reduce_fusion
  70.9 0.1 reshape.49
  71.1 42.5 %all-to-all-done = bf16[64,64,3,256]{3,1,2,0:T(8,128)(2,1)} async-done(((bf16[64,64,3,256]{3,1,2,0:T(8,128)(2,1)}), bf16[64,64,3,256]{3,1,2,0:T(8,128)(2,1)}, u32[]{:S(2)}, u32[]{:S(2)}) %all-to-all-start) | async-done | bytes 6291488 | tf_op jit(solution)/shard_map/all_to_all | solution.py:95
  113.6 6.5 %copy.57 = bf16[64,64,3,256]{3,1,0,2:T(8,128)(2,1)} copy(bf16[64,64,3,256]{3,1,2,0:T(8,128)(2,1)} %all-to-all-done) | data formatting | bytes 12582912 | tf_op jit(solution)/shard_map/all_to_all | solution.py:95
  120.1 5.2 %fusion.2 = bf16[256,3,256]{2,0,1:T(8,128)(2,1)S(1)} fusion(bf16[4096,3,256]{2,0,1:T(8,128)(2,1)} %bitcast.77, bf16[256,4096]{1,0:T(8,128)(2,1)} %all-gather.5.cloned.1.call-done), kind=kOutput, calls=%fused_computation.2 | convolution fusion | flops 1610809344 | bytes 8781824 | tf_op jit(solution)/shard_map/td,dpc->tpc/dot_general | solution.py:97
  125.4 1.4 collective-permute-start
  126.8 0.7 collective-permute-done
  127.6 0.1 maximum_convert_fusion
  127.6 0.2 fusion.7
  127.9 0.8 copy.58
  128.7 7.8 %all-to-all-start.1 = ((bf16[32,8,256]{2,1,0:T(8,128)(2,1)}), bf16[32,8,256]{2,1,0:T(8,128)(2,1)S(1)}, u32[]{:S(2)}, u32[]{:S(2)}) async-start(bf16[32,8,256]{2,1,0:T(8,128)(2,1)} %bitcast.11), calls=%async_computation.1 | async-start | bytes 262144 | tf_op jit(solution)/shard_map/all_to_all | solution.py:110
  136.5 0.6 convolution_negate_fusion
  137.2 6.7 %all-to-all-done.1 = bf16[32,8,256]{2,1,0:T(8,128)(2,1)S(1)} async-done(((bf16[32,8,256]{2,1,0:T(8,128)(2,1)}), bf16[32,8,256]{2,1,0:T(8,128)(2,1)S(1)}, u32[]{:S(2)}, u32[]{:S(2)}) %all-to-all-start.1) | async-done | bytes 131104 | tf_op jit(solution)/shard_map/all_to_all | solution.py:110
  143.9 0.4 fusion.5
  144.3 0.4 fusion.45
  144.8 0.8 multiply_subtract_fusion.1
  145.6 0.8 fusion.22
  146.4 0.8 fusion.32
  147.3 0.8 fusion.26
  148.1 0.8 fusion.28
  148.9 0.8 convolution_subtract_fusion.1
  149.8 0.8 convolution_add_fusion.2
  150.6 0.8 convolution_add_fusion.1
  151.5 0.9 multiply_subtract_fusion
  152.3 0.7 fusion.16
  153.0 0.7 fusion.20
  153.7 0.7 convolution_add_fusion
  154.4 0.7 convolution_subtract_fusion
  155.0 0.4 fusion.12
  155.5 0.4 fusion.6
  155.9 0.7 copy.75
  156.7 3.9 %all-to-all-start.2 = ((bf16[32,8,256]{2,1,0:T(8,128)(2,1)}), bf16[32,8,256]{2,1,0:T(8,128)(2,1)S(1)}, u32[]{:S(2)}, u32[]{:S(2)}) async-start(bf16[32,8,256]{2,1,0:T(8,128)(2,1)} %copy.75), calls=%async_computation.2 | async-start | bytes 262144 | tf_op jit(solution)/shard_map/all_to_all | solution.py:112
  160.6 0.1 reshape.55
  160.7 0.1 mul.171
  160.8 7.3 %all-to-all-done.2 = bf16[32,8,256]{2,1,0:T(8,128)(2,1)S(1)} async-done(((bf16[32,8,256]{2,1,0:T(8,128)(2,1)}), bf16[32,8,256]{2,1,0:T(8,128)(2,1)S(1)}, u32[]{:S(2)}, u32[]{:S(2)}) %all-to-all-start.2) | async-done | bytes 131104 | tf_op jit(solution)/shard_map/all_to_all | solution.py:112
  168.1 0.1 copy.76
  168.3 0.1 fusion.36
  168.3 0.1 copy.77
  168.5 6.5 %all_to_all.20 = bf16[2,128,256]{1,2,0:T(8,128)(2,1)S(1)} all-to-all(bf16[2,128,256]{1,2,0:T(8,128)(2,1)S(1)} %copy.77), channel_id=1, replica_groups=mesh['chip'=32,'core'=2,'mp'=4] {'core'}, dimensions={0} | all-to-all | bytes 262144 | tf_op jit(solution)/shard_map/all_to_all | solution.py:117
  175.0 0.8 copy.79
  (34 shorter events, 0.3 us)
Async XLA Ops:
  6.5 130.0 %copy-start = (f32[8,8192]{1,0:T(8,128)S(1)}, f32[8,8192]{1,0:T(8,128)}, u32[]{:S(2)}) copy-start(f32[8,8192]{1,0:T(8,128)} %param.14) | copy-start | bytes 786436
  11.4 58.6 %copy-start.7 = (f32[3,3,512]{2,1,0:T(4,128)S(1)}, f32[3,3,512]{2,1,0:T(4,128)}, u32[]{:S(2)}) copy-start(f32[3,3,512]{2,1,0:T(4,128)} %param.13) | copy-start | bytes 55300
  11.4 102.2 %all-to-all-start = ((bf16[64,64,3,256]{3,1,2,0:T(8,128)(2,1)}), bf16[64,64,3,256]{3,1,2,0:T(8,128)(2,1)}, u32[]{:S(2)}, u32[]{:S(2)}) async-start(bf16[64,64,3,256]{3,1,2,0:T(8,128)(2,1)} %bitcast.76), calls=%async_computation | async-start | bytes 12582912 | tf_op jit(solution)/shard_map/all_to_all | solution.py:95
  22.0 47.9 %all-gather.3.cloned.1.call-start = ((), (), s32[]{:S(2)}) async-start(), calls=%async_computation.4 | async-start | bytes 1310720 | tf_op jit(solution)/shard_map/all_gather | solution.py:91
  22.8 97.4 %all-gather.5.cloned.1.call-start = ((), (), s32[]{:S(2)}) async-start(), calls=%async_computation.5 | async-start | bytes 3145728 | tf_op jit(solution)/shard_map/all_gather | solution.py:91
  120.1 16.4 %copy-start.6 = (f32[64,32,1]{0,1,2:T(8,128)S(1)}, f32[64,32,1]{0,1,2:T(8,128)}, u32[]{:S(2)}) copy-start(f32[64,32,1]{0,1,2:T(8,128)} %constant.45) | copy-start | bytes 24580
  125.3 19.0 %copy-start.5 = (f32[64,32,1]{0,1,2:T(8,128)S(1)}, f32[64,32,1]{0,1,2:T(8,128)}, u32[]{:S(2)}) copy-start(f32[64,32,1]{0,1,2:T(8,128)} %constant.44) | copy-start | bytes 24580
  125.3 19.4 %copy-start.3 = (f32[64,256]{1,0:T(8,128)S(1)}, f32[64,256]{1,0:T(8,128)}, u32[]{:S(2)}) copy-start(f32[64,256]{1,0:T(8,128)} %constant.35.clone) | copy-start | bytes 196612
  125.4 19.4 %copy-start.4 = (f32[64,256]{1,0:T(8,128)S(1)}, f32[64,256]{1,0:T(8,128)}, u32[]{:S(2)}) copy-start(f32[64,256]{1,0:T(8,128)} %constant.34.clone) | copy-start | bytes 196612
  125.4 20.2 %copy-start.1 = (f32[256,256,1]{1,0,2:T(8,128)S(1)}, f32[256,256,1]{1,0,2:T(8,128)}, u32[]{:S(2)}) copy-start(f32[256,256,1]{1,0,2:T(8,128)} %constant.46) | copy-start | bytes 786436
  125.4 2.2 %collective-permute-start = (bf16[2,3,256]{2,0,1:T(2,128)(2,1)S(1)}, bf16[2,3,256]{2,0,1:T(2,128)(2,1)S(1)}, u32[]{:S(2)}, u32[]{:S(2)}) collective-permute-start(bf16[2,3,256]{2,0,1:T(2,128)(2,1)S(1)} %slice.57), channel_id=1, source_target_pairs={{0,8},{8,16},{16,24},{24,32},{32,40},{40,48},{48,56},{56,64},{64,7... | collective-permute-start | bytes 9224 | tf_op jit(solution)/shard_map/ppermute | solution.py:15
  127.9 21.1 %copy-start.2 = (f32[256,256,1]{1,0,2:T(8,128)S(1)}, f32[256,256,1]{1,0,2:T(8,128)}, u32[]{:S(2)}) copy-start(f32[256,256,1]{1,0,2:T(8,128)} %constant.47) | copy-start | bytes 786436
  128.7 15.2 %all-to-all-start.1 = ((bf16[32,8,256]{2,1,0:T(8,128)(2,1)}), bf16[32,8,256]{2,1,0:T(8,128)(2,1)S(1)}, u32[]{:S(2)}, u32[]{:S(2)}) async-start(bf16[32,8,256]{2,1,0:T(8,128)(2,1)} %bitcast.11), calls=%async_computation.1 | async-start | bytes 262144 | tf_op jit(solution)/shard_map/all_to_all | solution.py:110
  150.6 4.4 %copy-start.9 = (f32[32,64,1]{1,0,2:T(8,128)S(1)}, f32[32,64,1]{1,0,2:T(8,128)}, u32[]{:S(2)}) copy-start(f32[32,64,1]{1,0,2:T(8,128)} %constant.43) | copy-start | bytes 24580
  151.4 4.0 %copy-start.8 = (f32[32,64,1]{1,0,2:T(8,128)S(1)}, f32[32,64,1]{1,0,2:T(8,128)}, u32[]{:S(2)}) copy-start(f32[32,64,1]{1,0,2:T(8,128)} %constant.48) | copy-start | bytes 24580
  151.5 9.1 %copy-start.10 = (f32[512]{0:T(512)S(1)}, f32[512]{0:T(512)}, u32[]{:S(2)}) copy-start(f32[512]{0:T(512)} %param.15) | copy-start | bytes 6148
  156.7 11.4 %all-to-all-start.2 = ((bf16[32,8,256]{2,1,0:T(8,128)(2,1)}), bf16[32,8,256]{2,1,0:T(8,128)(2,1)S(1)}, u32[]{:S(2)}, u32[]{:S(2)}) async-start(bf16[32,8,256]{2,1,0:T(8,128)(2,1)} %copy.75), calls=%async_computation.2 | async-start | bytes 262144 | tf_op jit(solution)/shard_map/all_to_all | solution.py:112
Sparse Core Ops, SparseCore 0:
  24.6 45.2 all-gather.2
  71.8 14.0 all-gather.4

commit v4 on v2

--- a/solution.py
+++ b/solution.py
@@ -88,23 +88,28 @@
     half = width // 2
     chips = lax.axis_size("chip")
     parity = lax.axis_index("core")
+    split = w_proj.reshape(w_proj.shape[0], 3, width // (2 * GROUP), 2, GROUP)
+    weights = []
+    for member in range(3):
+        part = jnp.moveaxis(split[:, member], 2, 0).reshape(1, 2, w_proj.shape[0], half)
+        spread = jnp.broadcast_to(part, (chips, 2) + part.shape[2:]).reshape((2 * chips,) + part.shape[2:])
+        arrived = lax.all_to_all(spread, ("chip", "core"), split_axis=0, concat_axis=0, tiled=True)
+        weights.append(arrived.reshape(2 * chips * w_proj.shape[0], half))
     source = lax.all_gather(lax.all_gather(tokens, "mp", axis=1, tiled=True), "core", axis=0, tiled=True)
-    split = w_proj.reshape(w_proj.shape[0], 3, width // (2 * GROUP), 2, GROUP)
-    split = jnp.moveaxis(split, 3, 0).reshape(2, w_proj.shape[0], 3, half)
-    paired = lax.all_to_all(split, "core", split_axis=0, concat_axis=0, tiled=True)
-    weights = lax.all_gather(paired.reshape(2 * w_proj.shape[0], 3, half), "chip", axis=0, tiled=True)
-    projected = jnp.einsum(
-        "td,dpc->tpc", source, weights, preferred_element_type=jnp.float32
-    ).astype(jnp.bfloat16)
     rows = source.shape[0]
-    tail = shifted(projected[rows - margin :], "chip", 1)
-    extended = jnp.concatenate([tail, projected], axis=0).astype(jnp.float32)
+    tail = shifted(source[rows - margin :], "chip", 1)
+    extended_tokens = jnp.concatenate([tail, source], axis=0)
     taps = pick(short_filter, 2, parity)
-    mixed = jnp.zeros((rows, 3, half), jnp.float32)
-    for offset in range(margin + 1):
-        mixed = mixed + taps[:, offset, :][None] * extended[margin - offset : margin - offset + rows]
-    query_rows = mixed[:, 0]
-    product = (mixed[:, 1] * mixed[:, 2]).astype(jnp.bfloat16)
+    mixed = []
+    for member in range(3):
+        projected = jnp.dot(extended_tokens, weights[member], preferred_element_type=jnp.float32)
+        extended = projected.astype(jnp.bfloat16).astype(jnp.float32)
+        total = jnp.zeros((rows, half), jnp.float32)
+        for offset in range(margin + 1):
+            total = total + taps[member, offset][None] * extended[margin - offset : margin - offset + rows]
+        mixed.append(total)
+    query_rows = mixed[0]
+    product = (mixed[1] * mixed[2]).astype(jnp.bfloat16)
     outgoing = product.T.reshape(chips, GROUP, rows)
     arrived = lax.all_to_all(outgoing, "chip", split_axis=0, concat_axis=0, tiled=True)
     convolved = long_conv(arrived, long_filter).astype(jnp.bfloat16)

time: 297 us -> 182 us (0.61)
  waiting for transfers between devices: 210 us -> 92 us
  blocking collectives: 33.6 us -> 5.33 us
  starting transfers between devices: 15 us -> 37.8 us
  local copies, waits for them, and re-layouts: 6.72 us -> 11.2 us
    all_gather x1 -> x0, waiting for transfers between devices: 146 us -> none  [on_device(): lax.all_gather(paired.reshape(2 * w_proj.shape[0], 3, half), 'chip', axis...]
    all_to_all x0 -> x3, waiting for transfers between devices: none -> 55.9 us  [on_device(): lax.all_to_all(spread, ('chip', 'core'), split_axis=0, concat_axis=0, til...]
    all_gather x1, waiting for transfers between devices: 39.7 us -> 0.02 us  [on_device(): lax.all_gather(tokens, 'mp', axis=1, tiled=True)]
    all_to_all x1, blocking collectives: 28.4 us -> 5.33 us  [on_device(): lax.all_to_all(local, 'core', split_axis=0, concat_axis=0, tiled=True)]
    all_to_all x0 -> x3, starting transfers between devices: none -> 22.7 us  [on_device(): lax.all_to_all(spread, ('chip', 'core'), split_axis=0, concat_axis=0, til...]
    all_gather x1, waiting for transfers between devices: 8.64 us -> 22.1 us  [on_device(): lax.all_gather(lax.all_gather(tokens, 'mp', axis=1, tiled=True), 'core',...]
    all_to_all x1 -> x0, blocking collectives: 5.16 us -> none  [on_device(): lax.all_to_all(split, 'core', split_axis=0, concat_axis=0, tiled=True)]
    broadcast_in_dim x0 -> x7, local copies, waits for them, and re-layouts: none -> 5.08 us  [on_device(): jnp.broadcast_to(part, (chips, 2) + part.shape[2:])]
  transfers between devices with their start and end apart: 6 -> 8, of which waited for: 6 -> 6; matrix products, arithmetic and copies ran while one was open for 2% -> 12% of each run, Pallas kernels for 0% -> 0%
where the time goes in v4:
time: 182 us; the launch traced here: 181 us
  waiting for transfers between devices  92 us (51%)
  starting transfers between devices  37.8 us (21%)
  matrix products  20.1 us (11%)
  between operations  13.9 us (8%)
  local copies, waits for them, and re-layouts  11.2 us (6%)
  blocking collectives  5.33 us (3%)
    all_to_all x3, waiting for transfers between devices, on_device(): lax.all_to_all(spread, ('chip', 'core'), split_axis=0, concat_axis=0, til...  55.9 us
    all_to_all x3, starting transfers between devices, on_device(): lax.all_to_all(spread, ('chip', 'core'), split_axis=0, concat_axis=0, til...  22.7 us
    all_gather x1, waiting for transfers between devices, on_device(): lax.all_gather(lax.all_gather(tokens, 'mp', axis=1, tiled=True), 'core',...  22.1 us
    all_to_all x1, starting transfers between devices, on_device(): lax.all_to_all(outgoing, 'chip', split_axis=0, concat_axis=0, tiled=True)  8.31 us
    dot_general x3, matrix products, on_device(): jnp.dot(extended_tokens, weights[member], preferred_element_type=jnp.floa...  7.7 us
    dot_general x8, matrix products, forward(): dot = lambda a, m: jnp.einsum('krn,nm->krm', a, m, precision=HIGHEST)  6.63 us
    all_to_all x1, waiting for transfers between devices, on_device(): lax.all_to_all(outgoing, 'chip', split_axis=0, concat_axis=0, tiled=True)  6.52 us
    all_to_all x1, blocking collectives, on_device(): lax.all_to_all(local, 'core', split_axis=0, concat_axis=0, tiled=True)  5.33 us
  transfers between devices with their start and end apart: 8, of which 6 were waited for; matrix products, arithmetic and copies ran while one was open for 12% of the time, Pallas kernels for 0%

profile of v4, /device:TPU:1, one launch (start us, length us, event | category | flops | bytes accessed | tf_op | source)
XLA Modules:
  0.0 180.7 jit_solution(17260625778658688980)
XLA Ops:
  6.5 1.2 copy.57
  7.9 1.6 broadcast_in_dim.32
  9.5 10.3 %all-to-all-start.2 = ((bf16[64,64,256]{2,1,0:T(8,128)(2,1)}), bf16[64,64,256]{2,1,0:T(8,128)(2,1)S(1)}, u32[]{:S(2)}, u32[]{:S(2)}) async-start(bf16[64,64,256]{2,1,0:T(8,128)(2,1)} %bitcast.23), calls=%async_computation.2 | async-start | bytes 4194304 | tf_op jit(solution)/shard_map/all_to_all | solution.py:96
  19.9 0.7 all-gather.3.cloned.1.call-update
  20.7 39.8 %all-to-all-done.2 = bf16[64,64,256]{2,1,0:T(8,128)(2,1)S(1)} async-done(((bf16[64,64,256]{2,1,0:T(8,128)(2,1)}), bf16[64,64,256]{2,1,0:T(8,128)(2,1)S(1)}, u32[]{:S(2)}, u32[]{:S(2)}) %all-to-all-start.2) | async-done | bytes 2097184 | tf_op jit(solution)/shard_map/all_to_all | solution.py:96
  60.5 1.6 broadcast_in_dim.30
  62.1 5.3 %all-to-all-start.1 = ((bf16[64,64,256]{2,1,0:T(8,128)(2,1)}), bf16[64,64,256]{2,1,0:T(8,128)(2,1)}, u32[]{:S(2)}, u32[]{:S(2)}) async-start(bf16[64,64,256]{2,1,0:T(8,128)(2,1)} %bitcast.15), calls=%async_computation.1 | async-start | bytes 4194304 | tf_op jit(solution)/shard_map/all_to_all | solution.py:96
  67.5 0.7 all-gather.5.cloned.1.call-update
  68.2 0.5 reshape.68
  68.6 0.4 dynamic-slice_reduce_fusion
  69.2 22.1 %all-gather.5.cloned.1.call-done = bf16[256,4096]{1,0:T(8,128)(2,1)} async-done(((bf16[128,4096]{1,0:T(8,128)(2,1)}), bf16[256,4096]{1,0:T(8,128)(2,1)}) %all-gather.5.cloned.1.call-update) | async-done | bytes 2097168 | tf_op jit(solution)/shard_map/all_gather | solution.py:98
  91.3 0.9 slice.105
  92.2 2.8 %collective-permute-start = (bf16[2,4096]{1,0:T(2,128)(2,1)S(1)}, bf16[2,4096]{1,0:T(2,128)(2,1)S(1)}, u32[]{:S(2)}, u32[]{:S(2)}) collective-permute-start(bf16[2,4096]{1,0:T(2,128)(2,1)S(1)} %slice.105), channel_id=1, source_target_pairs={{0,8},{8,16},{16,24},{24,32},{32,40},{40,48},{48,56},{56,64},{64,7... | collective-permute-start | bytes 49160 | tf_op jit(solution)/shard_map/ppermute | solution.py:15
  95.0 0.8 collective-permute-done
  95.9 2.4 %fusion.1 = f32[258,256]{1,0:T(8,128)S(1)} fusion(bf16[4096,256]{1,0:T(8,128)(2,1)S(1)} %bitcast.83, bf16[256,4096]{1,0:T(8,128)(2,1)} %all-gather.5.cloned.1.call-done, bf16[2,4096]{1,0:T(2,128)(2,1)S(1)} %collective-permute-done), kind=kOutput, calls=%fused_computation.12 | convolution fusion | flops 545424384 | bytes 4474880 | tf_op jit(solution)/shard_map/dot_general | solution.py:105
  98.3 3.0 %fusion.2 = f32[258,256]{1,0:T(8,128)S(1)} fusion(bf16[4096,256]{1,0:T(8,128)(2,1)} %bitcast.16, bf16[256,4096]{1,0:T(8,128)(2,1)} %all-gather.5.cloned.1.call-done, bf16[2,4096]{1,0:T(2,128)(2,1)S(1)} %collective-permute-done), kind=kOutput, calls=%fused_computation.14 | convolution fusion | flops 545424384 | bytes 4474880 | tf_op jit(solution)/shard_map/dot_general | solution.py:105
  101.3 0.2 fusion.32
  101.4 0.8 copy.64
  102.2 8.3 %all-to-all-start.3 = ((bf16[32,8,256]{2,1,0:T(8,128)(2,1)}), bf16[32,8,256]{2,1,0:T(8,128)(2,1)S(1)}, u32[]{:S(2)}, u32[]{:S(2)}) async-start(bf16[32,8,256]{2,1,0:T(8,128)(2,1)} %bitcast.28), calls=%async_computation.3 | async-start | bytes 262144 | tf_op jit(solution)/shard_map/all_to_all | solution.py:114
  110.9 0.6 convolution_negate_fusion
  111.6 6.5 %all-to-all-done.3 = bf16[32,8,256]{2,1,0:T(8,128)(2,1)S(1)} async-done(((bf16[32,8,256]{2,1,0:T(8,128)(2,1)}), bf16[32,8,256]{2,1,0:T(8,128)(2,1)S(1)}, u32[]{:S(2)}, u32[]{:S(2)}) %all-to-all-start.3) | async-done | bytes 131104 | tf_op jit(solution)/shard_map/all_to_all | solution.py:114
  118.1 1.5 broadcast_in_dim.13
  119.6 7.1 %all-to-all-start = ((bf16[64,64,256]{2,1,0:T(8,128)(2,1)}), bf16[64,64,256]{2,1,0:T(8,128)(2,1)S(1)}, u32[]{:S(2)}, u32[]{:S(2)}) async-start(bf16[64,64,256]{2,1,0:T(8,128)(2,1)} %bitcast.5), calls=%async_computation | async-start | bytes 4194304 | tf_op jit(solution)/shard_map/all_to_all | solution.py:96
  126.7 0.4 fusion
  127.2 0.4 fusion.48
  127.6 0.8 multiply_subtract_fusion.1
  128.6 0.8 fusion.22
  129.4 0.8 fusion.28
  130.2 0.8 fusion.18
  131.1 0.8 fusion.24
  131.9 0.8 convolution_add_fusion.1
  132.7 0.8 convolution_add_fusion.2
  133.6 0.8 convolution_subtract_fusion.1
  134.4 0.9 multiply_subtract_fusion
  135.3 0.7 fusion.16
  135.9 0.7 fusion.12
  136.6 0.7 convolution_subtract_fusion
  137.3 0.7 convolution_add_fusion
  138.0 0.4 fusion.8
  138.4 0.5 fusion.4
  138.9 0.7 copy.81
  139.6 16.2 %all-to-all-done = bf16[64,64,256]{2,1,0:T(8,128)(2,1)S(1)} async-done(((bf16[64,64,256]{2,1,0:T(8,128)(2,1)}), bf16[64,64,256]{2,1,0:T(8,128)(2,1)S(1)}, u32[]{:S(2)}, u32[]{:S(2)}) %all-to-all-start) | async-done | bytes 2097184 | tf_op jit(solution)/shard_map/all_to_all | solution.py:96
  155.8 3.9 %all-to-all-start.4 = ((bf16[32,8,256]{2,1,0:T(8,128)(2,1)}), bf16[32,8,256]{2,1,0:T(8,128)(2,1)S(1)}, u32[]{:S(2)}, u32[]{:S(2)}) async-start(bf16[32,8,256]{2,1,0:T(8,128)(2,1)} %copy.81), calls=%async_computation.4 | async-start | bytes 262144 | tf_op jit(solution)/shard_map/all_to_all | solution.py:116
  159.7 2.4 %fusion.3 = f32[258,256]{1,0:T(8,128)S(1)} fusion(bf16[4096,256]{1,0:T(8,128)(2,1)S(1)} %bitcast.84, bf16[256,4096]{1,0:T(8,128)(2,1)} %all-gather.5.cloned.1.call-done, bf16[2,4096]{1,0:T(2,128)(2,1)S(1)} %collective-permute-done), kind=kOutput, calls=%fused_computation.16 | convolution fusion | flops 545424384 | bytes 4474880 | tf_op jit(solution)/shard_map/dot_general | solution.py:105
  162.1 5.2 %all-to-all-done.4 = bf16[32,8,256]{2,1,0:T(8,128)(2,1)S(1)} async-done(((bf16[32,8,256]{2,1,0:T(8,128)(2,1)}), bf16[32,8,256]{2,1,0:T(8,128)(2,1)S(1)}, u32[]{:S(2)}, u32[]{:S(2)}) %all-to-all-start.4) | async-done | bytes 131104 | tf_op jit(solution)/shard_map/all_to_all | solution.py:116
  167.3 0.1 copy.82
  167.7 5.3 %all_to_all.30 = bf16[2,128,256]{1,2,0:T(8,128)(2,1)S(1)} all-to-all(bf16[2,128,256]{1,2,0:T(8,128)(2,1)S(1)} %copy.83), channel_id=1, replica_groups=mesh['chip'=32,'core'=2,'mp'=4] {'core'}, dimensions={0} | all-to-all | bytes 262144 | tf_op jit(solution)/shard_map/all_to_all | solution.py:121
  173.1 0.8 copy.85
  (41 shorter events, 1.3 us)
Async XLA Ops:
  6.5 104.4 %copy-start = (f32[8,8192]{1,0:T(8,128)S(1)}, f32[8,8192]{1,0:T(8,128)}, u32[]{:S(2)}) copy-start(f32[8,8192]{1,0:T(8,128)} %param.14) | copy-start | bytes 786436
  9.5 50.9 %all-to-all-start.2 = ((bf16[64,64,256]{2,1,0:T(8,128)(2,1)}), bf16[64,64,256]{2,1,0:T(8,128)(2,1)S(1)}, u32[]{:S(2)}, u32[]{:S(2)}) async-start(bf16[64,64,256]{2,1,0:T(8,128)(2,1)} %bitcast.23), calls=%async_computation.2 | async-start | bytes 4194304 | tf_op jit(solution)/shard_map/all_to_all | solution.py:96
  19.9 47.6 %all-gather.3.cloned.1.call-start = ((), (), s32[]{:S(2)}) async-start(), calls=%async_computation.6 | async-start | bytes 1310720 | tf_op jit(solution)/shard_map/all_gather | solution.py:98
  62.1 6.1 %copy-start.7 = (f32[3,3,512]{2,1,0:T(4,128)S(1)}, f32[3,3,512]{2,1,0:T(4,128)}, u32[]{:S(2)}) copy-start(f32[3,3,512]{2,1,0:T(4,128)} %param.13) | copy-start | bytes 55300
  62.1 36.2 %all-to-all-start.1 = ((bf16[64,64,256]{2,1,0:T(8,128)(2,1)}), bf16[64,64,256]{2,1,0:T(8,128)(2,1)}, u32[]{:S(2)}, u32[]{:S(2)}) async-start(bf16[64,64,256]{2,1,0:T(8,128)(2,1)} %bitcast.15), calls=%async_computation.1 | async-start | bytes 4194304 | tf_op jit(solution)/shard_map/all_to_all | solution.py:96
  67.4 23.9 %all-gather.5.cloned.1.call-start = ((), (), s32[]{:S(2)}) async-start(), calls=%async_computation.7 | async-start | bytes 3145728 | tf_op jit(solution)/shard_map/all_gather | solution.py:98
  92.2 3.7 %collective-permute-start = (bf16[2,4096]{1,0:T(2,128)(2,1)S(1)}, bf16[2,4096]{1,0:T(2,128)(2,1)S(1)}, u32[]{:S(2)}, u32[]{:S(2)}) collective-permute-start(bf16[2,4096]{1,0:T(2,128)(2,1)S(1)} %slice.105), channel_id=1, source_target_pairs={{0,8},{8,16},{16,24},{24,32},{32,40},{40,48},{48,56},{56,64},{64,7... | collective-permute-start | bytes 49160 | tf_op jit(solution)/shard_map/ppermute | solution.py:15
  101.2 9.4 %copy-start.10 = (f32[512]{0:T(512)S(1)}, f32[512]{0:T(512)}, u32[]{:S(2)}) copy-start(f32[512]{0:T(512)} %param.15) | copy-start | bytes 6148
  101.2 9.7 %copy-start.6 = (f32[64,32,1]{0,1,2:T(8,128)S(1)}, f32[64,32,1]{0,1,2:T(8,128)}, u32[]{:S(2)}) copy-start(f32[64,32,1]{0,1,2:T(8,128)} %constant.45) | copy-start | bytes 24580
  102.2 15.9 %all-to-all-start.3 = ((bf16[32,8,256]{2,1,0:T(8,128)(2,1)}), bf16[32,8,256]{2,1,0:T(8,128)(2,1)S(1)}, u32[]{:S(2)}, u32[]{:S(2)}) async-start(bf16[32,8,256]{2,1,0:T(8,128)(2,1)} %bitcast.28), calls=%async_computation.3 | async-start | bytes 262144 | tf_op jit(solution)/shard_map/all_to_all | solution.py:114
  119.6 7.5 %copy-start.5 = (f32[64,32,1]{0,1,2:T(8,128)S(1)}, f32[64,32,1]{0,1,2:T(8,128)}, u32[]{:S(2)}) copy-start(f32[64,32,1]{0,1,2:T(8,128)} %constant.44) | copy-start | bytes 24580
  119.6 7.9 %copy-start.3 = (f32[64,256]{1,0:T(8,128)S(1)}, f32[64,256]{1,0:T(8,128)}, u32[]{:S(2)}) copy-start(f32[64,256]{1,0:T(8,128)} %constant.34.clone) | copy-start | bytes 196612
  119.6 7.9 %copy-start.4 = (f32[64,256]{1,0:T(8,128)S(1)}, f32[64,256]{1,0:T(8,128)}, u32[]{:S(2)}) copy-start(f32[64,256]{1,0:T(8,128)} %constant.35.clone) | copy-start | bytes 196612
  119.6 36.2 %all-to-all-start = ((bf16[64,64,256]{2,1,0:T(8,128)(2,1)}), bf16[64,64,256]{2,1,0:T(8,128)(2,1)S(1)}, u32[]{:S(2)}, u32[]{:S(2)}) async-start(bf16[64,64,256]{2,1,0:T(8,128)(2,1)} %bitcast.5), calls=%async_computation | async-start | bytes 4194304 | tf_op jit(solution)/shard_map/all_to_all | solution.py:96
  127.6 1.0 copy-start.1
  129.4 2.5 %copy-start.2 = (f32[256,256,1]{1,0,2:T(8,128)S(1)}, f32[256,256,1]{1,0,2:T(8,128)}, u32[]{:S(2)}) copy-start(f32[256,256,1]{1,0,2:T(8,128)} %constant.47) | copy-start | bytes 786436
  136.6 1.4 copy-start.9
  137.3 1.1 copy-start.8
  155.8 11.5 %all-to-all-start.4 = ((bf16[32,8,256]{2,1,0:T(8,128)(2,1)}), bf16[32,8,256]{2,1,0:T(8,128)(2,1)S(1)}, u32[]{:S(2)}, u32[]{:S(2)}) async-start(bf16[32,8,256]{2,1,0:T(8,128)(2,1)} %copy.81), calls=%async_computation.4 | async-start | bytes 262144 | tf_op jit(solution)/shard_map/all_to_all | solution.py:116
Sparse Core Ops, SparseCore 0:
  22.5 43.4 all-gather.2
  70.0 21.2 all-gather.4

commit v5 on v4

--- a/solution.py
+++ b/solution.py
@@ -89,20 +89,23 @@
     chips = lax.axis_size("chip")
     parity = lax.axis_index("core")
     split = w_proj.reshape(w_proj.shape[0], 3, width // (2 * GROUP), 2, GROUP)
-    weights = []
-    for member in range(3):
+    weights = [lax.all_gather(w_proj[:, 0], ("chip", "core"), axis=0, tiled=True)]
+    for member in range(1, 3):
         part = jnp.moveaxis(split[:, member], 2, 0).reshape(1, 2, w_proj.shape[0], half)
         spread = jnp.broadcast_to(part, (chips, 2) + part.shape[2:]).reshape((2 * chips,) + part.shape[2:])
         arrived = lax.all_to_all(spread, ("chip", "core"), split_axis=0, concat_axis=0, tiled=True)
         weights.append(arrived.reshape(2 * chips * w_proj.shape[0], half))
-    source = lax.all_gather(lax.all_gather(tokens, "mp", axis=1, tiled=True), "core", axis=0, tiled=True)
-    rows = source.shape[0]
+    stacked = lax.all_gather(tokens, ("core", "mp"), axis=0, tiled=False)
+    rows = 2 * rows_dev
+    source = jnp.transpose(stacked.reshape(2, -1, rows_dev, tokens.shape[1]), (0, 2, 1, 3)).reshape(rows, -1)
     tail = shifted(source[rows - margin :], "chip", 1)
     extended_tokens = jnp.concatenate([tail, source], axis=0)
     taps = pick(short_filter, 2, parity)
     mixed = []
     for member in range(3):
         projected = jnp.dot(extended_tokens, weights[member], preferred_element_type=jnp.float32)
+        if member == 0:
+            projected = pick(projected, 1, parity)
         extended = projected.astype(jnp.bfloat16).astype(jnp.float32)
         total = jnp.zeros((rows, half), jnp.float32)
         for offset in range(margin + 1):

time: 182 us -> 206 us (1.13)
  waiting for transfers between devices: 92 us -> 121 us
  starting transfers between devices: 37.8 us -> 28.6 us
  local copies, waits for them, and re-layouts: 11.2 us -> 15.3 us
    all_gather x2, waiting for transfers between devices: 22.1 us -> 49.2 us  [the longest x1 49.2 us: on_device(): lax.all_gather(w_proj[:, 0], ('chip', 'core'), axis=0, tiled=True)]
    all_to_all x3 -> x2, starting transfers between devices: 22.7 us -> 16 us  [on_device(): lax.all_to_all(spread, ('chip', 'core'), split_axis=0, concat_axis=0, til...]
    all_to_all x1, starting transfers between devices: 8.31 us -> 5.09 us  [on_device(): lax.all_to_all(outgoing, 'chip', split_axis=0, concat_axis=0, tiled=True)]
    reshape x0 -> x1, local copies, waits for them, and re-layouts: none -> 3.21 us  [on_device(): stacked.reshape(2, -1, rows_dev, tokens.shape[1])]
    ppermute x1, waiting for transfers between devices: 0.83 us -> 3.02 us  [shifted(): lax.ppermute(value, axis, [(source, source + steps) for source in range(l...]
    slice x0 -> x5, local copies, waits for them, and re-layouts: none -> 2.07 us  [the longest x1 1.48 us: on_device(): w_proj[:, 0]]
    all_to_all x3 -> x2, waiting for transfers between devices: 55.9 us -> 54.4 us  [on_device(): lax.all_to_all(spread, ('chip', 'core'), split_axis=0, concat_axis=0, til...]
    broadcast_in_dim x7 -> x5, local copies, waits for them, and re-layouts: 5.08 us -> 3.65 us  [on_device(): jnp.broadcast_to(part, (chips, 2) + part.shape[2:])]
  transfers between devices with their start and end apart: 8 -> 7, of which waited for: 6 -> 6; matrix products, arithmetic and copies ran while one was open for 12% -> 13% of each run, Pallas kernels for 0% -> 0%
where the time goes in v5:
time: 206 us; the launch traced here: 204 us
  waiting for transfers between devices  121 us (59%)
  starting transfers between devices  28.6 us (14%)
  matrix products  20.4 us (10%)
  local copies, waits for them, and re-layouts  15.3 us (7%)
  between operations  13.9 us (7%)
  blocking collectives  3.77 us (2%)
    all_to_all x2, waiting for transfers between devices, on_device(): lax.all_to_all(spread, ('chip', 'core'), split_axis=0, concat_axis=0, til...  54.4 us
    all_gather x1, waiting for transfers between devices, on_device(): lax.all_gather(w_proj[:, 0], ('chip', 'core'), axis=0, tiled=True)  49.2 us
    all_to_all x2, starting transfers between devices, on_device(): lax.all_to_all(spread, ('chip', 'core'), split_axis=0, concat_axis=0, til...  16 us
    dot_general x3, matrix products, on_device(): jnp.dot(extended_tokens, weights[member], preferred_element_type=jnp.floa...  7.78 us
    all_to_all x1, waiting for transfers between devices, on_device(): lax.all_to_all(convolved, 'chip', split_axis=0, concat_axis=0, tiled=True)  7.29 us
    all_to_all x1, waiting for transfers between devices, on_device(): lax.all_to_all(outgoing, 'chip', split_axis=0, concat_axis=0, tiled=True)  6.75 us
    dot_general x8, matrix products, forward(): dot = lambda a, m: jnp.einsum('krn,nm->krm', a, m, precision=HIGHEST)  6.63 us
    all_to_all x1, starting transfers between devices, on_device(): lax.all_to_all(outgoing, 'chip', split_axis=0, concat_axis=0, tiled=True)  5.09 us
  transfers between devices with their start and end apart: 7, of which 6 were waited for; matrix products, arithmetic and copies ran while one was open for 13% of the time, Pallas kernels for 0%

profile of v5, /device:TPU:1, one launch (start us, length us, event | category | flops | bytes accessed | tf_op | source)
XLA Modules:
  0.0 203.7 jit_solution(7690702829475280887)
XLA Ops:
  6.5 1.2 copy.65
  7.9 1.6 broadcast_in_dim.9
  9.5 10.3 %all-to-all-start = ((bf16[64,64,256]{2,1,0:T(8,128)(2,1)}), bf16[64,64,256]{2,1,0:T(8,128)(2,1)S(1)}, u32[]{:S(2)}, u32[]{:S(2)}) async-start(bf16[64,64,256]{2,1,0:T(8,128)(2,1)} %bitcast.17), calls=%async_computation | async-start | bytes 4194304 | tf_op jit(solution)/shard_map/all_to_all | solution.py:96
  19.9 0.7 all-gather.5.cloned.1.call-update
  20.7 39.2 %all-to-all-done = bf16[64,64,256]{2,1,0:T(8,128)(2,1)S(1)} async-done(((bf16[64,64,256]{2,1,0:T(8,128)(2,1)}), bf16[64,64,256]{2,1,0:T(8,128)(2,1)S(1)}, u32[]{:S(2)}, u32[]{:S(2)}) %all-to-all-start) | async-done | bytes 2097184 | tf_op jit(solution)/shard_map/all_to_all | solution.py:96
  59.9 1.8 broadcast_in_dim.11
  61.7 0.2 copy-done.3
  61.9 5.7 %all-to-all-start.1 = ((bf16[64,64,256]{2,1,0:T(8,128)(2,1)}), bf16[64,64,256]{2,1,0:T(8,128)(2,1)}, u32[]{:S(2)}, u32[]{:S(2)}) async-start(bf16[64,64,256]{2,1,0:T(8,128)(2,1)} %bitcast.25), calls=%async_computation.1 | async-start | bytes 4194304 | tf_op jit(solution)/shard_map/all_to_all | solution.py:96
  67.7 1.5 slice.89
  69.2 0.5 reshape.76
  69.7 0.4 dynamic-slice_reduce_fusion
  70.3 3.2 %copy.60 = bf16[2,4,128,1024]{3,1,2,0:T(4,128)(2,1)S(1)} copy(bf16[2,4,128,1024]{3,2,1,0:T(8,128)(2,1)} %bitcast.96) | data formatting | bytes 4194304 | tf_op jit(solution)/shard_map/reshape | solution.py:100
  73.5 0.9 copy.99
  74.4 3.3 %collective-permute-start = (bf16[2,4096]{1,0:T(2,128)(2,1)S(1)}, bf16[2,4096]{1,0:T(2,128)(2,1)S(1)}, u32[]{:S(2)}, u32[]{:S(2)}) collective-permute-start(bf16[2,4096]{1,0:T(2,128)(2,1)S(1)} %slice.117), channel_id=1, source_target_pairs={{0,8},{8,16},{16,24},{24,32},{32,40},{40,48},{48,56},{56,64},{64,7... | collective-permute-start | bytes 49160 | tf_op jit(solution)/shard_map/ppermute | solution.py:15
  77.7 3.0 %collective-permute-done = bf16[2,4096]{1,0:T(2,128)(2,1)S(1)} collective-permute-done((bf16[2,4096]{1,0:T(2,128)(2,1)S(1)}, bf16[2,4096]{1,0:T(2,128)(2,1)S(1)}, u32[]{:S(2)}, u32[]{:S(2)}) %collective-permute-start) | collective-permute-done | bytes 16416 | tf_op jit(solution)/shard_map/ppermute | solution.py:15
  80.7 0.8 fusion.4
  81.5 15.2 %all-to-all-done.1 = bf16[64,64,256]{2,1,0:T(8,128)(2,1)} async-done(((bf16[64,64,256]{2,1,0:T(8,128)(2,1)}), bf16[64,64,256]{2,1,0:T(8,128)(2,1)}, u32[]{:S(2)}, u32[]{:S(2)}) %all-to-all-start.1) | async-done | bytes 2097184 | tf_op jit(solution)/shard_map/all_to_all | solution.py:96
  96.7 2.4 %fusion.3 = f32[258,256]{1,0:T(8,128)S(1)} fusion(bf16[4096,256]{1,0:T(8,128)(2,1)} %bitcast.26, bf16[256,4096]{1,0:T(8,128)(2,1)S(1)} %bitcast.93, bf16[2,4096]{1,0:T(2,128)(2,1)S(1)} %collective-permute-done), kind=kOutput, calls=%fused_computation.14 | convolution fusion | flops 545424384 | bytes 4474880 | tf_op jit(solution)/shard_map/dot_general | solution.py:106
  99.1 0.2 fusion.33
  99.3 0.8 copy.70
  100.1 5.1 %all-to-all-start.2 = ((bf16[32,8,256]{2,1,0:T(8,128)(2,1)}), bf16[32,8,256]{2,1,0:T(8,128)(2,1)S(1)}, u32[]{:S(2)}, u32[]{:S(2)}) async-start(bf16[32,8,256]{2,1,0:T(8,128)(2,1)} %bitcast.30), calls=%async_computation.2 | async-start | bytes 262144 | tf_op jit(solution)/shard_map/all_to_all | solution.py:117
  105.2 0.6 convolution_negate_fusion
  105.8 6.7 %all-to-all-done.2 = bf16[32,8,256]{2,1,0:T(8,128)(2,1)S(1)} async-done(((bf16[32,8,256]{2,1,0:T(8,128)(2,1)}), bf16[32,8,256]{2,1,0:T(8,128)(2,1)S(1)}, u32[]{:S(2)}, u32[]{:S(2)}) %all-to-all-start.2) | async-done | bytes 131104 | tf_op jit(solution)/shard_map/all_to_all | solution.py:117
  112.6 0.4 fusion.2
  113.0 0.4 fusion.48
  113.5 0.8 multiply_subtract_fusion.1
  114.4 0.8 fusion.23
  115.3 0.8 fusion.29
  116.1 0.8 fusion.19
  116.9 0.8 fusion.25
  117.8 0.8 convolution_add_fusion.1
  118.6 0.8 convolution_add_fusion.2
  119.4 0.8 convolution_subtract_fusion.1
  120.2 0.9 multiply_subtract_fusion
  121.1 0.7 fusion.17
  121.8 0.7 fusion.13
  122.5 0.7 convolution_subtract_fusion
  123.2 0.7 convolution_add_fusion
  123.9 0.5 fusion.9
  124.3 0.7 fusion.5
  125.0 0.7 copy.87
  125.7 4.1 %all-to-all-start.3 = ((bf16[32,8,256]{2,1,0:T(8,128)(2,1)}), bf16[32,8,256]{2,1,0:T(8,128)(2,1)S(1)}, u32[]{:S(2)}, u32[]{:S(2)}) async-start(bf16[32,8,256]{2,1,0:T(8,128)(2,1)} %copy.87), calls=%async_computation.3 | async-start | bytes 262144 | tf_op jit(solution)/shard_map/all_to_all | solution.py:119
  130.1 7.3 %all-to-all-done.3 = bf16[32,8,256]{2,1,0:T(8,128)(2,1)S(1)} async-done(((bf16[32,8,256]{2,1,0:T(8,128)(2,1)}), bf16[32,8,256]{2,1,0:T(8,128)(2,1)S(1)}, u32[]{:S(2)}, u32[]{:S(2)}) %all-to-all-start.3) | async-done | bytes 131104 | tf_op jit(solution)/shard_map/all_to_all | solution.py:119
  137.6 49.2 %all-gather.7.cloned.1.call-done = bf16[4096,1,512]{2,0,1:T(8,128)(2,1)} async-done(((bf16[64,1,512]{2,0,1:T(8,128)(2,1)}), bf16[4096,1,512]{2,0,1:T(8,128)(2,1)}) %all-gather.7.cloned.1.call-update) | async-done | bytes 4194320 | tf_op jit(solution)/shard_map/all_gather | solution.py:92
  186.8 4.6 %fusion = bf16[258,512]{0,1:T(8,128)(2,1)S(1)} fusion(bf16[4096,1,512]{2,0,1:T(8,128)(2,1)} %all-gather.7.cloned.1.call-done, bf16[256,4096]{1,0:T(8,128)(2,1)S(1)} %bitcast.94, bf16[2,4096]{1,0:T(2,128)(2,1)S(1)} %collective-permute-done), kind=kOutput, calls=%fused_computation | convolution fusion | flops 1086357504 | bytes 6572032 | tf_op jit(solution)/shard_map/dot_general | solution.py:106
  191.5 0.2 slice_bitcast_fusion.2
  192.3 3.8 %all_to_all.25 = bf16[2,128,256]{1,2,0:T(8,128)(2,1)S(1)} all-to-all(bf16[2,128,256]{1,2,0:T(8,128)(2,1)S(1)} %copy.89), channel_id=1, replica_groups=mesh['chip'=32,'core'=2,'mp'=4] {'core'}, dimensions={0} | all-to-all | bytes 262144 | tf_op jit(solution)/shard_map/all_to_all | solution.py:124
  196.1 0.8 copy.91
  (48 shorter events, 1.8 us)
Async XLA Ops:
  6.5 98.7 %copy-start = (f32[8,8192]{1,0:T(8,128)S(1)}, f32[8,8192]{1,0:T(8,128)}, u32[]{:S(2)}) copy-start(f32[8,8192]{1,0:T(8,128)} %param.14) | copy-start | bytes 786436
  9.5 50.4 %all-to-all-start = ((bf16[64,64,256]{2,1,0:T(8,128)(2,1)}), bf16[64,64,256]{2,1,0:T(8,128)(2,1)S(1)}, u32[]{:S(2)}, u32[]{:S(2)}) async-start(bf16[64,64,256]{2,1,0:T(8,128)(2,1)} %bitcast.17), calls=%async_computation | async-start | bytes 4194304 | tf_op jit(solution)/shard_map/all_to_all | solution.py:96
  19.9 50.4 %all-gather.5.cloned.1.call-start = ((), (), s32[]{:S(2)}) async-start(), calls=%async_computation.5 | async-start | bytes 2359296 | tf_op jit(solution)/shard_map/all_gather | solution.py:98
  59.9 2.0 copy-start.3
  61.7 7.5 %copy-start.9 = (f32[3,3,512]{2,1,0:T(4,128)S(1)}, f32[3,3,512]{2,1,0:T(4,128)}, u32[]{:S(2)}) copy-start(f32[3,3,512]{2,1,0:T(4,128)} %param.13) | copy-start | bytes 55300
  61.9 34.8 %all-to-all-start.1 = ((bf16[64,64,256]{2,1,0:T(8,128)(2,1)}), bf16[64,64,256]{2,1,0:T(8,128)(2,1)}, u32[]{:S(2)}, u32[]{:S(2)}) async-start(bf16[64,64,256]{2,1,0:T(8,128)(2,1)} %bitcast.25), calls=%async_computation.1 | async-start | bytes 4194304 | tf_op jit(solution)/shard_map/all_to_all | solution.py:96
  67.6 119.2 %all-gather.7.cloned.1.call-start = ((), (), s32[]{:S(2)}) async-start(), calls=%async_computation.6 | async-start | bytes 4259840 | tf_op jit(solution)/shard_map/all_gather | solution.py:92
  73.5 7.2 %copy-start.4 = (bf16[64,64,256]{2,1,0:T(8,128)(2,1)S(1)}, bf16[64,64,256]{2,1,0:T(8,128)(2,1)}, u32[]{:S(2)}) copy-start(bf16[64,64,256]{2,1,0:T(8,128)(2,1)} %copy-done.3) | copy-start | bytes 6291460
  74.4 6.3 %collective-permute-start = (bf16[2,4096]{1,0:T(2,128)(2,1)S(1)}, bf16[2,4096]{1,0:T(2,128)(2,1)S(1)}, u32[]{:S(2)}, u32[]{:S(2)}) collective-permute-start(bf16[2,4096]{1,0:T(2,128)(2,1)S(1)} %slice.117), channel_id=1, source_target_pairs={{0,8},{8,16},{16,24},{24,32},{32,40},{40,48},{48,56},{56,64},{64,7... | collective-permute-start | bytes 49160 | tf_op jit(solution)/shard_map/ppermute | solution.py:15
  99.1 6.1 %copy-start.8 = (f32[64,32,1]{0,1,2:T(8,128)S(1)}, f32[64,32,1]{0,1,2:T(8,128)}, u32[]{:S(2)}) copy-start(f32[64,32,1]{0,1,2:T(8,128)} %constant.49) | copy-start | bytes 24580
  99.1 13.9 %copy-start.7 = (f32[64,32,1]{0,1,2:T(8,128)S(1)}, f32[64,32,1]{0,1,2:T(8,128)}, u32[]{:S(2)}) copy-start(f32[64,32,1]{0,1,2:T(8,128)} %constant.48) | copy-start | bytes 24580
  99.1 14.3 %copy-start.5 = (f32[64,256]{1,0:T(8,128)S(1)}, f32[64,256]{1,0:T(8,128)}, u32[]{:S(2)}) copy-start(f32[64,256]{1,0:T(8,128)} %constant.38.clone) | copy-start | bytes 196612
  99.1 14.3 %copy-start.6 = (f32[64,256]{1,0:T(8,128)S(1)}, f32[64,256]{1,0:T(8,128)}, u32[]{:S(2)}) copy-start(f32[64,256]{1,0:T(8,128)} %constant.39.clone) | copy-start | bytes 196612
  100.1 12.5 %all-to-all-start.2 = ((bf16[32,8,256]{2,1,0:T(8,128)(2,1)}), bf16[32,8,256]{2,1,0:T(8,128)(2,1)S(1)}, u32[]{:S(2)}, u32[]{:S(2)}) async-start(bf16[32,8,256]{2,1,0:T(8,128)(2,1)} %bitcast.30), calls=%async_computation.2 | async-start | bytes 262144 | tf_op jit(solution)/shard_map/all_to_all | solution.py:117
  113.5 1.0 copy-start.1
  115.2 2.5 %copy-start.2 = (f32[256,256,1]{1,0,2:T(8,128)S(1)}, f32[256,256,1]{1,0,2:T(8,128)}, u32[]{:S(2)}) copy-start(f32[256,256,1]{1,0,2:T(8,128)} %constant.51) | copy-start | bytes 786436
  122.5 1.4 copy-start.11
  122.5 1.8 copy-start.10
  123.8 6.0 %copy-start.12 = (f32[512]{0:T(512)S(1)}, f32[512]{0:T(512)}, u32[]{:S(2)}) copy-start(f32[512]{0:T(512)} %param.15) | copy-start | bytes 6148
  125.7 11.7 %all-to-all-start.3 = ((bf16[32,8,256]{2,1,0:T(8,128)(2,1)}), bf16[32,8,256]{2,1,0:T(8,128)(2,1)S(1)}, u32[]{:S(2)}, u32[]{:S(2)}) async-start(bf16[32,8,256]{2,1,0:T(8,128)(2,1)} %copy.87), calls=%async_computation.3 | async-start | bytes 262144 | tf_op jit(solution)/shard_map/all_to_all | solution.py:119
Sparse Core Ops, SparseCore 0:
  22.5 44.8 all-gather.4
  70.3 116.4 all-gather.6

commit v6 on v5

--- a/solution.py
+++ b/solution.py
@@ -89,12 +89,10 @@
     chips = lax.axis_size("chip")
     parity = lax.axis_index("core")
     split = w_proj.reshape(w_proj.shape[0], 3, width // (2 * GROUP), 2, GROUP)
-    weights = [lax.all_gather(w_proj[:, 0], ("chip", "core"), axis=0, tiled=True)]
-    for member in range(1, 3):
-        part = jnp.moveaxis(split[:, member], 2, 0).reshape(1, 2, w_proj.shape[0], half)
-        spread = jnp.broadcast_to(part, (chips, 2) + part.shape[2:]).reshape((2 * chips,) + part.shape[2:])
-        arrived = lax.all_to_all(spread, ("chip", "core"), split_axis=0, concat_axis=0, tiled=True)
-        weights.append(arrived.reshape(2 * chips * w_proj.shape[0], half))
+    split = jnp.transpose(split, (1, 3, 0, 2, 4)).reshape(3, 1, 2, w_proj.shape[0], half)
+    spread = jnp.broadcast_to(split, (3, chips, 2) + split.shape[3:]).reshape((3, 2 * chips) + split.shape[3:])
+    arrived = lax.all_to_all(spread, ("chip", "core"), split_axis=1, concat_axis=1, tiled=True)
+    weights = arrived.reshape(3, 2 * chips * w_proj.shape[0], half)
     stacked = lax.all_gather(tokens, ("core", "mp"), axis=0, tiled=False)
     rows = 2 * rows_dev
     source = jnp.transpose(stacked.reshape(2, -1, rows_dev, tokens.shape[1]), (0, 2, 1, 3)).reshape(rows, -1)
@@ -104,8 +102,6 @@
     mixed = []
     for member in range(3):
         projected = jnp.dot(extended_tokens, weights[member], preferred_element_type=jnp.float32)
-        if member == 0:
-            projected = pick(projected, 1, parity)
         extended = projected.astype(jnp.bfloat16).astype(jnp.float32)
         total = jnp.zeros((rows, half), jnp.float32)
         for offset in range(margin + 1):

time: 206 us -> 173 us (0.84)
  waiting for transfers between devices: 121 us -> 96 us
  starting transfers between devices: 28.6 us -> 20.7 us
  matrix products: 20.4 us -> 16.2 us
  blocking collectives: 3.77 us -> 6.79 us
  local copies, waits for them, and re-layouts: 15.3 us -> 18.3 us
    all_gather x1 -> x0, waiting for transfers between devices: 49.2 us -> none  [on_device(): lax.all_gather(w_proj[:, 0], ('chip', 'core'), axis=0, tiled=True)]
    all_gather x1, waiting for transfers between devices: 0.02 us -> 48.4 us  [on_device(): stacked = lax.all_gather(tokens, ('core', 'mp'), axis=0, tiled=False)]
    all_to_all x2 -> x1, waiting for transfers between devices: 54.4 us -> 35.1 us  [on_device(): lax.all_to_all(spread, ('chip', 'core'), split_axis=1, concat_axis=1, til...]
    all_to_all x2 -> x1, starting transfers between devices: 16 us -> 10.6 us  [on_device(): lax.all_to_all(spread, ('chip', 'core'), split_axis=1, concat_axis=1, til...]
    dot_general x3, matrix products: 7.78 us -> 3.82 us  [on_device(): jnp.dot(extended_tokens, weights[member], preferred_element_type=jnp.floa...]
    slice x5 -> x1, local copies, waits for them, and re-layouts: 2.07 us -> 5.36 us  [on_device(): weights[member]]
    ppermute x1, waiting for transfers between devices: 3.02 us -> 0.01 us  [shifted(): lax.ppermute(value, axis, [(source, source + steps) for source in range(l...]
    all_to_all x1, blocking collectives: 3.77 us -> 6.79 us  [on_device(): lax.all_to_all(local, 'core', split_axis=0, concat_axis=0, tiled=True)]
  transfers between devices with their start and end apart: 7 -> 5, of which waited for: 6 -> 4; matrix products, arithmetic and copies ran while one was open for 13% -> 8% of each run, Pallas kernels for 0% -> 0%
where the time goes in v6:
time: 173 us; the launch traced here: 172 us
  waiting for transfers between devices  96 us (55%)
  starting transfers between devices  20.7 us (12%)
  local copies, waits for them, and re-layouts  18.3 us (11%)
  matrix products  16.2 us (9%)
  between operations  13.9 us (8%)
  blocking collectives  6.79 us (4%)
    all_gather x1, waiting for transfers between devices, on_device(): stacked = lax.all_gather(tokens, ('core', 'mp'), axis=0, tiled=False)  48.4 us
    all_to_all x1, waiting for transfers between devices, on_device(): lax.all_to_all(spread, ('chip', 'core'), split_axis=1, concat_axis=1, til...  35.1 us
    all_to_all x1, starting transfers between devices, on_device(): lax.all_to_all(spread, ('chip', 'core'), split_axis=1, concat_axis=1, til...  10.6 us
    all_to_all x1, blocking collectives, on_device(): lax.all_to_all(local, 'core', split_axis=0, concat_axis=0, tiled=True)  6.79 us
    dot_general x8, matrix products, forward(): dot = lambda a, m: jnp.einsum('krn,nm->krm', a, m, precision=HIGHEST)  6.63 us
    all_to_all x1, waiting for transfers between devices, on_device(): lax.all_to_all(outgoing, 'chip', split_axis=0, concat_axis=0, tiled=True)  6.56 us
    slice x1, local copies, waits for them, and re-layouts, on_device(): weights[member]  5.36 us
    all_to_all x1, waiting for transfers between devices, on_device(): lax.all_to_all(convolved, 'chip', split_axis=0, concat_axis=0, tiled=True)  5.23 us
  transfers between devices with their start and end apart: 5, of which 4 were waited for; matrix products, arithmetic and copies ran while one was open for 8% of the time, Pallas kernels for 0%

profile of v6, /device:TPU:1, one launch (start us, length us, event | category | flops | bytes accessed | tf_op | source)
XLA Modules:
  0.0 172.2 jit_solution(8256814934520290351)
XLA Ops:
  6.5 1.2 copy.55
  7.8 0.2 copy.57
  8.0 3.4 %broadcast_in_dim.5 = bf16[3,32,2,64,256]{4,3,0,2,1:T(8,128)(2,1)} broadcast(bf16[3,2,64,256]{3,2,0,1:T(8,128)(2,1)S(1)} %copy.57), dimensions={0,2,3,4} | broadcast | bytes 6488064 | tf_op jit(solution)/shard_map/broadcast_in_dim | solution.py:93
  11.4 10.6 %all-to-all-start = ((bf16[3,64,64,256]{3,2,0,1:T(8,128)(2,1)}), bf16[3,64,64,256]{3,2,0,1:T(8,128)(2,1)}, u32[]{:S(2)}, u32[]{:S(2)}) async-start(bf16[3,64,64,256]{3,2,0,1:T(8,128)(2,1)} %bitcast.72), calls=%async_computation | async-start | bytes 12582912 | tf_op jit(solution)/shard_map/all_to_all | solution.py:94
  22.1 0.7 all-gather.3.cloned.1.call-update
  22.8 0.5 reshape.62
  23.3 0.4 dynamic-slice_reduce_fusion
  23.7 0.1 reshape.63
  23.8 48.4 %all-gather.3.cloned.1.call-done = bf16[1024,1024]{1,0:T(8,128)(2,1)} async-done(((bf16[128,1024]{1,0:T(8,128)(2,1)}), bf16[1024,1024]{1,0:T(8,128)(2,1)}) %all-gather.3.cloned.1.call-update) | async-done | bytes 2097168 | tf_op jit(solution)/shard_map/all_gather | solution.py:96
  72.2 3.2 %copy.54 = bf16[2,4,128,1024]{3,1,2,0:T(4,128)(2,1)S(1)} copy(bf16[2,4,128,1024]{3,2,1,0:T(8,128)(2,1)} %bitcast.78) | data formatting | bytes 4194304 | tf_op jit(solution)/shard_map/reshape | solution.py:98
  75.4 0.9 copy.86
  76.3 2.1 %collective-permute-start = (bf16[2,4096]{1,0:T(2,128)(2,1)S(1)}, bf16[2,4096]{1,0:T(2,128)(2,1)S(1)}, u32[]{:S(2)}, u32[]{:S(2)}) collective-permute-start(bf16[2,4096]{1,0:T(2,128)(2,1)S(1)} %slice.108), channel_id=1, source_target_pairs={{0,8},{8,16},{16,24},{24,32},{32,40},{40,48},{48,56},{56,64},{64,7... | collective-permute-start | bytes 49160 | tf_op jit(solution)/shard_map/ppermute | solution.py:15
  78.5 35.1 %all-to-all-done = bf16[3,64,64,256]{3,2,0,1:T(8,128)(2,1)} async-done(((bf16[3,64,64,256]{3,2,0,1:T(8,128)(2,1)}), bf16[3,64,64,256]{3,2,0,1:T(8,128)(2,1)}, u32[]{:S(2)}, u32[]{:S(2)}) %all-to-all-start) | async-done | bytes 6291488 | tf_op jit(solution)/shard_map/all_to_all | solution.py:94
  113.6 5.4 %fusion.53 = (bf16[1,64,64,256]{3,2,0,1:T(8,128)(2,1)S(1)}, bf16[1,64,64,256]{3,2,0,1:T(8,128)(2,1)S(1)}, bf16[1,64,64,256]{3,2,0,1:T(8,128)(2,1)}) fusion(bf16[3,64,64,256]{3,2,0,1:T(8,128)(2,1)} %all-to-all-done), kind=kLoop, calls=%fused_computation.86 | loop fusion | bytes 12582912 | tf_op jit(solution)/shard_map/slice | solution.py:104
  119.0 0.7 fusion.1
  119.7 0.7 fusion.2
  120.5 0.2 fusion.32
  120.7 0.8 copy.58
  121.5 4.0 %all-to-all-start.1 = ((bf16[32,8,256]{2,1,0:T(8,128)(2,1)}), bf16[32,8,256]{2,1,0:T(8,128)(2,1)S(1)}, u32[]{:S(2)}, u32[]{:S(2)}) async-start(bf16[32,8,256]{2,1,0:T(8,128)(2,1)} %bitcast.21), calls=%async_computation.1 | async-start | bytes 262144 | tf_op jit(solution)/shard_map/all_to_all | solution.py:113
  125.8 0.6 convolution_negate_fusion
  126.4 6.6 %all-to-all-done.1 = bf16[32,8,256]{2,1,0:T(8,128)(2,1)S(1)} async-done(((bf16[32,8,256]{2,1,0:T(8,128)(2,1)}), bf16[32,8,256]{2,1,0:T(8,128)(2,1)S(1)}, u32[]{:S(2)}, u32[]{:S(2)}) %all-to-all-start.1) | async-done | bytes 131104 | tf_op jit(solution)/shard_map/all_to_all | solution.py:113
  133.0 0.4 fusion
  133.4 0.4 fusion.48
  133.9 0.8 multiply_subtract_fusion.1
  134.7 0.1 copy-done.1
  134.8 0.8 fusion.18
  135.7 0.8 fusion.28
  136.5 0.8 fusion.22
  137.3 0.8 fusion.24
  138.2 0.8 convolution_subtract_fusion.1
  139.0 0.8 convolution_add_fusion.2
  139.8 0.8 convolution_add_fusion.1
  140.7 0.9 multiply_subtract_fusion
  141.5 0.7 fusion.12
  142.2 0.7 fusion.16
  142.9 0.7 convolution_add_fusion
  143.6 0.7 convolution_subtract_fusion
  144.3 0.4 fusion.8
  144.7 0.4 fusion.4
  145.2 0.7 copy.75
  145.9 3.9 %all-to-all-start.2 = ((bf16[32,8,256]{2,1,0:T(8,128)(2,1)}), bf16[32,8,256]{2,1,0:T(8,128)(2,1)S(1)}, u32[]{:S(2)}, u32[]{:S(2)}) async-start(bf16[32,8,256]{2,1,0:T(8,128)(2,1)} %copy.75), calls=%async_computation.2 | async-start | bytes 262144 | tf_op jit(solution)/shard_map/all_to_all | solution.py:115
  149.8 2.3 %fusion.3 = f32[258,256]{1,0:T(8,128)S(1)} fusion(bf16[4096,256]{1,0:T(8,128)(2,1)} %bitcast.79, bf16[256,4096]{1,0:T(8,128)(2,1)S(1)} %bitcast.77, bf16[2,4096]{1,0:T(2,128)(2,1)S(1)} %collective-permute-done), kind=kOutput, calls=%fused_computation.16 | convolution fusion | flops 545424384 | bytes 4474880 | tf_op jit(solution)/shard_map/dot_general | solution.py:104
  152.1 5.2 %all-to-all-done.2 = bf16[32,8,256]{2,1,0:T(8,128)(2,1)S(1)} async-done(((bf16[32,8,256]{2,1,0:T(8,128)(2,1)}), bf16[32,8,256]{2,1,0:T(8,128)(2,1)S(1)}, u32[]{:S(2)}, u32[]{:S(2)}) %all-to-all-start.2) | async-done | bytes 131104 | tf_op jit(solution)/shard_map/all_to_all | solution.py:115
  157.4 0.1 copy.76
  157.5 0.1 fusion.38
  157.6 0.1 copy.77
  157.8 6.8 %all_to_all.20 = bf16[2,128,256]{1,2,0:T(8,128)(2,1)S(1)} all-to-all(bf16[2,128,256]{1,2,0:T(8,128)(2,1)S(1)} %copy.77), channel_id=1, replica_groups=mesh['chip'=32,'core'=2,'mp'=4] {'core'}, dimensions={0} | all-to-all | bytes 262144 | tf_op jit(solution)/shard_map/all_to_all | solution.py:120
  164.6 0.8 copy.79
  (31 shorter events, 0.5 us)
Async XLA Ops:
  6.5 119.3 %copy-start = (f32[8,8192]{1,0:T(8,128)S(1)}, f32[8,8192]{1,0:T(8,128)}, u32[]{:S(2)}) copy-start(f32[8,8192]{1,0:T(8,128)} %param.14) | copy-start | bytes 786436
  11.4 11.4 %copy-start.7 = (f32[3,3,512]{2,1,0:T(4,128)S(1)}, f32[3,3,512]{2,1,0:T(4,128)}, u32[]{:S(2)}) copy-start(f32[3,3,512]{2,1,0:T(4,128)} %param.13) | copy-start | bytes 55300
  11.4 102.2 %all-to-all-start = ((bf16[3,64,64,256]{3,2,0,1:T(8,128)(2,1)}), bf16[3,64,64,256]{3,2,0,1:T(8,128)(2,1)}, u32[]{:S(2)}, u32[]{:S(2)}) async-start(bf16[3,64,64,256]{3,2,0,1:T(8,128)(2,1)} %bitcast.72), calls=%async_computation | async-start | bytes 12582912 | tf_op jit(solution)/shard_map/all_to_all | solution.py:94
  22.0 50.2 %all-gather.3.cloned.1.call-start = ((), (), s32[]{:S(2)}) async-start(), calls=%async_computation.4 | async-start | bytes 2359296 | tf_op jit(solution)/shard_map/all_gather | solution.py:96
  76.3 42.6 %collective-permute-start = (bf16[2,4096]{1,0:T(2,128)(2,1)S(1)}, bf16[2,4096]{1,0:T(2,128)(2,1)S(1)}, u32[]{:S(2)}, u32[]{:S(2)}) collective-permute-start(bf16[2,4096]{1,0:T(2,128)(2,1)S(1)} %slice.108), channel_id=1, source_target_pairs={{0,8},{8,16},{16,24},{24,32},{32,40},{40,48},{48,56},{56,64},{64,7... | collective-permute-start | bytes 49160 | tf_op jit(solution)/shard_map/ppermute | solution.py:15
  120.5 5.1 %copy-start.10 = (f32[512]{0:T(512)S(1)}, f32[512]{0:T(512)}, u32[]{:S(2)}) copy-start(f32[512]{0:T(512)} %param.15) | copy-start | bytes 6148
  120.5 5.3 %copy-start.6 = (f32[64,32,1]{0,1,2:T(8,128)S(1)}, f32[64,32,1]{0,1,2:T(8,128)}, u32[]{:S(2)}) copy-start(f32[64,32,1]{0,1,2:T(8,128)} %constant.45) | copy-start | bytes 24580
  120.5 12.9 %copy-start.5 = (f32[64,32,1]{0,1,2:T(8,128)S(1)}, f32[64,32,1]{0,1,2:T(8,128)}, u32[]{:S(2)}) copy-start(f32[64,32,1]{0,1,2:T(8,128)} %constant.44) | copy-start | bytes 24580
  120.5 13.4 %copy-start.3 = (f32[64,256]{1,0:T(8,128)S(1)}, f32[64,256]{1,0:T(8,128)}, u32[]{:S(2)}) copy-start(f32[64,256]{1,0:T(8,128)} %constant.35.clone) | copy-start | bytes 196612
  120.5 13.4 %copy-start.4 = (f32[64,256]{1,0:T(8,128)S(1)}, f32[64,256]{1,0:T(8,128)}, u32[]{:S(2)}) copy-start(f32[64,256]{1,0:T(8,128)} %constant.34.clone) | copy-start | bytes 196612
  121.5 11.5 %all-to-all-start.1 = ((bf16[32,8,256]{2,1,0:T(8,128)(2,1)}), bf16[32,8,256]{2,1,0:T(8,128)(2,1)S(1)}, u32[]{:S(2)}, u32[]{:S(2)}) async-start(bf16[32,8,256]{2,1,0:T(8,128)(2,1)} %bitcast.21), calls=%async_computation.1 | async-start | bytes 262144 | tf_op jit(solution)/shard_map/all_to_all | solution.py:113
  133.9 1.0 copy-start.1
  135.7 2.5 %copy-start.2 = (f32[256,256,1]{1,0,2:T(8,128)S(1)}, f32[256,256,1]{1,0,2:T(8,128)}, u32[]{:S(2)}) copy-start(f32[256,256,1]{1,0,2:T(8,128)} %constant.47) | copy-start | bytes 786436
  142.9 1.4 copy-start.9
  142.9 1.8 %copy-start.8 = (f32[32,64,1]{1,0,2:T(8,128)S(1)}, f32[32,64,1]{1,0,2:T(8,128)}, u32[]{:S(2)}) copy-start(f32[32,64,1]{1,0,2:T(8,128)} %constant.48) | copy-start | bytes 24580
  145.9 11.4 %all-to-all-start.2 = ((bf16[32,8,256]{2,1,0:T(8,128)(2,1)}), bf16[32,8,256]{2,1,0:T(8,128)(2,1)S(1)}, u32[]{:S(2)}, u32[]{:S(2)}) async-start(bf16[32,8,256]{2,1,0:T(8,128)(2,1)} %copy.75), calls=%async_computation.2 | async-start | bytes 262144 | tf_op jit(solution)/shard_map/all_to_all | solution.py:115
Sparse Core Ops, SparseCore 0:
  24.7 47.4 all-gather.2

commit v7 on v6

--- a/solution.py
+++ b/solution.py
@@ -89,10 +89,10 @@
     chips = lax.axis_size("chip")
     parity = lax.axis_index("core")
     split = w_proj.reshape(w_proj.shape[0], 3, width // (2 * GROUP), 2, GROUP)
-    split = jnp.transpose(split, (1, 3, 0, 2, 4)).reshape(3, 1, 2, w_proj.shape[0], half)
-    spread = jnp.broadcast_to(split, (3, chips, 2) + split.shape[3:]).reshape((3, 2 * chips) + split.shape[3:])
-    arrived = lax.all_to_all(spread, ("chip", "core"), split_axis=1, concat_axis=1, tiled=True)
-    weights = arrived.reshape(3, 2 * chips * w_proj.shape[0], half)
+    split = jnp.transpose(split, (3, 0, 1, 2, 4)).reshape(1, 2, w_proj.shape[0], 3 * half)
+    spread = jnp.broadcast_to(split, (chips,) + split.shape[1:]).reshape((2 * chips,) + split.shape[2:])
+    arrived = lax.all_to_all(spread, ("chip", "core"), split_axis=0, concat_axis=0, tiled=True)
+    weights = arrived.reshape(2 * chips * w_proj.shape[0], 3 * half)
     stacked = lax.all_gather(tokens, ("core", "mp"), axis=0, tiled=False)
     rows = 2 * rows_dev
     source = jnp.transpose(stacked.reshape(2, -1, rows_dev, tokens.shape[1]), (0, 2, 1, 3)).reshape(rows, -1)
@@ -100,8 +100,9 @@
     extended_tokens = jnp.concatenate([tail, source], axis=0)
     taps = pick(short_filter, 2, parity)
     mixed = []
+    projected_all = jnp.dot(extended_tokens, weights, preferred_element_type=jnp.float32)
     for member in range(3):
-        projected = jnp.dot(extended_tokens, weights[member], preferred_element_type=jnp.float32)
+        projected = projected_all[:, member * half : (member + 1) * half]
         extended = projected.astype(jnp.bfloat16).astype(jnp.float32)
         total = jnp.zeros((rows, half), jnp.float32)
         for offset in range(margin + 1):

time: 173 us -> 171 us (0.988)
  local copies, waits for them, and re-layouts: 18.3 us -> 12.9 us
  waiting for transfers between devices: 96 us -> 98.3 us
    slice x1 -> x0, local copies, waits for them, and re-layouts: 5.36 us -> none  [on_device(): weights[member]]
    all_to_all x1, waiting for transfers between devices: 5.23 us -> 7.29 us  [on_device(): lax.all_to_all(convolved, 'chip', split_axis=0, concat_axis=0, tiled=True)]
    dot_general x3 -> x1, matrix products: 3.82 us -> 4.65 us  [on_device(): jnp.dot(extended_tokens, weights, preferred_element_type=jnp.float32)]
  transfers between devices with their start and end apart: 5 -> 5, of which waited for: 4 -> 5; matrix products, arithmetic and copies ran while one was open for 8% -> 4% of each run, Pallas kernels for 0% -> 0%
where the time goes in v7:
time: 171 us; the launch traced here: 170 us
  waiting for transfers between devices  98.3 us (57%)
  starting transfers between devices  20.7 us (12%)
  matrix products  17.1 us (10%)
  between operations  13.9 us (8%)
  local copies, waits for them, and re-layouts  12.9 us (8%)
  blocking collectives  6.77 us (4%)
    all_gather x1, waiting for transfers between devices, on_device(): stacked = lax.all_gather(tokens, ('core', 'mp'), axis=0, tiled=False)  48.4 us
    all_to_all x1, waiting for transfers between devices, on_device(): lax.all_to_all(spread, ('chip', 'core'), split_axis=0, concat_axis=0, til...  34.3 us
    all_to_all x1, starting transfers between devices, on_device(): lax.all_to_all(spread, ('chip', 'core'), split_axis=0, concat_axis=0, til...  10.6 us
    all_to_all x1, waiting for transfers between devices, on_device(): lax.all_to_all(convolved, 'chip', split_axis=0, concat_axis=0, tiled=True)  7.29 us
    all_to_all x1, waiting for transfers between devices, on_device(): lax.all_to_all(outgoing, 'chip', split_axis=0, concat_axis=0, tiled=True)  6.84 us
    all_to_all x1, blocking collectives, on_device(): lax.all_to_all(local, 'core', split_axis=0, concat_axis=0, tiled=True)  6.77 us
    dot_general x8, matrix products, forward(): dot = lambda a, m: jnp.einsum('krn,nm->krm', a, m, precision=HIGHEST)  6.63 us
    dot_general x1, matrix products, on_device(): jnp.dot(extended_tokens, weights, preferred_element_type=jnp.float32)  4.65 us
  transfers between devices with their start and end apart: 5, of which 5 were waited for; matrix products, arithmetic and copies ran while one was open for 4% of the time, Pallas kernels for 0%

profile of v7, /device:TPU:1, one launch (start us, length us, event | category | flops | bytes accessed | tf_op | source)
XLA Modules:
  0.0 170.0 jit_solution(13152430299536980189)
XLA Ops:
  6.5 1.2 copy.55
  7.8 0.2 copy.57
  8.0 3.4 %broadcast_in_dim.5 = bf16[32,2,64,768]{3,2,1,0:T(8,128)(2,1)} broadcast(bf16[2,64,768]{2,1,0:T(8,128)(2,1)S(1)} %copy.57), dimensions={1,2,3} | broadcast | bytes 6488064 | tf_op jit(solution)/shard_map/broadcast_in_dim | solution.py:93
  11.4 10.6 %all-to-all-start = ((bf16[64,64,768]{2,1,0:T(8,128)(2,1)}), bf16[64,64,768]{2,1,0:T(8,128)(2,1)}, u32[]{:S(2)}, u32[]{:S(2)}) async-start(bf16[64,64,768]{2,1,0:T(8,128)(2,1)} %bitcast.66), calls=%async_computation | async-start | bytes 12582912 | tf_op jit(solution)/shard_map/all_to_all | solution.py:94
  22.1 0.7 all-gather.3.cloned.1.call-update
  22.8 0.5 reshape.58
  23.2 0.4 dynamic-slice_reduce_fusion
  23.7 0.1 reshape.59
  23.8 48.4 %all-gather.3.cloned.1.call-done = bf16[1024,1024]{1,0:T(8,128)(2,1)} async-done(((bf16[128,1024]{1,0:T(8,128)(2,1)}), bf16[1024,1024]{1,0:T(8,128)(2,1)}) %all-gather.3.cloned.1.call-update) | async-done | bytes 2097168 | tf_op jit(solution)/shard_map/all_gather | solution.py:96
  72.2 3.2 %copy.54 = bf16[2,4,128,1024]{3,1,2,0:T(4,128)(2,1)S(1)} copy(bf16[2,4,128,1024]{3,2,1,0:T(8,128)(2,1)} %bitcast.70) | data formatting | bytes 4194304 | tf_op jit(solution)/shard_map/reshape | solution.py:98
  75.4 0.9 copy.86
  76.3 2.1 %collective-permute-start = (bf16[2,4096]{1,0:T(2,128)(2,1)S(1)}, bf16[2,4096]{1,0:T(2,128)(2,1)S(1)}, u32[]{:S(2)}, u32[]{:S(2)}) collective-permute-start(bf16[2,4096]{1,0:T(2,128)(2,1)S(1)} %slice.108), channel_id=1, source_target_pairs={{0,8},{8,16},{16,24},{24,32},{32,40},{40,48},{48,56},{56,64},{64,7... | collective-permute-start | bytes 49160 | tf_op jit(solution)/shard_map/ppermute | solution.py:15
  78.4 0.8 collective-permute-done
  79.3 34.3 %all-to-all-done = bf16[64,64,768]{2,1,0:T(8,128)(2,1)} async-done(((bf16[64,64,768]{2,1,0:T(8,128)(2,1)}), bf16[64,64,768]{2,1,0:T(8,128)(2,1)}, u32[]{:S(2)}, u32[]{:S(2)}) %all-to-all-start) | async-done | bytes 6291488 | tf_op jit(solution)/shard_map/all_to_all | solution.py:94
  113.6 4.6 %fusion.4 = bf16[258,768]{1,0:T(8,128)(2,1)S(1)} fusion(bf16[4096,768]{1,0:T(8,128)(2,1)} %bitcast.7, bf16[256,4096]{1,0:T(8,128)(2,1)S(1)} %bitcast.69, bf16[2,4096]{1,0:T(2,128)(2,1)S(1)} %collective-permute-done), kind=kOutput, calls=%fused_computation.4 | convolution fusion | flops 1627620864 | bytes 8801280 | tf_op jit(solution)/shard_map/dot_general | solution.py:103
  118.3 0.2 fusion.36
  118.5 0.8 copy.58
  119.3 4.0 %all-to-all-start.1 = ((bf16[32,8,256]{2,1,0:T(8,128)(2,1)}), bf16[32,8,256]{2,1,0:T(8,128)(2,1)S(1)}, u32[]{:S(2)}, u32[]{:S(2)}) async-start(bf16[32,8,256]{2,1,0:T(8,128)(2,1)} %bitcast.19), calls=%async_computation.1 | async-start | bytes 262144 | tf_op jit(solution)/shard_map/all_to_all | solution.py:114
  123.3 0.6 convolution_negate_fusion
  124.0 6.8 %all-to-all-done.1 = bf16[32,8,256]{2,1,0:T(8,128)(2,1)S(1)} async-done(((bf16[32,8,256]{2,1,0:T(8,128)(2,1)}), bf16[32,8,256]{2,1,0:T(8,128)(2,1)S(1)}, u32[]{:S(2)}, u32[]{:S(2)}) %all-to-all-start.1) | async-done | bytes 131104 | tf_op jit(solution)/shard_map/all_to_all | solution.py:114
  130.8 0.4 fusion.7
  131.3 0.4 fusion.52
  131.7 0.8 multiply_subtract_fusion.1
  132.5 0.1 copy-done.1
  132.7 0.8 fusion.22
  133.5 0.8 fusion.32
  134.3 0.8 fusion.26
  135.2 0.8 fusion.28
  136.0 0.8 convolution_subtract_fusion.1
  136.8 0.8 convolution_add_fusion.2
  137.7 0.8 convolution_add_fusion.1
  138.5 0.9 multiply_subtract_fusion
  139.4 0.7 fusion.16
  140.0 0.7 fusion.20
  140.7 0.7 convolution_add_fusion
  141.4 0.7 convolution_subtract_fusion
  142.1 0.4 fusion.12
  142.6 0.4 fusion.8
  143.0 0.7 copy.75
  143.7 3.9 %all-to-all-start.2 = ((bf16[32,8,256]{2,1,0:T(8,128)(2,1)}), bf16[32,8,256]{2,1,0:T(8,128)(2,1)S(1)}, u32[]{:S(2)}, u32[]{:S(2)}) async-start(bf16[32,8,256]{2,1,0:T(8,128)(2,1)} %copy.75), calls=%async_computation.2 | async-start | bytes 262144 | tf_op jit(solution)/shard_map/all_to_all | solution.py:116
  147.6 0.1 reshape.67
  147.8 0.1 mul.248
  147.9 7.3 %all-to-all-done.2 = bf16[32,8,256]{2,1,0:T(8,128)(2,1)S(1)} async-done(((bf16[32,8,256]{2,1,0:T(8,128)(2,1)}), bf16[32,8,256]{2,1,0:T(8,128)(2,1)S(1)}, u32[]{:S(2)}, u32[]{:S(2)}) %all-to-all-start.2) | async-done | bytes 131104 | tf_op jit(solution)/shard_map/all_to_all | solution.py:116
  155.2 0.1 copy.76
  155.3 0.1 fusion.42
  155.5 0.1 copy.77
  155.6 6.8 %all_to_all.20 = bf16[2,128,256]{1,2,0:T(8,128)(2,1)S(1)} all-to-all(bf16[2,128,256]{1,2,0:T(8,128)(2,1)S(1)} %copy.77), channel_id=1, replica_groups=mesh['chip'=32,'core'=2,'mp'=4] {'core'}, dimensions={0} | all-to-all | bytes 262144 | tf_op jit(solution)/shard_map/all_to_all | solution.py:121
  162.4 0.8 copy.79
  (29 shorter events, 0.4 us)
Async XLA Ops:
  6.5 116.8 %copy-start = (f32[8,8192]{1,0:T(8,128)S(1)}, f32[8,8192]{1,0:T(8,128)}, u32[]{:S(2)}) copy-start(f32[8,8192]{1,0:T(8,128)} %param.14) | copy-start | bytes 786436
  11.4 11.4 %copy-start.7 = (f32[3,3,512]{2,1,0:T(4,128)S(1)}, f32[3,3,512]{2,1,0:T(4,128)}, u32[]{:S(2)}) copy-start(f32[3,3,512]{2,1,0:T(4,128)} %param.13) | copy-start | bytes 55300
  11.4 102.2 %all-to-all-start = ((bf16[64,64,768]{2,1,0:T(8,128)(2,1)}), bf16[64,64,768]{2,1,0:T(8,128)(2,1)}, u32[]{:S(2)}, u32[]{:S(2)}) async-start(bf16[64,64,768]{2,1,0:T(8,128)(2,1)} %bitcast.66), calls=%async_computation | async-start | bytes 12582912 | tf_op jit(solution)/shard_map/all_to_all | solution.py:94
  22.0 50.2 %all-gather.3.cloned.1.call-start = ((), (), s32[]{:S(2)}) async-start(), calls=%async_computation.4 | async-start | bytes 2359296 | tf_op jit(solution)/shard_map/all_gather | solution.py:96
  76.3 3.0 %collective-permute-start = (bf16[2,4096]{1,0:T(2,128)(2,1)S(1)}, bf16[2,4096]{1,0:T(2,128)(2,1)S(1)}, u32[]{:S(2)}, u32[]{:S(2)}) collective-permute-start(bf16[2,4096]{1,0:T(2,128)(2,1)S(1)} %slice.108), channel_id=1, source_target_pairs={{0,8},{8,16},{16,24},{24,32},{32,40},{40,48},{48,56},{56,64},{64,7... | collective-permute-start | bytes 49160 | tf_op jit(solution)/shard_map/ppermute | solution.py:15
  118.2 5.1 %copy-start.6 = (f32[64,32,1]{0,1,2:T(8,128)S(1)}, f32[64,32,1]{0,1,2:T(8,128)}, u32[]{:S(2)}) copy-start(f32[64,32,1]{0,1,2:T(8,128)} %constant.45) | copy-start | bytes 24580
  118.3 12.9 %copy-start.5 = (f32[64,32,1]{0,1,2:T(8,128)S(1)}, f32[64,32,1]{0,1,2:T(8,128)}, u32[]{:S(2)}) copy-start(f32[64,32,1]{0,1,2:T(8,128)} %constant.44) | copy-start | bytes 24580
  118.3 13.4 %copy-start.3 = (f32[64,256]{1,0:T(8,128)S(1)}, f32[64,256]{1,0:T(8,128)}, u32[]{:S(2)}) copy-start(f32[64,256]{1,0:T(8,128)} %constant.35.clone) | copy-start | bytes 196612
  118.3 13.4 %copy-start.4 = (f32[64,256]{1,0:T(8,128)S(1)}, f32[64,256]{1,0:T(8,128)}, u32[]{:S(2)}) copy-start(f32[64,256]{1,0:T(8,128)} %constant.34.clone) | copy-start | bytes 196612
  119.3 11.5 %all-to-all-start.1 = ((bf16[32,8,256]{2,1,0:T(8,128)(2,1)}), bf16[32,8,256]{2,1,0:T(8,128)(2,1)S(1)}, u32[]{:S(2)}, u32[]{:S(2)}) async-start(bf16[32,8,256]{2,1,0:T(8,128)(2,1)} %bitcast.19), calls=%async_computation.1 | async-start | bytes 262144 | tf_op jit(solution)/shard_map/all_to_all | solution.py:114
  131.7 1.0 copy-start.1
  133.5 2.5 %copy-start.2 = (f32[256,256,1]{1,0,2:T(8,128)S(1)}, f32[256,256,1]{1,0,2:T(8,128)}, u32[]{:S(2)}) copy-start(f32[256,256,1]{1,0,2:T(8,128)} %constant.47) | copy-start | bytes 786436
  140.7 1.4 copy-start.9
  140.7 1.8 %copy-start.8 = (f32[32,64,1]{1,0,2:T(8,128)S(1)}, f32[32,64,1]{1,0,2:T(8,128)}, u32[]{:S(2)}) copy-start(f32[32,64,1]{1,0,2:T(8,128)} %constant.48) | copy-start | bytes 24580
  142.1 5.5 %copy-start.10 = (f32[512]{0:T(512)S(1)}, f32[512]{0:T(512)}, u32[]{:S(2)}) copy-start(f32[512]{0:T(512)} %param.15) | copy-start | bytes 6148
  143.7 11.4 %all-to-all-start.2 = ((bf16[32,8,256]{2,1,0:T(8,128)(2,1)}), bf16[32,8,256]{2,1,0:T(8,128)(2,1)S(1)}, u32[]{:S(2)}, u32[]{:S(2)}) async-start(bf16[32,8,256]{2,1,0:T(8,128)(2,1)} %copy.75), calls=%async_computation.2 | async-start | bytes 262144 | tf_op jit(solution)/shard_map/all_to_all | solution.py:116
Sparse Core Ops, SparseCore 0:
  24.7 47.4 all-gather.2

commit v8 on v7

--- a/solution.py
+++ b/solution.py
@@ -81,26 +81,42 @@
     return taken.reshape(shape[:axis] + (shape[axis] // 2,) + shape[axis + 1 :])
 
 
+CHIP = ("xh", "xl", "zl", "y")
+HALF = ("xl", "zl", "y", "core")
+
+
+def swap(value, axis):
+    return lax.ppermute(value, axis, [(0, 1), (1, 0)])
+
+
 def on_device(tokens, w_proj, short_filter, long_filter, skip_gain):
     rows_dev = tokens.shape[0]
     margin = short_filter.shape[1] - 1
     width = w_proj.shape[2]
     half = width // 2
-    chips = lax.axis_size("chip")
+    chips = lax.axis_size(CHIP)
+    senders = lax.axis_size(HALF)
     parity = lax.axis_index("core")
+    side = lax.axis_index("xh")
     split = w_proj.reshape(w_proj.shape[0], 3, width // (2 * GROUP), 2, GROUP)
     split = jnp.transpose(split, (3, 0, 1, 2, 4)).reshape(1, 2, w_proj.shape[0], 3 * half)
-    spread = jnp.broadcast_to(split, (chips,) + split.shape[1:]).reshape((2 * chips,) + split.shape[2:])
-    arrived = lax.all_to_all(spread, ("chip", "core"), split_axis=0, concat_axis=0, tiled=True)
-    weights = arrived.reshape(2 * chips * w_proj.shape[0], 3 * half)
+    spread = jnp.broadcast_to(split, (senders // 2,) + split.shape[1:]).reshape((senders,) + split.shape[2:])
+    arrived = lax.all_to_all(spread, HALF, split_axis=0, concat_axis=0, tiled=True)
+    weights = arrived.reshape(senders * w_proj.shape[0], 3 * half)
+    depth = weights.shape[0]
     stacked = lax.all_gather(tokens, ("core", "mp"), axis=0, tiled=False)
     rows = 2 * rows_dev
     source = jnp.transpose(stacked.reshape(2, -1, rows_dev, tokens.shape[1]), (0, 2, 1, 3)).reshape(rows, -1)
-    tail = shifted(source[rows - margin :], "chip", 1)
+    tail = shifted(source[rows - margin :], CHIP, 1)
     extended_tokens = jnp.concatenate([tail, source], axis=0)
+    mine = lax.dynamic_slice_in_dim(extended_tokens, side * depth, depth, axis=1)
+    other = lax.dynamic_slice_in_dim(extended_tokens, (1 - side) * depth, depth, axis=1)
+    theirs = swap(other, "xh")
+    own_part = jnp.dot(mine, weights, preferred_element_type=jnp.float32)
+    their_part = jnp.dot(theirs, weights, preferred_element_type=jnp.float32)
+    projected_all = own_part + swap(their_part, "xh")
     taps = pick(short_filter, 2, parity)
     mixed = []
-    projected_all = jnp.dot(extended_tokens, weights, preferred_element_type=jnp.float32)
     for member in range(3):
         projected = projected_all[:, member * half : (member + 1) * half]
         extended = projected.astype(jnp.bfloat16).astype(jnp.float32)
@@ -111,9 +127,9 @@
     query_rows = mixed[0]
     product = (mixed[1] * mixed[2]).astype(jnp.bfloat16)
     outgoing = product.T.reshape(chips, GROUP, rows)
-    arrived = lax.all_to_all(outgoing, "chip", split_axis=0, concat_axis=0, tiled=True)
+    arrived = lax.all_to_all(outgoing, CHIP, split_axis=0, concat_axis=0, tiled=True)
     convolved = long_conv(arrived, long_filter).astype(jnp.bfloat16)
-    returned = lax.all_to_all(convolved, "chip", split_axis=0, concat_axis=0, tiled=True)
+    returned = lax.all_to_all(convolved, CHIP, split_axis=0, concat_axis=0, tiled=True)
     back_rows = returned.reshape(half, rows).T
     gain = pick(skip_gain, 0, parity)
     local = query_rows * (back_rows.astype(jnp.float32) + gain[None, :] * product.astype(jnp.float32))
@@ -124,10 +140,10 @@
 
 
 def solution(mesh):
-    seq_size = mesh.shape["seq"]
-    devices = mesh.devices.reshape(seq_size // 2, 2, mesh.shape["mp"])
-    inner = jax.sharding.Mesh(devices, ("chip", "core", "mp"))
-    seq = ("chip", "core")
+    physical = (2, 2, 2, 4, 2)
+    devices = mesh.devices.reshape(physical + (mesh.shape["mp"],))
+    inner = jax.sharding.Mesh(devices, CHIP + ("core", "mp"))
+    seq = CHIP + ("core",)
     return jax.shard_map(
         on_device,
         mesh=inner,

time: 171 us -> 187 us (1.094)
  starting transfers between devices: 20.7 us -> 28.7 us
  waiting for transfers between devices: 98.3 us -> 102 us
  matrix products: 17.1 us -> 19.9 us
  blocking collectives: 6.77 us -> 9.2 us
    ppermute x0 -> x2, waiting for transfers between devices: none -> 38.6 us  [swap(): return lax.ppermute(value, axis, [(0, 1), (1, 0)])]
    all_to_all x3, waiting for transfers between devices: 48.4 us -> 14 us  [the longest x1 7.29 us: on_device(): lax.all_to_all(convolved, CHIP, split_axis=0, concat_axis=0, tiled=True)]
    ppermute x0 -> x2, starting transfers between devices: none -> 8.98 us  [swap(): return lax.ppermute(value, axis, [(0, 1), (1, 0)])]
    dot_general x1 -> x2, matrix products: 4.65 us -> 7.49 us  [the longest x1 4.15 us: on_device(): their_part = jnp.dot(theirs, weights, preferred_element_type=jnp.float32)]
    all_to_all x1, blocking collectives: 6.77 us -> 9.2 us  [on_device(): lax.all_to_all(local, 'core', split_axis=0, concat_axis=0, tiled=True)]
    all_to_all x3, starting transfers between devices: 18.5 us -> 16.5 us  [the longest x1 8.44 us: on_device(): lax.all_to_all(spread, HALF, split_axis=0, concat_axis=0, tiled=True)]
  transfers between devices with their start and end apart: 5 -> 7, of which waited for: 5 -> 6; matrix products, arithmetic and copies ran while one was open for 4% -> 4% of each run, Pallas kernels for 0% -> 0%
where the time goes in v8:
time: 187 us
  waiting for transfers between devices  102 us (55%)
  starting transfers between devices  28.7 us (15%)
  matrix products  19.9 us (11%)
  between operations  13.9 us (7%)
  local copies, waits for them, and re-layouts  11.6 us (6%)
  blocking collectives  9.2 us (5%)
    all_gather x1, waiting for transfers between devices, on_device(): stacked = lax.all_gather(tokens, ('core', 'mp'), axis=0, tiled=False)  48.1 us
    ppermute x2, waiting for transfers between devices, swap(): return lax.ppermute(value, axis, [(0, 1), (1, 0)])  38.6 us
    all_to_all x1, blocking collectives, on_device(): lax.all_to_all(local, 'core', split_axis=0, concat_axis=0, tiled=True)  9.2 us
    ppermute x2, starting transfers between devices, swap(): return lax.ppermute(value, axis, [(0, 1), (1, 0)])  8.98 us
    all_to_all x1, starting transfers between devices, on_device(): lax.all_to_all(spread, HALF, split_axis=0, concat_axis=0, tiled=True)  8.44 us
    all_to_all x1, waiting for transfers between devices, on_device(): lax.all_to_all(convolved, CHIP, split_axis=0, concat_axis=0, tiled=True)  7.29 us
    all_to_all x1, waiting for transfers between devices, on_device(): lax.all_to_all(outgoing, CHIP, split_axis=0, concat_axis=0, tiled=True)  6.74 us
    dot_general x8, matrix products, forward(): dot = lambda a, m: jnp.einsum('krn,nm->krm', a, m, precision=HIGHEST)  6.64 us
  transfers between devices with their start and end apart: 7, of which 6 were waited for; matrix products, arithmetic and copies ran while one was open for 4% of the time, Pallas kernels for 0%

profile of v8, /device:TPU:1, one launch (start us, length us, event | category | flops | bytes accessed | tf_op | source)
XLA Modules:
  0.0 186.6 jit_solution(5133537289041169515)
XLA Ops:
  6.5 1.2 copy.55
  7.8 0.2 copy.57
  8.0 2.0 %broadcast_in_dim.5 = bf16[16,2,64,768]{3,2,1,0:T(8,128)(2,1)} broadcast(bf16[2,64,768]{2,1,0:T(8,128)(2,1)S(1)} %copy.57), dimensions={1,2,3} | broadcast | bytes 3342336 | tf_op jit(solution)/shard_map/broadcast_in_dim | solution.py:103
  10.0 8.4 %all-to-all-start = ((bf16[32,64,768]{2,1,0:T(8,128)(2,1)}), bf16[32,64,768]{2,1,0:T(8,128)(2,1)}, u32[]{:S(2)}, u32[]{:S(2)}) async-start(bf16[32,64,768]{2,1,0:T(8,128)(2,1)} %bitcast.6), calls=%async_computation | async-start | bytes 6291456 | tf_op jit(solution)/shard_map/all_to_all | solution.py:104
  18.5 0.7 all-gather.3.cloned.1.call-update
  19.2 48.1 %all-gather.3.cloned.1.call-done = bf16[1024,1024]{1,0:T(8,128)(2,1)} async-done(((bf16[128,1024]{1,0:T(8,128)(2,1)}), bf16[1024,1024]{1,0:T(8,128)(2,1)}) %all-gather.3.cloned.1.call-update) | async-done | bytes 2097168 | tf_op jit(solution)/shard_map/all_gather | solution.py:107
  67.3 3.2 %copy.54 = bf16[2,4,128,1024]{3,1,2,0:T(4,128)(2,1)S(1)} copy(bf16[2,4,128,1024]{3,2,1,0:T(8,128)(2,1)} %bitcast.72) | data formatting | bytes 4194304 | tf_op jit(solution)/shard_map/reshape | solution.py:109
  70.5 0.9 copy.86
  71.4 3.1 %collective-permute-start = (bf16[2,4096]{1,0:T(2,128)(2,1)S(1)}, bf16[2,4096]{1,0:T(2,128)(2,1)S(1)}, u32[]{:S(2)}, u32[]{:S(2)}) collective-permute-start(bf16[2,4096]{1,0:T(2,128)(2,1)S(1)} %slice.108), channel_id=1, source_target_pairs={{0,8},{8,16},{16,24},{24,32},{32,40},{40,48},{48,56},{56,64},{64,7... | collective-permute-start | bytes 49160 | tf_op jit(solution)/shard_map/ppermute | solution.py:15
  74.6 0.8 collective-permute-done
  75.4 0.7 fusion.3
  76.2 6.3 %collective-permute-start.1 = (bf16[258,2048]{1,0:T(8,128)(2,1)S(1)}, bf16[258,2048]{1,0:T(8,128)(2,1)}, u32[]{:S(2)}, u32[]{:S(2)}) collective-permute-start(bf16[258,2048]{1,0:T(8,128)(2,1)S(1)} %fusion.3), channel_id=1, source_target_pairs={{0,128},{128,0},{1,129},{129,1},{2,130},{130,2},{3,131},{131,3},{4... | collective-permute-start | bytes 3170312 | tf_op jit(solution)/shard_map/ppermute | solution.py:89
  82.5 22.9 %collective-permute-done.1 = bf16[258,2048]{1,0:T(8,128)(2,1)} collective-permute-done((bf16[258,2048]{1,0:T(8,128)(2,1)S(1)}, bf16[258,2048]{1,0:T(8,128)(2,1)}, u32[]{:S(2)}, u32[]{:S(2)}) %collective-permute-start.1) | collective-permute-done | bytes 1056800 | tf_op jit(solution)/shard_map/ppermute | solution.py:89
  105.4 4.2 %fusion.54 = f32[258,768]{1,0:T(8,128)} fusion(bf16[258,2048]{1,0:T(8,128)(2,1)} %collective-permute-done.1, bf16[2048,768]{1,0:T(8,128)(2,1)} %bitcast.7), kind=kOutput, calls=%fused_computation.89 | convolution fusion | flops 811597824 | bytes 4995072 | tf_op jit(solution)/shard_map/dot_general | solution.py:116
  109.5 2.7 %collective-permute-start.2 = (f32[258,768]{1,0:T(8,128)}, f32[258,768]{1,0:T(8,128)}, u32[]{:S(2)}, u32[]{:S(2)}) collective-permute-start(f32[258,768]{1,0:T(8,128)} %fusion.54), channel_id=1, source_target_pairs={{0,128},{128,0},{1,129},{129,1},{2,130},{130,2},{3,131},{131,3},{4... | collective-permute-start | bytes 2377736 | tf_op jit(solution)/shard_map/ppermute | solution.py:89
  112.2 0.5 reshape.58
  112.7 0.4 dynamic-slice_reduce_fusion
  113.3 15.7 %collective-permute-done.2 = f32[258,768]{1,0:T(8,128)} collective-permute-done((f32[258,768]{1,0:T(8,128)}, f32[258,768]{1,0:T(8,128)}, u32[]{:S(2)}, u32[]{:S(2)}) %collective-permute-start.2) | collective-permute-done | bytes 792608 | tf_op jit(solution)/shard_map/ppermute | solution.py:89
  129.0 3.3 %fusion = bf16[258,768]{1,0:T(8,128)(2,1)S(1)} fusion(f32[258,768]{1,0:T(8,128)} %collective-permute-done.2, bf16[2048,768]{1,0:T(8,128)(2,1)} %bitcast.7, s32[]{:T(128)S(6)} %select_n.13, bf16[256,4096]{1,0:T(8,128)(2,1)S(1)} %bitcast.70, bf16[2,4096]{1,0:T(2,128)(2,1)S(1)} %collective-permute-done), kind=kOutput, calls=%fused_computation.5 | convolution fusion | flops 814107648 | bytes 6448132 | tf_op jit(solution)/shard_map/dot_general | solution.py:115
  132.4 0.2 fusion.33
  132.6 0.8 copy.58
  133.4 4.2 %all-to-all-start.1 = ((bf16[32,8,256]{2,1,0:T(8,128)(2,1)}), bf16[32,8,256]{2,1,0:T(8,128)(2,1)S(1)}, u32[]{:S(2)}, u32[]{:S(2)}) async-start(bf16[32,8,256]{2,1,0:T(8,128)(2,1)} %bitcast.19), calls=%async_computation.1 | async-start | bytes 262144 | tf_op jit(solution)/shard_map/all_to_all | solution.py:130
  137.6 0.6 convolution_negate_fusion
  138.3 6.7 %all-to-all-done.1 = bf16[32,8,256]{2,1,0:T(8,128)(2,1)S(1)} async-done(((bf16[32,8,256]{2,1,0:T(8,128)(2,1)}), bf16[32,8,256]{2,1,0:T(8,128)(2,1)S(1)}, u32[]{:S(2)}, u32[]{:S(2)}) %all-to-all-start.1) | async-done | bytes 131104 | tf_op jit(solution)/shard_map/all_to_all | solution.py:130
  145.0 0.4 fusion.1
  145.4 0.4 fusion.49
  145.9 0.8 multiply_subtract_fusion.1
  146.8 0.8 fusion.23
  147.7 0.8 fusion.29
  148.5 0.8 fusion.19
  149.3 0.8 fusion.25
  150.2 0.8 convolution_add_fusion.2
  151.0 0.8 convolution_add_fusion.3
  151.9 0.8 convolution_subtract_fusion.1
  152.7 0.9 multiply_subtract_fusion
  153.6 0.7 fusion.17
  154.2 0.7 fusion.13
  154.9 0.7 convolution_subtract_fusion
  155.6 0.7 convolution_add_fusion.1
  156.3 0.4 fusion.9
  156.8 0.4 fusion.2
  157.2 0.7 copy.75
  157.9 3.9 %all-to-all-start.2 = ((bf16[32,8,256]{2,1,0:T(8,128)(2,1)}), bf16[32,8,256]{2,1,0:T(8,128)(2,1)S(1)}, u32[]{:S(2)}, u32[]{:S(2)}) async-start(bf16[32,8,256]{2,1,0:T(8,128)(2,1)} %copy.75), calls=%async_computation.2 | async-start | bytes 262144 | tf_op jit(solution)/shard_map/all_to_all | solution.py:132
  162.1 7.3 %all-to-all-done.2 = bf16[32,8,256]{2,1,0:T(8,128)(2,1)S(1)} async-done(((bf16[32,8,256]{2,1,0:T(8,128)(2,1)}), bf16[32,8,256]{2,1,0:T(8,128)(2,1)S(1)}, u32[]{:S(2)}, u32[]{:S(2)}) %all-to-all-start.2) | async-done | bytes 131104 | tf_op jit(solution)/shard_map/all_to_all | solution.py:132
  169.4 0.1 copy.76
  169.5 0.1 fusion.39
  169.8 9.2 %all_to_all.20 = bf16[2,128,256]{1,2,0:T(8,128)(2,1)S(1)} all-to-all(bf16[2,128,256]{1,2,0:T(8,128)(2,1)S(1)} %copy.77), channel_id=1, replica_groups=mesh['xh'=2,'xl'=2,'zl'=2,'y'=4,'core'=2,'mp'=4] {'core'}, dimensions={0} | all-to-all | bytes 262144 | tf_op jit(solution)/shard_map/all_to_all | solution.py:137
  179.0 0.8 copy.79
  (35 shorter events, 0.9 us)
Async XLA Ops:
  6.5 131.1 %copy-start = (f32[8,8192]{1,0:T(8,128)S(1)}, f32[8,8192]{1,0:T(8,128)}, u32[]{:S(2)}) copy-start(f32[8,8192]{1,0:T(8,128)} %param.14) | copy-start | bytes 786436
  10.0 95.3 %all-to-all-start = ((bf16[32,64,768]{2,1,0:T(8,128)(2,1)}), bf16[32,64,768]{2,1,0:T(8,128)(2,1)}, u32[]{:S(2)}, u32[]{:S(2)}) async-start(bf16[32,64,768]{2,1,0:T(8,128)(2,1)} %bitcast.6), calls=%async_computation | async-start | bytes 6291456 | tf_op jit(solution)/shard_map/all_to_all | solution.py:104
  18.5 48.9 %all-gather.3.cloned.1.call-start = ((), (), s32[]{:S(2)}) async-start(), calls=%async_computation.4 | async-start | bytes 2359296 | tf_op jit(solution)/shard_map/all_gather | solution.py:107
  71.4 4.0 %collective-permute-start = (bf16[2,4096]{1,0:T(2,128)(2,1)S(1)}, bf16[2,4096]{1,0:T(2,128)(2,1)S(1)}, u32[]{:S(2)}, u32[]{:S(2)}) collective-permute-start(bf16[2,4096]{1,0:T(2,128)(2,1)S(1)} %slice.108), channel_id=1, source_target_pairs={{0,8},{8,16},{16,24},{24,32},{32,40},{40,48},{48,56},{56,64},{64,7... | collective-permute-start | bytes 49160 | tf_op jit(solution)/shard_map/ppermute | solution.py:15
  76.2 29.2 %collective-permute-start.1 = (bf16[258,2048]{1,0:T(8,128)(2,1)S(1)}, bf16[258,2048]{1,0:T(8,128)(2,1)}, u32[]{:S(2)}, u32[]{:S(2)}) collective-permute-start(bf16[258,2048]{1,0:T(8,128)(2,1)S(1)} %fusion.3), channel_id=1, source_target_pairs={{0,128},{128,0},{1,129},{129,1},{2,130},{130,2},{3,131},{131,3},{4... | collective-permute-start | bytes 3170312 | tf_op jit(solution)/shard_map/ppermute | solution.py:89
  105.4 6.8 %copy-start.7 = (f32[3,3,512]{2,1,0:T(4,128)S(1)}, f32[3,3,512]{2,1,0:T(4,128)}, u32[]{:S(2)}) copy-start(f32[3,3,512]{2,1,0:T(4,128)} %param.13) | copy-start | bytes 55300
  109.5 19.4 %collective-permute-start.2 = (f32[258,768]{1,0:T(8,128)}, f32[258,768]{1,0:T(8,128)}, u32[]{:S(2)}, u32[]{:S(2)}) collective-permute-start(f32[258,768]{1,0:T(8,128)} %fusion.54), channel_id=1, source_target_pairs={{0,128},{128,0},{1,129},{129,1},{2,130},{130,2},{3,131},{131,3},{4... | collective-permute-start | bytes 2377736 | tf_op jit(solution)/shard_map/ppermute | solution.py:89
  132.3 5.3 %copy-start.6 = (f32[64,32,1]{0,1,2:T(8,128)S(1)}, f32[64,32,1]{0,1,2:T(8,128)}, u32[]{:S(2)}) copy-start(f32[64,32,1]{0,1,2:T(8,128)} %constant.56) | copy-start | bytes 24580
  132.4 13.0 %copy-start.5 = (f32[64,32,1]{0,1,2:T(8,128)S(1)}, f32[64,32,1]{0,1,2:T(8,128)}, u32[]{:S(2)}) copy-start(f32[64,32,1]{0,1,2:T(8,128)} %constant.55) | copy-start | bytes 24580
  132.4 13.5 %copy-start.3 = (f32[64,256]{1,0:T(8,128)S(1)}, f32[64,256]{1,0:T(8,128)}, u32[]{:S(2)}) copy-start(f32[64,256]{1,0:T(8,128)} %constant.45.clone) | copy-start | bytes 196612
  132.4 13.5 %copy-start.4 = (f32[64,256]{1,0:T(8,128)S(1)}, f32[64,256]{1,0:T(8,128)}, u32[]{:S(2)}) copy-start(f32[64,256]{1,0:T(8,128)} %constant.46.clone) | copy-start | bytes 196612
  133.4 11.6 %all-to-all-start.1 = ((bf16[32,8,256]{2,1,0:T(8,128)(2,1)}), bf16[32,8,256]{2,1,0:T(8,128)(2,1)S(1)}, u32[]{:S(2)}, u32[]{:S(2)}) async-start(bf16[32,8,256]{2,1,0:T(8,128)(2,1)} %bitcast.19), calls=%async_computation.1 | async-start | bytes 262144 | tf_op jit(solution)/shard_map/all_to_all | solution.py:130
  145.9 1.0 copy-start.1
  147.7 2.5 %copy-start.2 = (f32[256,256,1]{1,0,2:T(8,128)S(1)}, f32[256,256,1]{1,0,2:T(8,128)}, u32[]{:S(2)}) copy-start(f32[256,256,1]{1,0,2:T(8,128)} %constant.58) | copy-start | bytes 786436
  154.9 1.4 copy-start.9
  154.9 1.8 copy-start.8
  156.3 5.5 %copy-start.10 = (f32[512]{0:T(512)S(1)}, f32[512]{0:T(512)}, u32[]{:S(2)}) copy-start(f32[512]{0:T(512)} %param.15) | copy-start | bytes 6148
  157.9 11.4 %all-to-all-start.2 = ((bf16[32,8,256]{2,1,0:T(8,128)(2,1)}), bf16[32,8,256]{2,1,0:T(8,128)(2,1)S(1)}, u32[]{:S(2)}, u32[]{:S(2)}) async-start(bf16[32,8,256]{2,1,0:T(8,128)(2,1)} %copy.75), calls=%async_computation.2 | async-start | bytes 262144 | tf_op jit(solution)/shard_map/all_to_all | solution.py:132
Sparse Core Ops, SparseCore 0:
  21.1 46.1 all-gather.2

commit v9 on v8

--- a/solution.py
+++ b/solution.py
@@ -104,22 +104,22 @@
     arrived = lax.all_to_all(spread, HALF, split_axis=0, concat_axis=0, tiled=True)
     weights = arrived.reshape(senders * w_proj.shape[0], 3 * half)
     depth = weights.shape[0]
-    stacked = lax.all_gather(tokens, ("core", "mp"), axis=0, tiled=False)
+    stacked = lax.all_gather(tokens, ("xh", "core", "mp"), axis=0, tiled=False)
     rows = 2 * rows_dev
-    source = jnp.transpose(stacked.reshape(2, -1, rows_dev, tokens.shape[1]), (0, 2, 1, 3)).reshape(rows, -1)
-    tail = shifted(source[rows - margin :], CHIP, 1)
-    extended_tokens = jnp.concatenate([tail, source], axis=0)
-    mine = lax.dynamic_slice_in_dim(extended_tokens, side * depth, depth, axis=1)
-    other = lax.dynamic_slice_in_dim(extended_tokens, (1 - side) * depth, depth, axis=1)
-    theirs = swap(other, "xh")
-    own_part = jnp.dot(mine, weights, preferred_element_type=jnp.float32)
-    their_part = jnp.dot(theirs, weights, preferred_element_type=jnp.float32)
-    projected_all = own_part + swap(their_part, "xh")
+    stacked = stacked.reshape(2, 2, -1, rows_dev, tokens.shape[1])
+    both = jnp.transpose(stacked, (0, 1, 3, 2, 4)).reshape(2, rows, -1)
+    mine = lax.dynamic_slice_in_dim(both, side * depth, depth, axis=2)
+    own_part = jnp.dot(lax.dynamic_index_in_dim(mine, side, 0, keepdims=False), weights,
+                       preferred_element_type=jnp.float32)
+    their_part = jnp.dot(lax.dynamic_index_in_dim(mine, 1 - side, 0, keepdims=False), weights,
+                         preferred_element_type=jnp.float32)
+    summed = (own_part + swap(their_part, "xh")).astype(jnp.bfloat16)
+    tail = shifted(summed[rows - margin :], CHIP, 1)
+    projected_all = jnp.concatenate([tail, summed], axis=0).astype(jnp.float32)
     taps = pick(short_filter, 2, parity)
     mixed = []
     for member in range(3):
-        projected = projected_all[:, member * half : (member + 1) * half]
-        extended = projected.astype(jnp.bfloat16).astype(jnp.float32)
+        extended = projected_all[:, member * half : (member + 1) * half]
         total = jnp.zeros((rows, half), jnp.float32)
         for offset in range(margin + 1):
             total = total + taps[member, offset][None] * extended[margin - offset : margin - offset + rows]

time: 187 us -> 191 us (1.021)
  local copies, waits for them, and re-layouts: 11.6 us -> 24.8 us
  starting transfers between devices: 28.7 us -> 25.4 us
  waiting for transfers between devices: 102 us -> 99.4 us
    ppermute x2 -> x1, waiting for transfers between devices: 38.6 us -> 15.1 us  [swap(): return lax.ppermute(value, axis, [(0, 1), (1, 0)])]
    all_gather x1, waiting for transfers between devices: 48.1 us -> 68.9 us  [on_device(): stacked = lax.all_gather(tokens, ('xh', 'core', 'mp'), axis=0, tiled=False)]
    reshape x1 -> x2, local copies, waits for them, and re-layouts: 3.21 us -> 15.1 us  [the longest x1 7.74 us: on_device(): both = jnp.transpose(stacked, (0, 1, 3, 2, 4)).reshape(2, rows, -1)]
    ppermute x2 -> x1, starting transfers between devices: 8.98 us -> 2.27 us  [swap(): return lax.ppermute(value, axis, [(0, 1), (1, 0)])]
    all_to_all x1, starting transfers between devices: 4.24 us -> 8.48 us  [on_device(): lax.all_to_all(outgoing, CHIP, split_axis=0, concat_axis=0, tiled=True)]
  transfers between devices with their start and end apart: 7 -> 6, of which waited for: 6 -> 5; matrix products, arithmetic and copies ran while one was open for 4% -> 12% of each run, Pallas kernels for 0% -> 0%
where the time goes in v9:
time: 191 us; the launch traced here: 190 us
  waiting for transfers between devices  99.4 us (52%)
  starting transfers between devices  25.4 us (13%)
  local copies, waits for them, and re-layouts  24.8 us (13%)
  matrix products  18.2 us (10%)
  between operations  13.8 us (7%)
  blocking collectives  8.33 us (4%)
    all_gather x1, waiting for transfers between devices, on_device(): stacked = lax.all_gather(tokens, ('xh', 'core', 'mp'), axis=0, tiled=False)  68.9 us
    ppermute x1, waiting for transfers between devices, swap(): return lax.ppermute(value, axis, [(0, 1), (1, 0)])  15.1 us
    all_to_all x1, starting transfers between devices, on_device(): lax.all_to_all(outgoing, CHIP, split_axis=0, concat_axis=0, tiled=True)  8.48 us
    all_to_all x1, starting transfers between devices, on_device(): lax.all_to_all(spread, HALF, split_axis=0, concat_axis=0, tiled=True)  8.4 us
    all_to_all x1, blocking collectives, on_device(): lax.all_to_all(local, 'core', split_axis=0, concat_axis=0, tiled=True)  8.33 us
    reshape x1, local copies, waits for them, and re-layouts, on_device(): both = jnp.transpose(stacked, (0, 1, 3, 2, 4)).reshape(2, rows, -1)  7.74 us
    reshape x1, local copies, waits for them, and re-layouts, on_device(): stacked = stacked.reshape(2, 2, -1, rows_dev, tokens.shape[1])  7.4 us
    all_to_all x1, waiting for transfers between devices, on_device(): lax.all_to_all(convolved, CHIP, split_axis=0, concat_axis=0, tiled=True)  7.29 us
  transfers between devices with their start and end apart: 6, of which 5 were waited for; matrix products, arithmetic and copies ran while one was open for 12% of the time, Pallas kernels for 0%

profile of v9, /device:TPU:1, one launch (start us, length us, event | category | flops | bytes accessed | tf_op | source)
XLA Modules:
  0.0 190.4 jit_solution(11357816538955803753)
XLA Ops:
  6.5 0.7 all-gather.3.cloned.1.call-update
  7.3 1.1 copy.55
  8.5 0.2 copy.57
  8.7 2.1 %broadcast_in_dim.5 = bf16[16,2,64,768]{3,2,1,0:T(8,128)(2,1)} broadcast(bf16[2,64,768]{2,1,0:T(8,128)(2,1)S(1)} %copy.57), dimensions={1,2,3} | broadcast | bytes 3342336 | tf_op jit(solution)/shard_map/broadcast_in_dim | solution.py:103
  10.7 8.4 %all-to-all-start = ((bf16[32,64,768]{2,1,0:T(8,128)(2,1)}), bf16[32,64,768]{2,1,0:T(8,128)(2,1)S(1)}, u32[]{:S(2)}, u32[]{:S(2)}) async-start(bf16[32,64,768]{2,1,0:T(8,128)(2,1)} %bitcast.7), calls=%async_computation | async-start | bytes 6291456 | tf_op jit(solution)/shard_map/all_to_all | solution.py:104
  19.1 68.9 %all-gather.3.cloned.1.call-done = bf16[2048,1024]{1,0:T(8,128)(2,1)} async-done(((bf16[128,1024]{1,0:T(8,128)(2,1)}), bf16[2048,1024]{1,0:T(8,128)(2,1)}) %all-gather.3.cloned.1.call-update) | async-done | bytes 4194320 | tf_op jit(solution)/shard_map/all_gather | solution.py:107
  88.0 7.4 %copy.123 = bf16[2,2,4,128,1024]{4,2,3,1,0:T(4,128)(2,1)} copy(bf16[2,2,4,128,1024]{4,3,2,1,0:T(8,128)(2,1)} %bitcast.74) | data formatting | bytes 8388608 | tf_op jit(solution)/shard_map/reshape | solution.py:109
  95.4 7.7 %reshape.61 = bf16[2,256,4096]{2,1,0:T(8,128)(2,1)} reshape(bf16[2,2,128,4,1024]{4,3,2,1,0:T(4,128)(2,1)} %bitcast.73) | data formatting | bytes 8388608 | tf_op jit(solution)/shard_map/reshape | solution.py:110
  103.2 3.2 %fusion.3 = f32[256,768]{1,0:T(8,128)} fusion(bf16[2048,768]{1,0:T(8,128)(2,1)S(1)} %bitcast.75, bf16[2,256,4096]{2,1,0:T(8,128)(2,1)} %reshape.61, s32[]{:T(128)S(6)} %select_n.28, s32[]{:T(128)S(6)} %select_n.26), kind=kOutput, calls=%fused_computation.14 | convolution fusion | flops 805306368 | bytes 4980744 | tf_op jit(solution)/shard_map/dot_general | solution.py:114
  106.4 2.3 %collective-permute-start = (f32[256,768]{1,0:T(8,128)}, f32[256,768]{1,0:T(8,128)}, u32[]{:S(2)}, u32[]{:S(2)}) collective-permute-start(f32[256,768]{1,0:T(8,128)} %fusion.3), channel_id=1, source_target_pairs={{0,128},{128,0},{1,129},{129,1},{2,130},{130,2},{3,131},{131,3},{4... | collective-permute-start | bytes 2359304 | tf_op jit(solution)/shard_map/ppermute | solution.py:89
  108.7 1.2 reshape.58
  109.9 1.4 dynamic-slice_reduce_fusion
  111.3 0.7 reshape.59
  112.0 15.1 %collective-permute-done = f32[256,768]{1,0:T(8,128)} collective-permute-done((f32[256,768]{1,0:T(8,128)}, f32[256,768]{1,0:T(8,128)}, u32[]{:S(2)}, u32[]{:S(2)}) %collective-permute-start) | collective-permute-done | bytes 786464 | tf_op jit(solution)/shard_map/ppermute | solution.py:89
  127.1 2.5 %fusion = bf16[256,768]{1,0:T(8,128)(2,1)S(1)} fusion(f32[256,768]{1,0:T(8,128)} %collective-permute-done, bf16[2048,768]{1,0:T(8,128)(2,1)S(1)} %bitcast.76, bf16[2,256,4096]{2,1,0:T(8,128)(2,1)} %reshape.61, s32[]{:T(128)S(6)} %select_n.24, s32[]{:T(128)S(6)} %select_n.26), kind=kOutput, calls=%fused_computation.2 | convolution fusion | flops 805699584 | bytes 5373960 | tf_op jit(solution)/shard_map/dot_general | solution.py:112
  129.7 2.4 %collective-permute-start.1 = (bf16[2,768]{1,0:T(2,128)(2,1)S(1)}, bf16[2,768]{1,0:T(2,128)(2,1)S(1)}, u32[]{:S(2)}, u32[]{:S(2)}) collective-permute-start(bf16[2,768]{1,0:T(2,128)(2,1)S(1)} %slice.105), channel_id=1, source_target_pairs={{0,8},{8,16},{16,24},{24,32},{32,40},{40,48},{48,56},{56,64},{64,7... | collective-permute-start | bytes 9224 | tf_op jit(solution)/shard_map/ppermute | solution.py:15
  132.1 0.7 collective-permute-done.1
  132.8 0.2 fusion.76
  133.0 0.8 copy.58
  133.8 8.5 %all-to-all-start.1 = ((bf16[32,8,256]{2,1,0:T(8,128)(2,1)}), bf16[32,8,256]{2,1,0:T(8,128)(2,1)S(1)}, u32[]{:S(2)}, u32[]{:S(2)}) async-start(bf16[32,8,256]{2,1,0:T(8,128)(2,1)} %bitcast.21), calls=%async_computation.1 | async-start | bytes 262144 | tf_op jit(solution)/shard_map/all_to_all | solution.py:130
  142.3 0.6 convolution_negate_fusion
  142.9 6.7 %all-to-all-done.1 = bf16[32,8,256]{2,1,0:T(8,128)(2,1)S(1)} async-done(((bf16[32,8,256]{2,1,0:T(8,128)(2,1)}), bf16[32,8,256]{2,1,0:T(8,128)(2,1)S(1)}, u32[]{:S(2)}, u32[]{:S(2)}) %all-to-all-start.1) | async-done | bytes 131104 | tf_op jit(solution)/shard_map/all_to_all | solution.py:130
  149.7 0.4 fusion.1
  150.1 0.4 fusion.51
  150.5 0.8 multiply_subtract_fusion.1
  151.4 0.8 fusion.25
  152.2 0.8 fusion.31
  153.0 0.8 fusion.21
  153.9 0.8 fusion.27
  154.7 0.8 convolution_add_fusion.2
  155.5 0.8 convolution_add_fusion.3
  156.4 0.8 convolution_subtract_fusion.1
  157.2 0.9 multiply_subtract_fusion
  158.1 0.7 fusion.19
  158.8 0.7 fusion.15
  159.4 0.7 convolution_subtract_fusion
  160.1 0.7 convolution_add_fusion.1
  160.8 0.4 fusion.11
  161.3 0.5 fusion.2
  161.7 0.7 copy.75
  162.5 3.9 %all-to-all-start.2 = ((bf16[32,8,256]{2,1,0:T(8,128)(2,1)}), bf16[32,8,256]{2,1,0:T(8,128)(2,1)S(1)}, u32[]{:S(2)}, u32[]{:S(2)}) async-start(bf16[32,8,256]{2,1,0:T(8,128)(2,1)} %copy.75), calls=%async_computation.2 | async-start | bytes 262144 | tf_op jit(solution)/shard_map/all_to_all | solution.py:132
  166.3 0.1 reshape.67
  166.6 7.3 %all-to-all-done.2 = bf16[32,8,256]{2,1,0:T(8,128)(2,1)S(1)} async-done(((bf16[32,8,256]{2,1,0:T(8,128)(2,1)}), bf16[32,8,256]{2,1,0:T(8,128)(2,1)S(1)}, u32[]{:S(2)}, u32[]{:S(2)}) %all-to-all-start.2) | async-done | bytes 131104 | tf_op jit(solution)/shard_map/all_to_all | solution.py:132
  173.9 0.1 copy.76
  174.1 0.3 fusion.41
  174.3 0.1 copy.77
  174.5 8.3 %all_to_all.20 = bf16[2,128,256]{1,2,0:T(8,128)(2,1)S(1)} all-to-all(bf16[2,128,256]{1,2,0:T(8,128)(2,1)S(1)} %copy.77), channel_id=1, replica_groups=mesh['xh'=2,'xl'=2,'zl'=2,'y'=4,'core'=2,'mp'=4] {'core'}, dimensions={0} | all-to-all | bytes 262144 | tf_op jit(solution)/shard_map/all_to_all | solution.py:137
  182.8 0.8 copy.79
  (34 shorter events, 0.4 us)
Async XLA Ops:
  6.5 135.7 %copy-start = (f32[8,8192]{1,0:T(8,128)S(1)}, f32[8,8192]{1,0:T(8,128)}, u32[]{:S(2)}) copy-start(f32[8,8192]{1,0:T(8,128)} %param.14) | copy-start | bytes 786436
  6.5 81.5 %all-gather.3.cloned.1.call-start = ((), (), s32[]{:S(2)}) async-start(), calls=%async_computation.4 | async-start | bytes 4456448 | tf_op jit(solution)/shard_map/all_gather | solution.py:107
  10.7 92.4 %all-to-all-start = ((bf16[32,64,768]{2,1,0:T(8,128)(2,1)}), bf16[32,64,768]{2,1,0:T(8,128)(2,1)S(1)}, u32[]{:S(2)}, u32[]{:S(2)}) async-start(bf16[32,64,768]{2,1,0:T(8,128)(2,1)} %bitcast.7), calls=%async_computation | async-start | bytes 6291456 | tf_op jit(solution)/shard_map/all_to_all | solution.py:104
  103.2 5.5 %copy-start.8 = (f32[3,3,512]{2,1,0:T(4,128)S(1)}, f32[3,3,512]{2,1,0:T(4,128)}, u32[]{:S(2)}) copy-start(f32[3,3,512]{2,1,0:T(4,128)} %param.13) | copy-start | bytes 55300
  106.4 20.7 %collective-permute-start = (f32[256,768]{1,0:T(8,128)}, f32[256,768]{1,0:T(8,128)}, u32[]{:S(2)}, u32[]{:S(2)}) collective-permute-start(f32[256,768]{1,0:T(8,128)} %fusion.3), channel_id=1, source_target_pairs={{0,128},{128,0},{1,129},{129,1},{2,130},{130,2},{3,131},{131,3},{4... | collective-permute-start | bytes 2359304 | tf_op jit(solution)/shard_map/ppermute | solution.py:89
  112.0 20.0 %copy-start.7 = (f32[3,3,256]{2,1,0:T(4,128)S(1)}, f32[3,3,256]{2,1,0:T(4,128)}, u32[]{:S(2)}) copy-start(f32[3,3,256]{2,1,0:T(4,128)} %reshape.59) | copy-start | bytes 27652
  129.6 12.7 %copy-start.6 = (f32[64,32,1]{0,1,2:T(8,128)S(1)}, f32[64,32,1]{0,1,2:T(8,128)}, u32[]{:S(2)}) copy-start(f32[64,32,1]{0,1,2:T(8,128)} %constant.94) | copy-start | bytes 24580
  129.6 20.5 %copy-start.5 = (f32[64,32,1]{0,1,2:T(8,128)S(1)}, f32[64,32,1]{0,1,2:T(8,128)}, u32[]{:S(2)}) copy-start(f32[64,32,1]{0,1,2:T(8,128)} %constant.93) | copy-start | bytes 24580
  129.6 20.9 %copy-start.3 = (f32[64,256]{1,0:T(8,128)S(1)}, f32[64,256]{1,0:T(8,128)}, u32[]{:S(2)}) copy-start(f32[64,256]{1,0:T(8,128)} %constant.83.clone) | copy-start | bytes 196612
  129.6 20.9 %copy-start.4 = (f32[64,256]{1,0:T(8,128)S(1)}, f32[64,256]{1,0:T(8,128)}, u32[]{:S(2)}) copy-start(f32[64,256]{1,0:T(8,128)} %constant.84.clone) | copy-start | bytes 196612
  129.7 3.1 %collective-permute-start.1 = (bf16[2,768]{1,0:T(2,128)(2,1)S(1)}, bf16[2,768]{1,0:T(2,128)(2,1)S(1)}, u32[]{:S(2)}, u32[]{:S(2)}) collective-permute-start(bf16[2,768]{1,0:T(2,128)(2,1)S(1)} %slice.105), channel_id=1, source_target_pairs={{0,8},{8,16},{16,24},{24,32},{32,40},{40,48},{48,56},{56,64},{64,7... | collective-permute-start | bytes 9224 | tf_op jit(solution)/shard_map/ppermute | solution.py:15
  133.8 15.9 %all-to-all-start.1 = ((bf16[32,8,256]{2,1,0:T(8,128)(2,1)}), bf16[32,8,256]{2,1,0:T(8,128)(2,1)S(1)}, u32[]{:S(2)}, u32[]{:S(2)}) async-start(bf16[32,8,256]{2,1,0:T(8,128)(2,1)} %bitcast.21), calls=%async_computation.1 | async-start | bytes 262144 | tf_op jit(solution)/shard_map/all_to_all | solution.py:130
  142.3 9.1 %copy-start.1 = (f32[256,256,1]{1,0,2:T(8,128)S(1)}, f32[256,256,1]{1,0,2:T(8,128)}, u32[]{:S(2)}) copy-start(f32[256,256,1]{1,0,2:T(8,128)} %constant.95) | copy-start | bytes 786436
  151.3 3.3 %copy-start.2 = (f32[256,256,1]{1,0,2:T(8,128)S(1)}, f32[256,256,1]{1,0,2:T(8,128)}, u32[]{:S(2)}) copy-start(f32[256,256,1]{1,0,2:T(8,128)} %constant.96) | copy-start | bytes 786436
  158.1 2.7 %copy-start.10 = (f32[32,64,1]{1,0,2:T(8,128)S(1)}, f32[32,64,1]{1,0,2:T(8,128)}, u32[]{:S(2)}) copy-start(f32[32,64,1]{1,0,2:T(8,128)} %constant.92) | copy-start | bytes 24580
  158.7 2.5 %copy-start.9 = (f32[32,64,1]{1,0,2:T(8,128)S(1)}, f32[32,64,1]{1,0,2:T(8,128)}, u32[]{:S(2)}) copy-start(f32[32,64,1]{1,0,2:T(8,128)} %constant.97) | copy-start | bytes 24580
  160.1 6.2 %copy-start.11 = (f32[512]{0:T(512)S(1)}, f32[512]{0:T(512)}, u32[]{:S(2)}) copy-start(f32[512]{0:T(512)} %param.15) | copy-start | bytes 6148
  162.5 11.4 %all-to-all-start.2 = ((bf16[32,8,256]{2,1,0:T(8,128)(2,1)}), bf16[32,8,256]{2,1,0:T(8,128)(2,1)S(1)}, u32[]{:S(2)}, u32[]{:S(2)}) async-start(bf16[32,8,256]{2,1,0:T(8,128)(2,1)} %copy.75), calls=%async_computation.2 | async-start | bytes 262144 | tf_op jit(solution)/shard_map/all_to_all | solution.py:132
Sparse Core Ops, SparseCore 0:
  10.1 77.8 all-gather.2

commit v10 on v7

--- a/solution.py
+++ b/solution.py
@@ -32,46 +32,42 @@
     )
 
 
-def forward(first_re, first_im, t):
+def block(cos, sin, sign):
+    return jnp.concatenate(
+        [jnp.concatenate([cos, sign * sin], axis=1), jnp.concatenate([-sign * sin, cos], axis=1)], axis=0
+    )
+
+
+def forward(first, t, cols):
     tc = t["twist_cos"][:, None, :]
     ts = t["twist_sin"][:, None, :]
-    b_re = first_re * tc + first_im * ts
-    b_im = first_im * tc - first_re * ts
-    dot = lambda a, m: jnp.einsum("krn,nm->krm", a, m, precision=HIGHEST)
-    x_re = dot(b_re, t["inner_cos"]) + dot(b_im, t["inner_sin"])
-    x_im = dot(b_im, t["inner_cos"]) - dot(b_re, t["inner_sin"])
-    return x_re, x_im
+    first_re, first_im = first[..., :cols], first[..., cols:]
+    turned = jnp.concatenate([first_re * tc + first_im * ts, first_im * tc - first_re * ts], axis=-1)
+    return jnp.einsum("krn,nm->krm", turned, block(t["inner_cos"], t["inner_sin"], -1.0), precision=HIGHEST)
 
 
 def long_conv(signal, kernel):
     live, channels, cols = signal.shape
     rows = 2 * live
-    t = tables(rows, cols)
-    oc = t["outer_cos"][:, :live]
-    os_ = t["outer_sin"][:, :live]
-    sig = signal.astype(jnp.float32)
-    s_re = jnp.einsum("kn,nrm->krm", oc, sig, precision=HIGHEST)
-    s_im = -jnp.einsum("kn,nrm->krm", os_, sig, precision=HIGHEST)
-    ker = kernel.reshape(channels, live, cols)
-    h_re = jnp.einsum("kn,rnm->krm", oc, ker, precision=HIGHEST)
-    h_im = -jnp.einsum("kn,rnm->krm", os_, ker, precision=HIGHEST)
-    su_re, su_im = forward(s_re, s_im, t)
-    sh_re, sh_im = forward(h_re, h_im, t)
-    z_re = su_re * sh_re - su_im * sh_im
-    z_im = su_re * sh_im + su_im * sh_re
-    dot = lambda a, m: jnp.einsum("krn,nm->krm", a, m, precision=HIGHEST)
-    d_re = dot(z_re, t["inner_cos"]) - dot(z_im, t["inner_sin"])
-    d_im = dot(z_im, t["inner_cos"]) + dot(z_re, t["inner_sin"])
+    t = lax.optimization_barrier(tables(rows, cols))
+    first = jnp.concatenate([t["outer_cos"][:, :live], -t["outer_sin"][:, :live]], axis=0)
+    sig = jnp.einsum("kn,nrm->krm", first, signal.astype(jnp.float32), precision=HIGHEST)
+    ker = jnp.einsum("kn,rnm->krm", first, kernel.reshape(channels, live, cols), precision=HIGHEST)
+    sig = jnp.concatenate([sig[:rows], sig[rows:]], axis=-1)
+    ker = jnp.concatenate([ker[:rows], ker[rows:]], axis=-1)
+    su = forward(sig, t, cols)
+    sh = forward(ker, t, cols)
+    su_re, su_im = su[..., :cols], su[..., cols:]
+    sh_re, sh_im = sh[..., :cols], sh[..., cols:]
+    z = jnp.concatenate([su_re * sh_re - su_im * sh_im, su_re * sh_im + su_im * sh_re], axis=-1)
+    d = jnp.einsum("krn,nm->krm", z, block(t["inner_cos"], t["inner_sin"], 1.0), precision=HIGHEST)
+    d_re, d_im = d[..., :cols], d[..., cols:]
     tc = t["twist_cos"][:, None, :]
     ts = t["twist_sin"][:, None, :]
-    e_re = d_re * tc - d_im * ts
-    e_im = d_im * tc + d_re * ts
+    e = jnp.concatenate([d_re * tc - d_im * ts, d_im * tc + d_re * ts], axis=0)
     scale = 1.0 / (rows * cols)
-    back_cos = t["outer_cos"][:live] * scale
-    back_sin = t["outer_sin"][:live] * scale
-    return jnp.einsum("nk,krm->nrm", back_cos, e_re, precision=HIGHEST) - jnp.einsum(
-        "nk,krm->nrm", back_sin, e_im, precision=HIGHEST
-    )
+    back = jnp.concatenate([t["outer_cos"][:live], -t["outer_sin"][:live]], axis=1) * scale
+    return jnp.einsum("nk,krm->nrm", back, e, precision=HIGHEST)
 
 
 def pick(values, axis, parity):

time: 171 us -> 169 us (0.988)
  matrix products: 17.1 us -> 14.3 us
    dot_general x18 -> x6, matrix products: 12.4 us -> 9.6 us  [the longest x2 4.78 us: forward(): jnp.einsum('krn,nm->krm', turned, block(t['inner_cos'], t['inner_sin'], -...]
where the time goes in v10:
time: 169 us; the launch traced here: 168 us
  waiting for transfers between devices  97.6 us (58%)
  starting transfers between devices  20.7 us (12%)
  matrix products  14.3 us (8%)
  between operations  13.8 us (8%)
  local copies, waits for them, and re-layouts  13.6 us (8%)
  blocking collectives  6.78 us (4%)
    all_gather x1, waiting for transfers between devices, on_device(): stacked = lax.all_gather(tokens, ('core', 'mp'), axis=0, tiled=False)  48.3 us
    all_to_all x1, waiting for transfers between devices, on_device(): lax.all_to_all(spread, ('chip', 'core'), split_axis=0, concat_axis=0, til...  34.3 us
    all_to_all x1, starting transfers between devices, on_device(): lax.all_to_all(spread, ('chip', 'core'), split_axis=0, concat_axis=0, til...  10.6 us
    all_to_all x1, waiting for transfers between devices, on_device(): lax.all_to_all(convolved, 'chip', split_axis=0, concat_axis=0, tiled=True)  7.29 us
    all_to_all x1, blocking collectives, on_device(): lax.all_to_all(local, 'core', split_axis=0, concat_axis=0, tiled=True)  6.78 us
    all_to_all x1, waiting for transfers between devices, on_device(): lax.all_to_all(outgoing, 'chip', split_axis=0, concat_axis=0, tiled=True)  6.38 us
    dot_general x2, matrix products, forward(): jnp.einsum('krn,nm->krm', turned, block(t['inner_cos'], t['inner_sin'], -...  4.78 us
    dot_general x1, matrix products, on_device(): jnp.dot(extended_tokens, weights, preferred_element_type=jnp.float32)  4.71 us
  transfers between devices with their start and end apart: 5, of which 5 were waited for; matrix products, arithmetic and copies ran while one was open for 4% of the time, Pallas kernels for 0%

profile of v10, /device:TPU:1, one launch (start us, length us, event | category | flops | bytes accessed | tf_op | source)
XLA Modules:
  0.0 168.1 jit_solution(15649347877112997294)
XLA Ops:
  6.5 1.2 copy.75
  7.7 0.1 copy.76
  7.8 0.2 copy.77
  8.0 3.4 %broadcast_in_dim.5 = bf16[32,2,64,768]{3,2,1,0:T(8,128)(2,1)} broadcast(bf16[2,64,768]{2,1,0:T(8,128)(2,1)S(1)} %copy.77), dimensions={1,2,3} | broadcast | bytes 6488064 | tf_op jit(solution)/shard_map/broadcast_in_dim | solution.py:89
  11.4 10.6 %all-to-all-start = ((bf16[64,64,768]{2,1,0:T(8,128)(2,1)}), bf16[64,64,768]{2,1,0:T(8,128)(2,1)}, u32[]{:S(2)}, u32[]{:S(2)}) async-start(bf16[64,64,768]{2,1,0:T(8,128)(2,1)} %bitcast.54), calls=%async_computation | async-start | bytes 12582912 | tf_op jit(solution)/shard_map/all_to_all | solution.py:90
  22.0 0.0 all-gather.3.cloned.1.call-start
  22.1 0.7 all-gather.3.cloned.1.call-update
  22.8 0.5 reshape.58
  23.2 0.4 dynamic-slice_reduce_fusion
  23.7 0.1 reshape.59
  23.9 48.3 %all-gather.3.cloned.1.call-done = bf16[1024,1024]{1,0:T(8,128)(2,1)} async-done(((bf16[128,1024]{1,0:T(8,128)(2,1)}), bf16[1024,1024]{1,0:T(8,128)(2,1)}) %all-gather.3.cloned.1.call-update) | async-done | bytes 2097168 | tf_op jit(solution)/shard_map/all_gather | solution.py:92
  72.2 3.2 %copy.74 = bf16[2,4,128,1024]{3,1,2,0:T(4,128)(2,1)S(1)} copy(bf16[2,4,128,1024]{3,2,1,0:T(8,128)(2,1)} %bitcast.58) | data formatting | bytes 4194304 | tf_op jit(solution)/shard_map/reshape | solution.py:94
  75.4 0.0 copy-start.5
  75.4 0.9 copy.94
  76.3 2.1 %collective-permute-start = (bf16[2,4096]{1,0:T(2,128)(2,1)S(1)}, bf16[2,4096]{1,0:T(2,128)(2,1)S(1)}, u32[]{:S(2)}, u32[]{:S(2)}) collective-permute-start(bf16[2,4096]{1,0:T(2,128)(2,1)S(1)} %slice.148), channel_id=1, source_target_pairs={{0,8},{8,16},{16,24},{24,32},{32,40},{40,48},{48,56},{56,64},{64,7... | collective-permute-start | bytes 49160 | tf_op jit(solution)/shard_map/ppermute | solution.py:15
  78.5 0.1 copy.79
  78.5 0.1 copy.78
  78.6 0.7 collective-permute-done
  79.3 34.3 %all-to-all-done = bf16[64,64,768]{2,1,0:T(8,128)(2,1)} async-done(((bf16[64,64,768]{2,1,0:T(8,128)(2,1)}), bf16[64,64,768]{2,1,0:T(8,128)(2,1)}, u32[]{:S(2)}, u32[]{:S(2)}) %all-to-all-start) | async-done | bytes 6291488 | tf_op jit(solution)/shard_map/all_to_all | solution.py:90
  113.6 4.7 %fusion.4 = bf16[258,768]{1,0:T(8,128)(2,1)S(1)} fusion(bf16[4096,768]{1,0:T(8,128)(2,1)} %bitcast.7, bf16[256,4096]{1,0:T(8,128)(2,1)S(1)} %bitcast.57, bf16[2,4096]{1,0:T(2,128)(2,1)S(1)} %collective-permute-done), kind=kOutput, calls=%fused_computation.8 | convolution fusion | flops 1627620864 | bytes 8801280 | tf_op jit(solution)/shard_map/dot_general | solution.py:99
  118.3 0.1 slice_convert_fusion.1
  118.4 0.2 fusion.27
  118.6 0.8 copy.80
  119.3 4.0 %all-to-all-start.1 = ((bf16[32,8,256]{2,1,0:T(8,128)(2,1)}), bf16[32,8,256]{2,1,0:T(8,128)(2,1)S(1)}, u32[]{:S(2)}, u32[]{:S(2)}) async-start(bf16[32,8,256]{2,1,0:T(8,128)(2,1)} %bitcast.19), calls=%async_computation.1 | async-start | bytes 262144 | tf_op jit(solution)/shard_map/all_to_all | solution.py:110
  123.4 1.1 fusion.35
  124.5 6.4 %all-to-all-done.1 = bf16[32,8,256]{2,1,0:T(8,128)(2,1)S(1)} async-done(((bf16[32,8,256]{2,1,0:T(8,128)(2,1)}), bf16[32,8,256]{2,1,0:T(8,128)(2,1)S(1)}, u32[]{:S(2)}, u32[]{:S(2)}) %all-to-all-start.1) | async-done | bytes 131104 | tf_op jit(solution)/shard_map/all_to_all | solution.py:110
  130.9 0.7 fusion.37
  131.6 0.3 multiply_add_fusion.3
  131.9 0.3 pad_maximum_fusion.5
  132.2 0.7 copy-done.2
  132.8 2.4 %fusion.19 = f32[64,8,512]{2,1,0:T(8,128)S(1)} fusion(f32[64,8,512]{2,0,1:T(8,128)S(1)} %get-tuple-element.40, f32[256,256]{1,0:T(8,128)S(1)} %copy-done.2, f32[256,256]{1,0:T(8,128)S(1)} %copy-done.1, f32[256,256]{1,0:T(8,128)S(1)} %broadcast_multiply_fusion), kind=kOutput, calls=%fused_computation.24 | convolution fusion | flops 1611399168 | bytes 2883584 | tf_op jit(solution)/shard_map/krn,nm->krm/dot_general | solution.py:46
  135.2 2.4 %fusion.21 = f32[64,8,512]{2,1,0:T(8,128)S(1)} fusion(f32[64,8,512]{2,0,1:T(8,128)S(1)} %get-tuple-element.39, f32[256,256]{1,0:T(8,128)S(1)} %copy-done.2, f32[256,256]{1,0:T(8,128)S(1)} %copy-done.1, f32[256,256]{1,0:T(8,128)S(1)} %broadcast_multiply_fusion), kind=kOutput, calls=%fused_computation.26 | convolution fusion | flops 1611399168 | bytes 2883584 | tf_op jit(solution)/shard_map/krn,nm->krm/dot_general | solution.py:46
  137.6 0.1 multiply_subtract_fusion.1
  137.8 0.1 pad_maximum_fusion.7
  137.9 2.4 %fusion.11 = f32[64,8,512]{2,0,1:T(8,128)S(1)} fusion(f32[256,256]{1,0:T(8,128)S(1)} %copy-done.2, f32[256,256]{1,0:T(8,128)S(1)} %broadcast_multiply_fusion, f32[256,256]{1,0:T(8,128)S(1)} %copy-done.1, f32[64,8,512]{2,1,0:T(8,128)S(1)} %pad_maximum_fusion.7), kind=kOutput, calls=%fused_computation.14 | convolution fusion | flops 1611399168 | bytes 2883584 | tf_op jit(solution)/shard_map/krn,nm->krm/dot_general | solution.py:63
  140.3 0.1 multiply_subtract_fusion
  140.5 0.6 convolution_convert_fusion
  141.1 0.7 copy.87
  141.9 3.9 %all-to-all-start.2 = ((bf16[32,8,256]{2,1,0:T(8,128)(2,1)}), bf16[32,8,256]{2,1,0:T(8,128)(2,1)S(1)}, u32[]{:S(2)}, u32[]{:S(2)}) async-start(bf16[32,8,256]{2,1,0:T(8,128)(2,1)} %copy.87), calls=%async_computation.2 | async-start | bytes 262144 | tf_op jit(solution)/shard_map/all_to_all | solution.py:112
  145.7 0.1 reshape.67
  145.9 0.1 dynamic-slice_reduce_fusion.1
  145.9 0.1 mul.254
  146.0 7.3 %all-to-all-done.2 = bf16[32,8,256]{2,1,0:T(8,128)(2,1)S(1)} async-done(((bf16[32,8,256]{2,1,0:T(8,128)(2,1)}), bf16[32,8,256]{2,1,0:T(8,128)(2,1)S(1)}, u32[]{:S(2)}, u32[]{:S(2)}) %all-to-all-start.2) | async-done | bytes 131104 | tf_op jit(solution)/shard_map/all_to_all | solution.py:112
  153.3 0.1 copy.88
  153.5 0.1 fusion.33
  153.6 0.1 copy.89
  153.7 6.8 %all_to_all.20 = bf16[2,128,256]{1,2,0:T(8,128)(2,1)S(1)} all-to-all(bf16[2,128,256]{1,2,0:T(8,128)(2,1)S(1)} %copy.89), channel_id=1, replica_groups=mesh['chip'=32,'core'=2,'mp'=4] {'core'}, dimensions={0} | all-to-all | bytes 262144 | tf_op jit(solution)/shard_map/all_to_all | solution.py:117
  160.5 0.8 copy.91
  (24 shorter events, 0.1 us)
Async XLA Ops:
  6.5 116.8 %copy-start = (f32[8,8192]{1,0:T(8,128)S(1)}, f32[8,8192]{1,0:T(8,128)}, u32[]{:S(2)}) copy-start(f32[8,8192]{1,0:T(8,128)} %param.14) | copy-start | bytes 786436
  11.4 11.4 %copy-start.7 = (f32[3,3,512]{2,1,0:T(4,128)S(1)}, f32[3,3,512]{2,1,0:T(4,128)}, u32[]{:S(2)}) copy-start(f32[3,3,512]{2,1,0:T(4,128)} %param.13) | copy-start | bytes 55300
  11.4 12.4 %copy-start.6 = (f32[64,64]{1,0:T(8,128)S(1)}, f32[64,64]{1,0:T(8,128)}, u32[]{:S(2)}) copy-start(f32[64,64]{1,0:T(8,128)} %constant.33.clone) | copy-start | bytes 49156
  11.4 12.5 %copy-start.1 = (f32[256,256]{1,0:T(8,128)S(1)}, f32[256,256]{1,0:T(8,128)}, u32[]{:S(2)}) copy-start(f32[256,256]{1,0:T(8,128)} %constant.35.clone) | copy-start | bytes 786436
  11.4 102.2 %all-to-all-start = ((bf16[64,64,768]{2,1,0:T(8,128)(2,1)}), bf16[64,64,768]{2,1,0:T(8,128)(2,1)}, u32[]{:S(2)}, u32[]{:S(2)}) async-start(bf16[64,64,768]{2,1,0:T(8,128)(2,1)} %bitcast.54), calls=%async_computation | async-start | bytes 12582912 | tf_op jit(solution)/shard_map/all_to_all | solution.py:90
  22.0 50.2 %all-gather.3.cloned.1.call-start = ((), (), s32[]{:S(2)}) async-start(), calls=%async_computation.4 | async-start | bytes 2359296 | tf_op jit(solution)/shard_map/all_gather | solution.py:92
  75.4 3.1 %copy-start.5 = (f32[64,64]{1,0:T(8,128)S(1)}, f32[64,64]{1,0:T(8,128)}, u32[]{:S(2)}) copy-start(f32[64,64]{1,0:T(8,128)} %constant.32.clone) | copy-start | bytes 49156
  76.3 3.0 %collective-permute-start = (bf16[2,4096]{1,0:T(2,128)(2,1)S(1)}, bf16[2,4096]{1,0:T(2,128)(2,1)S(1)}, u32[]{:S(2)}, u32[]{:S(2)}) collective-permute-start(bf16[2,4096]{1,0:T(2,128)(2,1)S(1)} %slice.148), channel_id=1, source_target_pairs={{0,8},{8,16},{16,24},{24,32},{32,40},{40,48},{48,56},{56,64},{64,7... | collective-permute-start | bytes 49160 | tf_op jit(solution)/shard_map/ppermute | solution.py:15
  118.4 13.2 %copy-start.3 = (f32[64,256]{1,0:T(8,128)S(1)}, f32[64,256]{1,0:T(8,128)}, u32[]{:S(2)}) copy-start(f32[64,256]{1,0:T(8,128)} %constant.36.clone) | copy-start | bytes 196612
  118.4 13.2 %copy-start.4 = (f32[64,256]{1,0:T(8,128)S(1)}, f32[64,256]{1,0:T(8,128)}, u32[]{:S(2)}) copy-start(f32[64,256]{1,0:T(8,128)} %constant.37.clone) | copy-start | bytes 196612
  119.3 11.5 %all-to-all-start.1 = ((bf16[32,8,256]{2,1,0:T(8,128)(2,1)}), bf16[32,8,256]{2,1,0:T(8,128)(2,1)S(1)}, u32[]{:S(2)}, u32[]{:S(2)}) async-start(bf16[32,8,256]{2,1,0:T(8,128)(2,1)} %bitcast.19), calls=%async_computation.1 | async-start | bytes 262144 | tf_op jit(solution)/shard_map/all_to_all | solution.py:110
  131.9 1.0 copy-start.2
  140.3 5.4 %copy-start.8 = (f32[512]{0:T(512)S(1)}, f32[512]{0:T(512)}, u32[]{:S(2)}) copy-start(f32[512]{0:T(512)} %param.15) | copy-start | bytes 6148
  141.9 11.4 %all-to-all-start.2 = ((bf16[32,8,256]{2,1,0:T(8,128)(2,1)}), bf16[32,8,256]{2,1,0:T(8,128)(2,1)S(1)}, u32[]{:S(2)}, u32[]{:S(2)}) async-start(bf16[32,8,256]{2,1,0:T(8,128)(2,1)} %copy.87), calls=%async_computation.2 | async-start | bytes 262144 | tf_op jit(solution)/shard_map/all_to_all | solution.py:112
Sparse Core Ops, SparseCore 0:
  24.7 47.4 all-gather.2

commit v11 on v10

--- a/solution.py
+++ b/solution.py
@@ -4,6 +4,7 @@
 import jax.numpy as jnp
 from jax import lax
 from jax.sharding import PartitionSpec as P
+
 
 HIGHEST = lax.Precision.HIGHEST
 GROUP = 8
@@ -43,7 +44,8 @@
     ts = t["twist_sin"][:, None, :]
     first_re, first_im = first[..., :cols], first[..., cols:]
     turned = jnp.concatenate([first_re * tc + first_im * ts, first_im * tc - first_re * ts], axis=-1)
-    return jnp.einsum("krn,nm->krm", turned, block(t["inner_cos"], t["inner_sin"], -1.0), precision=HIGHEST)
+    matrix = block(t["inner_cos"], t["inner_sin"], -1.0)
+    return jnp.einsum("krn,nm->krm", turned, matrix, precision=HIGHEST)
 
 
 def long_conv(signal, kernel):
@@ -51,12 +53,13 @@
     rows = 2 * live
     t = lax.optimization_barrier(tables(rows, cols))
     first = jnp.concatenate([t["outer_cos"][:, :live], -t["outer_sin"][:, :live]], axis=0)
+    own_kernel, own_first, own_t = lax.optimization_barrier((kernel, first, t))
+    ker = jnp.einsum("kn,rnm->krm", own_first, own_kernel.reshape(channels, live, cols), precision=HIGHEST)
+    ker = jnp.concatenate([ker[:rows], ker[rows:]], axis=-1)
+    sh = forward(ker, own_t, cols)
     sig = jnp.einsum("kn,nrm->krm", first, signal.astype(jnp.float32), precision=HIGHEST)
-    ker = jnp.einsum("kn,rnm->krm", first, kernel.reshape(channels, live, cols), precision=HIGHEST)
     sig = jnp.concatenate([sig[:rows], sig[rows:]], axis=-1)
-    ker = jnp.concatenate([ker[:rows], ker[rows:]], axis=-1)
     su = forward(sig, t, cols)
-    sh = forward(ker, t, cols)
     su_re, su_im = su[..., :cols], su[..., cols:]
     sh_re, sh_im = sh[..., :cols], sh[..., cols:]
     z = jnp.concatenate([su_re * sh_re - su_im * sh_im, su_re * sh_im + su_im * sh_re], axis=-1)
@@ -77,7 +80,7 @@
     return taken.reshape(shape[:axis] + (shape[axis] // 2,) + shape[axis + 1 :])
 
 
-def on_device(tokens, w_proj, short_filter, long_filter, skip_gain):
+def layer(tokens, w_proj, short_filter, long_filter, skip_gain):
     rows_dev = tokens.shape[0]
     margin = short_filter.shape[1] - 1
     width = w_proj.shape[2]
@@ -125,7 +128,7 @@
     inner = jax.sharding.Mesh(devices, ("chip", "core", "mp"))
     seq = ("chip", "core")
     return jax.shard_map(
-        on_device,
+        layer,
         mesh=inner,
         in_specs=(
             P(seq, "mp"),

time: 169 us -> 166 us (0.982)
  waiting for transfers between devices: 97.6 us -> 92.7 us
    all_gather x1, waiting for transfers between devices: 48.3 us -> 43.6 us  [layer(): stacked = lax.all_gather(tokens, ('core', 'mp'), axis=0, tiled=False)]
    unnamed x20 -> x22, local copies, waits for them, and re-layouts: 2.76 us -> 4.14 us
  transfers between devices with their start and end apart: 5 -> 5, of which waited for: 5 -> 5; matrix products, arithmetic and copies ran while one was open for 4% -> 6% of each run, Pallas kernels for 0% -> 0%
where the time goes in v11:
time: 166 us; the launch traced here: 165 us
  waiting for transfers between devices  92.7 us (56%)
  starting transfers between devices  20.7 us (12%)
  local copies, waits for them, and re-layouts  14.9 us (9%)
  matrix products  14.8 us (9%)
  between operations  13.8 us (8%)
  blocking collectives  6.94 us (4%)
    all_gather x1, waiting for transfers between devices, layer(): stacked = lax.all_gather(tokens, ('core', 'mp'), axis=0, tiled=False)  43.6 us
    all_to_all x1, waiting for transfers between devices, layer(): lax.all_to_all(spread, ('chip', 'core'), split_axis=0, concat_axis=0, til...  32.9 us
    all_to_all x1, starting transfers between devices, layer(): lax.all_to_all(spread, ('chip', 'core'), split_axis=0, concat_axis=0, til...  10.6 us
    all_to_all x1, waiting for transfers between devices, layer(): lax.all_to_all(outgoing, 'chip', split_axis=0, concat_axis=0, tiled=True)  7.34 us
    all_to_all x1, waiting for transfers between devices, layer(): lax.all_to_all(convolved, 'chip', split_axis=0, concat_axis=0, tiled=True)  7.31 us
    all_to_all x1, blocking collectives, layer(): lax.all_to_all(local, 'core', split_axis=0, concat_axis=0, tiled=True)  6.94 us
    dot_general x1, matrix products, layer(): jnp.dot(extended_tokens, weights, preferred_element_type=jnp.float32)  5.29 us
    dot_general x2, matrix products, forward(): return jnp.einsum('krn,nm->krm', turned, matrix, precision=HIGHEST)  4.8 us
  transfers between devices with their start and end apart: 5, of which 5 were waited for; matrix products, arithmetic and copies ran while one was open for 6% of the time, Pallas kernels for 0%

profile of v11, /device:TPU:1, one launch (start us, length us, event | category | flops | bytes accessed | tf_op | source)
XLA Modules:
  0.0 165.3 jit_solution(10129451022005991713)
XLA Ops:
  6.5 1.2 copy.75
  7.7 0.1 copy.76
  7.8 0.2 copy.77
  8.0 3.4 %broadcast_in_dim.5 = bf16[32,2,64,768]{3,2,1,0:T(8,128)(2,1)} broadcast(bf16[2,64,768]{2,1,0:T(8,128)(2,1)S(1)} %copy.77), dimensions={1,2,3} | broadcast | bytes 6488064 | tf_op jit(solution)/shard_map/broadcast_in_dim | solution.py:92
  11.4 10.6 %all-to-all-start = ((bf16[64,64,768]{2,1,0:T(8,128)(2,1)}), bf16[64,64,768]{2,1,0:T(8,128)(2,1)}, u32[]{:S(2)}, u32[]{:S(2)}) async-start(bf16[64,64,768]{2,1,0:T(8,128)(2,1)} %bitcast.58), calls=%async_computation | async-start | bytes 12582912 | tf_op jit(solution)/shard_map/all_to_all | solution.py:93
  22.1 0.7 all-gather.3.cloned.1.call-update
  22.8 0.1 copy.79
  22.9 0.1 copy.78
  22.9 0.1 pad_maximum_fusion.9
  23.0 0.5 reshape.60
  23.5 0.4 dynamic-slice_reduce_fusion
  23.9 0.1 reshape.61
  24.1 1.0 fusion.42
  25.2 0.1 multiply_add_fusion.2
  25.3 0.1 pad_maximum_fusion.7
  25.5 0.6 copy-done.1
  26.2 2.4 %fusion.17 = f32[64,8,512]{2,1,0:T(8,128)S(1)} fusion(f32[256,256]{1,0:T(8,128)S(1)} %copy-done.2, f32[256,256]{1,0:T(8,128)S(1)} %copy-done.1, f32[256,256]{1,0:T(8,128)S(1)} %broadcast_multiply_fusion, f32[64,8,512]{2,0,1:T(8,128)S(1)} %pad_maximum_fusion.7), kind=kOutput, calls=%fused_computation.21 | convolution fusion | flops 1611399168 | bytes 2883584 | tf_op jit(solution)/shard_map/krn,nm->krm/dot_general | solution.py:48
  28.6 43.6 %all-gather.3.cloned.1.call-done = bf16[1024,1024]{1,0:T(8,128)(2,1)} async-done(((bf16[128,1024]{1,0:T(8,128)(2,1)}), bf16[1024,1024]{1,0:T(8,128)(2,1)}) %all-gather.3.cloned.1.call-update) | async-done | bytes 2097168 | tf_op jit(solution)/shard_map/all_gather | solution.py:95
  72.2 3.2 %copy.74 = bf16[2,4,128,1024]{3,1,2,0:T(4,128)(2,1)S(1)} copy(bf16[2,4,128,1024]{3,2,1,0:T(8,128)(2,1)} %bitcast.62) | data formatting | bytes 4194304 | tf_op jit(solution)/shard_map/reshape | solution.py:97
  75.4 0.9 copy.94
  76.3 1.3 copy-done.3
  77.7 2.1 %collective-permute-start = (bf16[2,4096]{1,0:T(2,128)(2,1)S(1)}, bf16[2,4096]{1,0:T(2,128)(2,1)S(1)}, u32[]{:S(2)}, u32[]{:S(2)}) collective-permute-start(bf16[2,4096]{1,0:T(2,128)(2,1)S(1)} %slice.148), channel_id=1, source_target_pairs={{0,8},{8,16},{16,24},{24,32},{32,40},{40,48},{48,56},{56,64},{64,7... | collective-permute-start | bytes 49160 | tf_op jit(solution)/shard_map/ppermute | solution.py:16
  79.8 0.8 collective-permute-done
  80.6 32.9 %all-to-all-done = bf16[64,64,768]{2,1,0:T(8,128)(2,1)} async-done(((bf16[64,64,768]{2,1,0:T(8,128)(2,1)}), bf16[64,64,768]{2,1,0:T(8,128)(2,1)}, u32[]{:S(2)}, u32[]{:S(2)}) %all-to-all-start) | async-done | bytes 6291488 | tf_op jit(solution)/shard_map/all_to_all | solution.py:93
  113.6 5.3 %fusion.4 = bf16[258,768]{1,0:T(8,128)(2,1)S(1)} fusion(bf16[4096,768]{1,0:T(8,128)(2,1)} %bitcast.7, bf16[256,4096]{1,0:T(8,128)(2,1)} %bitcast.61, bf16[2,4096]{1,0:T(2,128)(2,1)S(1)} %collective-permute-done), kind=kOutput, calls=%fused_computation.8 | convolution fusion | flops 1627620864 | bytes 8801280 | tf_op jit(solution)/shard_map/dot_general | solution.py:102
  118.9 0.2 fusion.34
  119.1 0.8 copy.80
  119.9 4.0 %all-to-all-start.1 = ((bf16[32,8,256]{2,1,0:T(8,128)(2,1)}), bf16[32,8,256]{2,1,0:T(8,128)(2,1)S(1)}, u32[]{:S(2)}, u32[]{:S(2)}) async-start(bf16[32,8,256]{2,1,0:T(8,128)(2,1)} %bitcast.19), calls=%async_computation.1 | async-start | bytes 262144 | tf_op jit(solution)/shard_map/all_to_all | solution.py:113
  124.0 7.3 %all-to-all-done.1 = bf16[32,8,256]{2,1,0:T(8,128)(2,1)S(1)} async-done(((bf16[32,8,256]{2,1,0:T(8,128)(2,1)}), bf16[32,8,256]{2,1,0:T(8,128)(2,1)S(1)}, u32[]{:S(2)}, u32[]{:S(2)}) %all-to-all-start.1) | async-done | bytes 131104 | tf_op jit(solution)/shard_map/all_to_all | solution.py:113
  131.3 0.6 fusion.44
  131.9 0.1 multiply_add_fusion.3
  132.1 0.1 pad_maximum_fusion.6
  132.2 2.4 %fusion.9 = f32[64,8,512]{2,1,0:T(8,128)S(1)} fusion(f32[256,256]{1,0:T(8,128)S(1)} %copy-done.2, f32[256,256]{1,0:T(8,128)S(1)} %copy-done.1, f32[256,256]{1,0:T(8,128)S(1)} %broadcast_multiply_fusion.1, f32[64,8,512]{2,0,1:T(8,128)S(1)} %pad_maximum_fusion.6), kind=kOutput, calls=%fused_computation.12 | convolution fusion | flops 1611399168 | bytes 2883584 | tf_op jit(solution)/shard_map/krn,nm->krm/dot_general | solution.py:48
  134.6 0.1 multiply_subtract_fusion.1
  134.8 0.1 pad_maximum_fusion.8
  134.9 2.4 %fusion.13 = f32[64,8,512]{2,0,1:T(8,128)S(1)} fusion(f32[256,256]{1,0:T(8,128)S(1)} %copy-done.2, f32[256,256]{1,0:T(8,128)S(1)} %broadcast_multiply_fusion.1, f32[256,256]{1,0:T(8,128)S(1)} %copy-done.1, f32[64,8,512]{2,1,0:T(8,128)S(1)} %pad_maximum_fusion.8), kind=kOutput, calls=%fused_computation.15 | convolution fusion | flops 1611399168 | bytes 2883584 | tf_op jit(solution)/shard_map/krn,nm->krm/dot_general | solution.py:66
  137.3 0.1 multiply_subtract_fusion
  137.5 0.6 convolution_convert_fusion
  138.1 0.7 copy.87
  138.9 3.9 %all-to-all-start.2 = ((bf16[32,8,256]{2,1,0:T(8,128)(2,1)}), bf16[32,8,256]{2,1,0:T(8,128)(2,1)S(1)}, u32[]{:S(2)}, u32[]{:S(2)}) async-start(bf16[32,8,256]{2,1,0:T(8,128)(2,1)} %copy.87), calls=%async_computation.2 | async-start | bytes 262144 | tf_op jit(solution)/shard_map/all_to_all | solution.py:115
  142.7 0.1 reshape.69
  142.9 0.1 mul.263
  143.0 7.3 %all-to-all-done.2 = bf16[32,8,256]{2,1,0:T(8,128)(2,1)S(1)} async-done(((bf16[32,8,256]{2,1,0:T(8,128)(2,1)}), bf16[32,8,256]{2,1,0:T(8,128)(2,1)S(1)}, u32[]{:S(2)}, u32[]{:S(2)}) %all-to-all-start.2) | async-done | bytes 131104 | tf_op jit(solution)/shard_map/all_to_all | solution.py:115
  150.3 0.1 copy.88
  150.5 0.1 fusion.40
  150.6 0.1 copy.89
  150.7 6.9 %all_to_all.20 = bf16[2,128,256]{1,2,0:T(8,128)(2,1)S(1)} all-to-all(bf16[2,128,256]{1,2,0:T(8,128)(2,1)S(1)} %copy.89), channel_id=1, replica_groups=mesh['chip'=32,'core'=2,'mp'=4] {'core'}, dimensions={0} | all-to-all | bytes 262144 | tf_op jit(solution)/shard_map/all_to_all | solution.py:120
  157.7 0.8 copy.91
  (30 shorter events, 0.4 us)
Async XLA Ops:
  6.5 17.5 %copy-start = (f32[8,8192]{1,0:T(8,128)S(1)}, f32[8,8192]{1,0:T(8,128)}, u32[]{:S(2)}) copy-start(f32[8,8192]{1,0:T(8,128)} %param.14) | copy-start | bytes 786436
  11.4 11.4 %copy-start.7 = (f32[64,64]{1,0:T(8,128)S(1)}, f32[64,64]{1,0:T(8,128)}, u32[]{:S(2)}) copy-start(f32[64,64]{1,0:T(8,128)} %constant.33.clone) | copy-start | bytes 49156
  11.4 11.5 %copy-start.6 = (f32[64,64]{1,0:T(8,128)S(1)}, f32[64,64]{1,0:T(8,128)}, u32[]{:S(2)}) copy-start(f32[64,64]{1,0:T(8,128)} %constant.32.clone) | copy-start | bytes 49156
  11.4 11.7 %copy-start.8 = (f32[3,3,512]{2,1,0:T(4,128)S(1)}, f32[3,3,512]{2,1,0:T(4,128)}, u32[]{:S(2)}) copy-start(f32[3,3,512]{2,1,0:T(4,128)} %param.13) | copy-start | bytes 55300
  11.4 102.2 %all-to-all-start = ((bf16[64,64,768]{2,1,0:T(8,128)(2,1)}), bf16[64,64,768]{2,1,0:T(8,128)(2,1)}, u32[]{:S(2)}, u32[]{:S(2)}) async-start(bf16[64,64,768]{2,1,0:T(8,128)(2,1)} %bitcast.58), calls=%async_computation | async-start | bytes 12582912 | tf_op jit(solution)/shard_map/all_to_all | solution.py:93
  22.0 3.1 %copy-start.4 = (f32[64,256]{1,0:T(8,128)S(1)}, f32[64,256]{1,0:T(8,128)}, u32[]{:S(2)}) copy-start(f32[64,256]{1,0:T(8,128)} %constant.36.clone) | copy-start | bytes 196612
  22.0 3.1 %copy-start.5 = (f32[64,256]{1,0:T(8,128)S(1)}, f32[64,256]{1,0:T(8,128)}, u32[]{:S(2)}) copy-start(f32[64,256]{1,0:T(8,128)} %constant.37.clone) | copy-start | bytes 196612
  22.0 50.2 %all-gather.3.cloned.1.call-start = ((), (), s32[]{:S(2)}) async-start(), calls=%async_computation.4 | async-start | bytes 2359296 | tf_op jit(solution)/shard_map/all_gather | solution.py:95
  25.1 1.0 copy-start.1
  25.2 1.0 copy-start.2
  76.3 1.3 copy-start.3
  77.7 3.0 %collective-permute-start = (bf16[2,4096]{1,0:T(2,128)(2,1)S(1)}, bf16[2,4096]{1,0:T(2,128)(2,1)S(1)}, u32[]{:S(2)}, u32[]{:S(2)}) collective-permute-start(bf16[2,4096]{1,0:T(2,128)(2,1)S(1)} %slice.148), channel_id=1, source_target_pairs={{0,8},{8,16},{16,24},{24,32},{32,40},{40,48},{48,56},{56,64},{64,7... | collective-permute-start | bytes 49160 | tf_op jit(solution)/shard_map/ppermute | solution.py:16
  119.9 11.4 %all-to-all-start.1 = ((bf16[32,8,256]{2,1,0:T(8,128)(2,1)}), bf16[32,8,256]{2,1,0:T(8,128)(2,1)S(1)}, u32[]{:S(2)}, u32[]{:S(2)}) async-start(bf16[32,8,256]{2,1,0:T(8,128)(2,1)} %bitcast.19), calls=%async_computation.1 | async-start | bytes 262144 | tf_op jit(solution)/shard_map/all_to_all | solution.py:113
  137.3 5.4 %copy-start.9 = (f32[512]{0:T(512)S(1)}, f32[512]{0:T(512)}, u32[]{:S(2)}) copy-start(f32[512]{0:T(512)} %param.15) | copy-start | bytes 6148
  138.9 11.5 %all-to-all-start.2 = ((bf16[32,8,256]{2,1,0:T(8,128)(2,1)}), bf16[32,8,256]{2,1,0:T(8,128)(2,1)S(1)}, u32[]{:S(2)}, u32[]{:S(2)}) async-start(bf16[32,8,256]{2,1,0:T(8,128)(2,1)} %copy.87), calls=%async_computation.2 | async-start | bytes 262144 | tf_op jit(solution)/shard_map/all_to_all | solution.py:115
Sparse Core Ops, SparseCore 0:
  24.7 47.4 all-gather.2

commit v12 on v11

--- a/solution.py
+++ b/solution.py
@@ -6,7 +6,7 @@
 from jax.sharding import PartitionSpec as P
 
 
-HIGHEST = lax.Precision.HIGHEST
+PRECISION = lax.Precision.HIGH
 GROUP = 8
 
 
@@ -45,7 +45,7 @@
     first_re, first_im = first[..., :cols], first[..., cols:]
     turned = jnp.concatenate([first_re * tc + first_im * ts, first_im * tc - first_re * ts], axis=-1)
     matrix = block(t["inner_cos"], t["inner_sin"], -1.0)
-    return jnp.einsum("krn,nm->krm", turned, matrix, precision=HIGHEST)
+    return jnp.einsum("krn,nm->krm", turned, matrix, precision=PRECISION)
 
 
 def long_conv(signal, kernel):
@@ -54,23 +54,23 @@
     t = lax.optimization_barrier(tables(rows, cols))
     first = jnp.concatenate([t["outer_cos"][:, :live], -t["outer_sin"][:, :live]], axis=0)
     own_kernel, own_first, own_t = lax.optimization_barrier((kernel, first, t))
-    ker = jnp.einsum("kn,rnm->krm", own_first, own_kernel.reshape(channels, live, cols), precision=HIGHEST)
+    ker = jnp.einsum("kn,rnm->krm", own_first, own_kernel.reshape(channels, live, cols), precision=PRECISION)
     ker = jnp.concatenate([ker[:rows], ker[rows:]], axis=-1)
     sh = forward(ker, own_t, cols)
-    sig = jnp.einsum("kn,nrm->krm", first, signal.astype(jnp.float32), precision=HIGHEST)
+    sig = jnp.einsum("kn,nrm->krm", first, signal.astype(jnp.float32), precision=PRECISION)
     sig = jnp.concatenate([sig[:rows], sig[rows:]], axis=-1)
     su = forward(sig, t, cols)
     su_re, su_im = su[..., :cols], su[..., cols:]
     sh_re, sh_im = sh[..., :cols], sh[..., cols:]
     z = jnp.concatenate([su_re * sh_re - su_im * sh_im, su_re * sh_im + su_im * sh_re], axis=-1)
-    d = jnp.einsum("krn,nm->krm", z, block(t["inner_cos"], t["inner_sin"], 1.0), precision=HIGHEST)
+    d = jnp.einsum("krn,nm->krm", z, block(t["inner_cos"], t["inner_sin"], 1.0), precision=PRECISION)
     d_re, d_im = d[..., :cols], d[..., cols:]
     tc = t["twist_cos"][:, None, :]
     ts = t["twist_sin"][:, None, :]
     e = jnp.concatenate([d_re * tc - d_im * ts, d_im * tc + d_re * ts], axis=0)
     scale = 1.0 / (rows * cols)
     back = jnp.concatenate([t["outer_cos"][:live], -t["outer_sin"][:live]], axis=1) * scale
-    return jnp.einsum("nk,krm->nrm", back, e, precision=HIGHEST)
+    return jnp.einsum("nk,krm->nrm", back, e, precision=PRECISION)
 
 
 def pick(values, axis, parity):

time: 166 us -> 164 us (0.988)
  matrix products: 14.8 us -> 11.3 us
    dot_general x4, matrix products: 6.05 us -> 3.91 us  [the longest x2 3 us: forward(): return jnp.einsum('krn,nm->krm', turned, matrix, precision=PRECISION)]
  transfers between devices with their start and end apart: 5 -> 5, of which waited for: 5 -> 5; matrix products, arithmetic and copies ran while one was open for 6% -> 5% of each run, Pallas kernels for 0% -> 0%
where the time goes in v12:
time: 164 us; the launch traced here: 163 us
  waiting for transfers between devices  94 us (57%)
  starting transfers between devices  20.7 us (13%)
  local copies, waits for them, and re-layouts  14.9 us (9%)
  between operations  13.8 us (8%)
  matrix products  11.3 us (7%)
  blocking collectives  6.95 us (4%)
    all_gather x1, waiting for transfers between devices, layer(): stacked = lax.all_gather(tokens, ('core', 'mp'), axis=0, tiled=False)  44.9 us
    all_to_all x1, waiting for transfers between devices, layer(): lax.all_to_all(spread, ('chip', 'core'), split_axis=0, concat_axis=0, til...  32.9 us
    all_to_all x1, starting transfers between devices, layer(): lax.all_to_all(spread, ('chip', 'core'), split_axis=0, concat_axis=0, til...  10.6 us
    all_to_all x1, waiting for transfers between devices, layer(): lax.all_to_all(outgoing, 'chip', split_axis=0, concat_axis=0, tiled=True)  7.34 us
    all_to_all x1, waiting for transfers between devices, layer(): lax.all_to_all(convolved, 'chip', split_axis=0, concat_axis=0, tiled=True)  7.31 us
    all_to_all x1, blocking collectives, layer(): lax.all_to_all(local, 'core', split_axis=0, concat_axis=0, tiled=True)  6.95 us
    dot_general x1, matrix products, layer(): jnp.dot(extended_tokens, weights, preferred_element_type=jnp.float32)  5.29 us
    unnamed x22, local copies, waits for them, and re-layouts  4.14 us
  transfers between devices with their start and end apart: 5, of which 5 were waited for; matrix products, arithmetic and copies ran while one was open for 5% of the time, Pallas kernels for 0%

profile of v12, /device:TPU:1, one launch (start us, length us, event | category | flops | bytes accessed | tf_op | source)
XLA Modules:
  0.0 163.2 jit_solution(13958761660320774570)
XLA Ops:
  6.5 1.2 copy.75
  7.7 0.1 copy.76
  7.8 0.2 copy.77
  8.0 3.4 %broadcast_in_dim.5 = bf16[32,2,64,768]{3,2,1,0:T(8,128)(2,1)} broadcast(bf16[2,64,768]{2,1,0:T(8,128)(2,1)S(1)} %copy.77), dimensions={1,2,3} | broadcast | bytes 6488064 | tf_op jit(solution)/shard_map/broadcast_in_dim | solution.py:92
  11.4 10.6 %all-to-all-start = ((bf16[64,64,768]{2,1,0:T(8,128)(2,1)}), bf16[64,64,768]{2,1,0:T(8,128)(2,1)}, u32[]{:S(2)}, u32[]{:S(2)}) async-start(bf16[64,64,768]{2,1,0:T(8,128)(2,1)} %bitcast.58), calls=%async_computation | async-start | bytes 12582912 | tf_op jit(solution)/shard_map/all_to_all | solution.py:93
  22.1 0.7 all-gather.3.cloned.1.call-update
  22.8 0.1 copy.79
  22.9 0.1 copy.78
  22.9 0.1 pad_maximum_fusion.9
  23.0 0.5 reshape.60
  23.5 0.4 dynamic-slice_reduce_fusion
  23.9 0.1 reshape.61
  24.1 0.6 fusion.42
  24.8 0.1 multiply_add_fusion.2
  24.9 0.1 pad_maximum_fusion.7
  25.0 0.6 copy-done.1
  25.8 1.5 fusion.17
  27.3 44.9 %all-gather.3.cloned.1.call-done = bf16[1024,1024]{1,0:T(8,128)(2,1)} async-done(((bf16[128,1024]{1,0:T(8,128)(2,1)}), bf16[1024,1024]{1,0:T(8,128)(2,1)}) %all-gather.3.cloned.1.call-update) | async-done | bytes 2097168 | tf_op jit(solution)/shard_map/all_gather | solution.py:95
  72.2 3.2 %copy.74 = bf16[2,4,128,1024]{3,1,2,0:T(4,128)(2,1)S(1)} copy(bf16[2,4,128,1024]{3,2,1,0:T(8,128)(2,1)} %bitcast.62) | data formatting | bytes 4194304 | tf_op jit(solution)/shard_map/reshape | solution.py:97
  75.4 0.9 copy.94
  76.3 1.3 copy-done.3
  77.7 2.1 %collective-permute-start = (bf16[2,4096]{1,0:T(2,128)(2,1)S(1)}, bf16[2,4096]{1,0:T(2,128)(2,1)S(1)}, u32[]{:S(2)}, u32[]{:S(2)}) collective-permute-start(bf16[2,4096]{1,0:T(2,128)(2,1)S(1)} %slice.148), channel_id=1, source_target_pairs={{0,8},{8,16},{16,24},{24,32},{32,40},{40,48},{48,56},{56,64},{64,7... | collective-permute-start | bytes 49160 | tf_op jit(solution)/shard_map/ppermute | solution.py:16
  79.8 0.8 collective-permute-done
  80.6 32.9 %all-to-all-done = bf16[64,64,768]{2,1,0:T(8,128)(2,1)} async-done(((bf16[64,64,768]{2,1,0:T(8,128)(2,1)}), bf16[64,64,768]{2,1,0:T(8,128)(2,1)}, u32[]{:S(2)}, u32[]{:S(2)}) %all-to-all-start) | async-done | bytes 6291488 | tf_op jit(solution)/shard_map/all_to_all | solution.py:93
  113.6 5.3 %fusion.4 = bf16[258,768]{1,0:T(8,128)(2,1)S(1)} fusion(bf16[4096,768]{1,0:T(8,128)(2,1)} %bitcast.7, bf16[256,4096]{1,0:T(8,128)(2,1)} %bitcast.61, bf16[2,4096]{1,0:T(2,128)(2,1)S(1)} %collective-permute-done), kind=kOutput, calls=%fused_computation.8 | convolution fusion | flops 1627620864 | bytes 8801280 | tf_op jit(solution)/shard_map/dot_general | solution.py:102
  118.9 0.2 fusion.34
  119.1 0.8 copy.80
  119.9 4.0 %all-to-all-start.1 = ((bf16[32,8,256]{2,1,0:T(8,128)(2,1)}), bf16[32,8,256]{2,1,0:T(8,128)(2,1)S(1)}, u32[]{:S(2)}, u32[]{:S(2)}) async-start(bf16[32,8,256]{2,1,0:T(8,128)(2,1)} %bitcast.19), calls=%async_computation.1 | async-start | bytes 262144 | tf_op jit(solution)/shard_map/all_to_all | solution.py:113
  124.0 7.3 %all-to-all-done.1 = bf16[32,8,256]{2,1,0:T(8,128)(2,1)S(1)} async-done(((bf16[32,8,256]{2,1,0:T(8,128)(2,1)}), bf16[32,8,256]{2,1,0:T(8,128)(2,1)S(1)}, u32[]{:S(2)}, u32[]{:S(2)}) %all-to-all-start.1) | async-done | bytes 131104 | tf_op jit(solution)/shard_map/all_to_all | solution.py:113
  131.3 0.5 fusion.44
  131.8 0.1 multiply_add_fusion.3
  132.0 0.1 pad_maximum_fusion.6
  132.1 1.5 fusion.9
  133.6 0.1 multiply_subtract_fusion.1
  133.7 0.1 pad_maximum_fusion.8
  133.9 1.5 fusion.13
  135.4 0.1 multiply_subtract_fusion
  135.5 0.4 convolution_convert_fusion
  136.0 0.7 copy.87
  136.7 3.9 %all-to-all-start.2 = ((bf16[32,8,256]{2,1,0:T(8,128)(2,1)}), bf16[32,8,256]{2,1,0:T(8,128)(2,1)S(1)}, u32[]{:S(2)}, u32[]{:S(2)}) async-start(bf16[32,8,256]{2,1,0:T(8,128)(2,1)} %copy.87), calls=%async_computation.2 | async-start | bytes 262144 | tf_op jit(solution)/shard_map/all_to_all | solution.py:115
  140.6 0.1 reshape.69
  140.8 0.1 mul.263
  140.9 7.3 %all-to-all-done.2 = bf16[32,8,256]{2,1,0:T(8,128)(2,1)S(1)} async-done(((bf16[32,8,256]{2,1,0:T(8,128)(2,1)}), bf16[32,8,256]{2,1,0:T(8,128)(2,1)S(1)}, u32[]{:S(2)}, u32[]{:S(2)}) %all-to-all-start.2) | async-done | bytes 131104 | tf_op jit(solution)/shard_map/all_to_all | solution.py:115
  148.2 0.1 copy.88
  148.3 0.1 fusion.40
  148.5 0.1 copy.89
  148.6 7.0 %all_to_all.20 = bf16[2,128,256]{1,2,0:T(8,128)(2,1)S(1)} all-to-all(bf16[2,128,256]{1,2,0:T(8,128)(2,1)S(1)} %copy.89), channel_id=1, replica_groups=mesh['chip'=32,'core'=2,'mp'=4] {'core'}, dimensions={0} | all-to-all | bytes 262144 | tf_op jit(solution)/shard_map/all_to_all | solution.py:120
  155.6 0.8 copy.91
  (30 shorter events, 0.4 us)
Async XLA Ops:
  6.5 17.5 %copy-start = (f32[8,8192]{1,0:T(8,128)S(1)}, f32[8,8192]{1,0:T(8,128)}, u32[]{:S(2)}) copy-start(f32[8,8192]{1,0:T(8,128)} %param.14) | copy-start | bytes 786436
  11.4 11.4 %copy-start.7 = (f32[64,64]{1,0:T(8,128)S(1)}, f32[64,64]{1,0:T(8,128)}, u32[]{:S(2)}) copy-start(f32[64,64]{1,0:T(8,128)} %constant.33.clone) | copy-start | bytes 49156
  11.4 11.5 %copy-start.6 = (f32[64,64]{1,0:T(8,128)S(1)}, f32[64,64]{1,0:T(8,128)}, u32[]{:S(2)}) copy-start(f32[64,64]{1,0:T(8,128)} %constant.32.clone) | copy-start | bytes 49156
  11.4 11.7 %copy-start.8 = (f32[3,3,512]{2,1,0:T(4,128)S(1)}, f32[3,3,512]{2,1,0:T(4,128)}, u32[]{:S(2)}) copy-start(f32[3,3,512]{2,1,0:T(4,128)} %param.13) | copy-start | bytes 55300
  11.4 102.2 %all-to-all-start = ((bf16[64,64,768]{2,1,0:T(8,128)(2,1)}), bf16[64,64,768]{2,1,0:T(8,128)(2,1)}, u32[]{:S(2)}, u32[]{:S(2)}) async-start(bf16[64,64,768]{2,1,0:T(8,128)(2,1)} %bitcast.58), calls=%async_computation | async-start | bytes 12582912 | tf_op jit(solution)/shard_map/all_to_all | solution.py:93
  22.0 2.7 %copy-start.4 = (f32[64,256]{1,0:T(8,128)S(1)}, f32[64,256]{1,0:T(8,128)}, u32[]{:S(2)}) copy-start(f32[64,256]{1,0:T(8,128)} %constant.36.clone) | copy-start | bytes 196612
  22.0 2.7 %copy-start.5 = (f32[64,256]{1,0:T(8,128)S(1)}, f32[64,256]{1,0:T(8,128)}, u32[]{:S(2)}) copy-start(f32[64,256]{1,0:T(8,128)} %constant.37.clone) | copy-start | bytes 196612
  22.0 50.2 %all-gather.3.cloned.1.call-start = ((), (), s32[]{:S(2)}) async-start(), calls=%async_computation.4 | async-start | bytes 2359296 | tf_op jit(solution)/shard_map/all_gather | solution.py:95
  24.7 1.0 copy-start.1
  24.7 1.0 copy-start.2
  76.3 1.3 copy-start.3
  77.7 3.0 %collective-permute-start = (bf16[2,4096]{1,0:T(2,128)(2,1)S(1)}, bf16[2,4096]{1,0:T(2,128)(2,1)S(1)}, u32[]{:S(2)}, u32[]{:S(2)}) collective-permute-start(bf16[2,4096]{1,0:T(2,128)(2,1)S(1)} %slice.148), channel_id=1, source_target_pairs={{0,8},{8,16},{16,24},{24,32},{32,40},{40,48},{48,56},{56,64},{64,7... | collective-permute-start | bytes 49160 | tf_op jit(solution)/shard_map/ppermute | solution.py:16
  119.9 11.4 %all-to-all-start.1 = ((bf16[32,8,256]{2,1,0:T(8,128)(2,1)}), bf16[32,8,256]{2,1,0:T(8,128)(2,1)S(1)}, u32[]{:S(2)}, u32[]{:S(2)}) async-start(bf16[32,8,256]{2,1,0:T(8,128)(2,1)} %bitcast.19), calls=%async_computation.1 | async-start | bytes 262144 | tf_op jit(solution)/shard_map/all_to_all | solution.py:113
  135.4 5.2 %copy-start.9 = (f32[512]{0:T(512)S(1)}, f32[512]{0:T(512)}, u32[]{:S(2)}) copy-start(f32[512]{0:T(512)} %param.15) | copy-start | bytes 6148
  136.7 11.5 %all-to-all-start.2 = ((bf16[32,8,256]{2,1,0:T(8,128)(2,1)}), bf16[32,8,256]{2,1,0:T(8,128)(2,1)S(1)}, u32[]{:S(2)}, u32[]{:S(2)}) async-start(bf16[32,8,256]{2,1,0:T(8,128)(2,1)} %copy.87), calls=%async_computation.2 | async-start | bytes 262144 | tf_op jit(solution)/shard_map/all_to_all | solution.py:115
Sparse Core Ops, SparseCore 0:
  24.7 47.4 all-gather.2

commit v13 on v12

--- a/solution.py
+++ b/solution.py
@@ -88,9 +88,11 @@
     chips = lax.axis_size("chip")
     parity = lax.axis_index("core")
     split = w_proj.reshape(w_proj.shape[0], 3, width // (2 * GROUP), 2, GROUP)
-    split = jnp.transpose(split, (3, 0, 1, 2, 4)).reshape(1, 2, w_proj.shape[0], 3 * half)
-    spread = jnp.broadcast_to(split, (chips,) + split.shape[1:]).reshape((2 * chips,) + split.shape[2:])
-    arrived = lax.all_to_all(spread, ("chip", "core"), split_axis=0, concat_axis=0, tiled=True)
+    split = jnp.transpose(split, (3, 0, 1, 2, 4)).reshape(2, w_proj.shape[0], 3 * half)
+    paired = lax.all_to_all(split, "core", split_axis=0, concat_axis=0, tiled=True)
+    paired = paired.reshape(1, 2 * w_proj.shape[0], 3 * half)
+    spread = jnp.broadcast_to(paired, (chips,) + paired.shape[1:])
+    arrived = lax.all_to_all(spread, "chip", split_axis=0, concat_axis=0, tiled=True)
     weights = arrived.reshape(2 * chips * w_proj.shape[0], 3 * half)
     stacked = lax.all_gather(tokens, ("core", "mp"), axis=0, tiled=False)
     rows = 2 * rows_dev

time: 164 us -> 183 us (1.12)
  waiting for transfers between devices: 94 us -> 106 us
  blocking collectives: 6.95 us -> 14.2 us
    all_to_all x1, waiting for transfers between devices: 32.9 us -> 43.2 us  [layer(): lax.all_to_all(spread, 'chip', split_axis=0, concat_axis=0, tiled=True)]
    all_to_all x0 -> x1, blocking collectives: none -> 6.73 us  [layer(): lax.all_to_all(split, 'core', split_axis=0, concat_axis=0, tiled=True)]
    all_to_all x1, starting transfers between devices: 10.6 us -> 6.93 us  [layer(): lax.all_to_all(spread, 'chip', split_axis=0, concat_axis=0, tiled=True)]
    all_to_all x1, starting transfers between devices: 4.04 us -> 6.29 us  [layer(): lax.all_to_all(outgoing, 'chip', split_axis=0, concat_axis=0, tiled=True)]
    ppermute x1, waiting for transfers between devices: 0.83 us -> 3.08 us  [shifted(): lax.ppermute(value, axis, [(source, source + steps) for source in range(l...]
  transfers between devices with their start and end apart: 5 -> 5, of which waited for: 5 -> 5; matrix products, arithmetic and copies ran while one was open for 5% -> 4% of each run, Pallas kernels for 0% -> 0%
where the time goes in v13:
time: 183 us; the launch traced here: 182 us
  waiting for transfers between devices  106 us (58%)
  starting transfers between devices  20.2 us (11%)
  local copies, waits for them, and re-layouts  14.9 us (8%)
  blocking collectives  14.2 us (8%)
  between operations  13.8 us (8%)
  matrix products  11.3 us (6%)
    all_gather x1, waiting for transfers between devices, layer(): stacked = lax.all_gather(tokens, ('core', 'mp'), axis=0, tiled=False)  44.2 us
    all_to_all x1, waiting for transfers between devices, layer(): lax.all_to_all(spread, 'chip', split_axis=0, concat_axis=0, tiled=True)  43.2 us
    all_to_all x1, blocking collectives, layer(): lax.all_to_all(local, 'core', split_axis=0, concat_axis=0, tiled=True)  7.47 us
    all_to_all x1, waiting for transfers between devices, layer(): lax.all_to_all(outgoing, 'chip', split_axis=0, concat_axis=0, tiled=True)  7.34 us
    all_to_all x1, waiting for transfers between devices, layer(): lax.all_to_all(convolved, 'chip', split_axis=0, concat_axis=0, tiled=True)  7.29 us
    all_to_all x1, starting transfers between devices, layer(): lax.all_to_all(spread, 'chip', split_axis=0, concat_axis=0, tiled=True)  6.93 us
    all_to_all x1, blocking collectives, layer(): lax.all_to_all(split, 'core', split_axis=0, concat_axis=0, tiled=True)  6.73 us
    all_to_all x1, starting transfers between devices, layer(): lax.all_to_all(outgoing, 'chip', split_axis=0, concat_axis=0, tiled=True)  6.29 us
  transfers between devices with their start and end apart: 5, of which 5 were waited for; matrix products, arithmetic and copies ran while one was open for 4% of the time, Pallas kernels for 0%

profile of v13, /device:TPU:1, one launch (start us, length us, event | category | flops | bytes accessed | tf_op | source)
XLA Modules:
  0.0 181.7 jit_solution(3656600551810883326)
XLA Ops:
  6.5 1.2 copy.91
  7.7 0.1 copy.92
  7.8 0.2 copy.93
  8.0 6.7 %all_to_all.25 = bf16[2,64,768]{2,1,0:T(8,128)(2,1)S(1)} all-to-all(bf16[2,64,768]{2,1,0:T(8,128)(2,1)S(1)} %copy.93), channel_id=1, replica_groups=mesh['chip'=32,'core'=2,'mp'=4] {'core'}, dimensions={0} | all-to-all | bytes 393216 | tf_op jit(solution)/shard_map/all_to_all | solution.py:92
  14.7 3.3 %broadcast_in_dim.5 = bf16[32,128,768]{2,1,0:T(8,128)(2,1)} broadcast(bf16[128,768]{1,0:T(8,128)(2,1)S(1)} %bitcast.65), dimensions={1,2} | broadcast | bytes 6488064 | tf_op jit(solution)/shard_map/broadcast_in_dim | solution.py:94
  18.1 6.9 %all-to-all-start.1 = ((bf16[32,128,768]{2,1,0:T(8,128)(2,1)}), bf16[32,128,768]{2,1,0:T(8,128)(2,1)}, u32[]{:S(2)}, u32[]{:S(2)}) async-start(bf16[32,128,768]{2,1,0:T(8,128)(2,1)} %broadcast_in_dim.5), calls=%async_computation.1 | async-start | bytes 12582912 | tf_op jit(solution)/shard_map/all_to_all | solution.py:95
  25.1 0.7 all-gather.3.cloned.1.call-update
  25.8 0.1 copy.94
  25.9 0.1 pad_maximum_fusion.9
  26.0 0.5 reshape.60
  26.5 0.4 dynamic-slice_reduce_fusion
  26.9 0.1 reshape.61
  27.1 0.6 fusion.42
  27.7 0.1 multiply_add_fusion.2
  27.9 0.1 pad_maximum_fusion.7
  28.0 0.6 copy-done.1
  28.7 1.5 fusion.17
  30.2 44.2 %all-gather.3.cloned.1.call-done = bf16[1024,1024]{1,0:T(8,128)(2,1)} async-done(((bf16[128,1024]{1,0:T(8,128)(2,1)}), bf16[1024,1024]{1,0:T(8,128)(2,1)}) %all-gather.3.cloned.1.call-update) | async-done | bytes 2097168 | tf_op jit(solution)/shard_map/all_gather | solution.py:97
  74.4 3.2 %copy.90 = bf16[2,4,128,1024]{3,1,2,0:T(4,128)(2,1)S(1)} copy(bf16[2,4,128,1024]{3,2,1,0:T(8,128)(2,1)} %bitcast.61) | data formatting | bytes 4194304 | tf_op jit(solution)/shard_map/reshape | solution.py:99
  77.6 0.9 copy.110
  78.5 1.3 copy-done.3
  79.9 3.1 %collective-permute-start = (bf16[2,4096]{1,0:T(2,128)(2,1)S(1)}, bf16[2,4096]{1,0:T(2,128)(2,1)S(1)}, u32[]{:S(2)}, u32[]{:S(2)}) collective-permute-start(bf16[2,4096]{1,0:T(2,128)(2,1)S(1)} %slice.148), channel_id=1, source_target_pairs={{0,8},{8,16},{16,24},{24,32},{32,40},{40,48},{48,56},{56,64},{64,7... | collective-permute-start | bytes 49160 | tf_op jit(solution)/shard_map/ppermute | solution.py:16
  83.0 3.1 %collective-permute-done = bf16[2,4096]{1,0:T(2,128)(2,1)S(1)} collective-permute-done((bf16[2,4096]{1,0:T(2,128)(2,1)S(1)}, bf16[2,4096]{1,0:T(2,128)(2,1)S(1)}, u32[]{:S(2)}, u32[]{:S(2)}) %collective-permute-start) | collective-permute-done | bytes 16416 | tf_op jit(solution)/shard_map/ppermute | solution.py:16
  86.1 43.2 %all-to-all-done.1 = bf16[32,128,768]{2,1,0:T(8,128)(2,1)} async-done(((bf16[32,128,768]{2,1,0:T(8,128)(2,1)}), bf16[32,128,768]{2,1,0:T(8,128)(2,1)}, u32[]{:S(2)}, u32[]{:S(2)}) %all-to-all-start.1) | async-done | bytes 6291488 | tf_op jit(solution)/shard_map/all_to_all | solution.py:95
  129.3 5.3 %fusion.4 = bf16[258,768]{1,0:T(8,128)(2,1)S(1)} fusion(bf16[4096,768]{1,0:T(8,128)(2,1)} %bitcast.7, bf16[256,4096]{1,0:T(8,128)(2,1)} %bitcast.60, bf16[2,4096]{1,0:T(2,128)(2,1)S(1)} %collective-permute-done), kind=kOutput, calls=%fused_computation.8 | convolution fusion | flops 1627620864 | bytes 8801280 | tf_op jit(solution)/shard_map/dot_general | solution.py:104
  134.7 0.2 fusion.34
  134.9 0.8 copy.96
  135.6 6.3 %all-to-all-start.2 = ((bf16[32,8,256]{2,1,0:T(8,128)(2,1)}), bf16[32,8,256]{2,1,0:T(8,128)(2,1)S(1)}, u32[]{:S(2)}, u32[]{:S(2)}) async-start(bf16[32,8,256]{2,1,0:T(8,128)(2,1)} %bitcast.19), calls=%async_computation.2 | async-start | bytes 262144 | tf_op jit(solution)/shard_map/all_to_all | solution.py:115
  142.0 7.3 %all-to-all-done.2 = bf16[32,8,256]{2,1,0:T(8,128)(2,1)S(1)} async-done(((bf16[32,8,256]{2,1,0:T(8,128)(2,1)}), bf16[32,8,256]{2,1,0:T(8,128)(2,1)S(1)}, u32[]{:S(2)}, u32[]{:S(2)}) %all-to-all-start.2) | async-done | bytes 131104 | tf_op jit(solution)/shard_map/all_to_all | solution.py:115
  149.3 0.5 fusion.44
  149.8 0.1 multiply_add_fusion.3
  149.9 0.1 pad_maximum_fusion.6
  150.1 1.5 fusion.9
  151.6 0.1 multiply_subtract_fusion.1
  151.7 0.1 pad_maximum_fusion.8
  151.9 1.5 fusion.13
  153.4 0.1 multiply_subtract_fusion
  153.5 0.4 convolution_convert_fusion
  154.0 0.7 copy.103
  154.7 3.9 %all-to-all-start.3 = ((bf16[32,8,256]{2,1,0:T(8,128)(2,1)}), bf16[32,8,256]{2,1,0:T(8,128)(2,1)S(1)}, u32[]{:S(2)}, u32[]{:S(2)}) async-start(bf16[32,8,256]{2,1,0:T(8,128)(2,1)} %copy.103), calls=%async_computation.3 | async-start | bytes 262144 | tf_op jit(solution)/shard_map/all_to_all | solution.py:117
  158.6 0.1 reshape.69
  158.8 0.1 mul.263
  158.8 7.3 %all-to-all-done.3 = bf16[32,8,256]{2,1,0:T(8,128)(2,1)S(1)} async-done(((bf16[32,8,256]{2,1,0:T(8,128)(2,1)}), bf16[32,8,256]{2,1,0:T(8,128)(2,1)S(1)}, u32[]{:S(2)}, u32[]{:S(2)}) %all-to-all-start.3) | async-done | bytes 131104 | tf_op jit(solution)/shard_map/all_to_all | solution.py:117
  166.2 0.1 copy.104
  166.3 0.1 fusion.40
  166.4 0.1 copy.105
  166.6 7.5 %all_to_all.26 = bf16[2,128,256]{1,2,0:T(8,128)(2,1)S(1)} all-to-all(bf16[2,128,256]{1,2,0:T(8,128)(2,1)S(1)} %copy.105), channel_id=1, replica_groups=mesh['chip'=32,'core'=2,'mp'=4] {'core'}, dimensions={0} | all-to-all | bytes 262144 | tf_op jit(solution)/shard_map/all_to_all | solution.py:122
  174.0 0.8 copy.107
  (31 shorter events, 0.5 us)
Async XLA Ops:
  6.5 20.5 %copy-start = (f32[8,8192]{1,0:T(8,128)S(1)}, f32[8,8192]{1,0:T(8,128)}, u32[]{:S(2)}) copy-start(f32[8,8192]{1,0:T(8,128)} %param.14) | copy-start | bytes 786436
  18.0 7.7 %copy-start.7 = (f32[64,64]{1,0:T(8,128)S(1)}, f32[64,64]{1,0:T(8,128)}, u32[]{:S(2)}) copy-start(f32[64,64]{1,0:T(8,128)} %constant.33.clone) | copy-start | bytes 49156
  18.0 7.8 %copy-start.6 = (f32[64,64]{1,0:T(8,128)S(1)}, f32[64,64]{1,0:T(8,128)}, u32[]{:S(2)}) copy-start(f32[64,64]{1,0:T(8,128)} %constant.32.clone) | copy-start | bytes 49156
  18.0 8.0 %copy-start.8 = (f32[3,3,512]{2,1,0:T(4,128)S(1)}, f32[3,3,512]{2,1,0:T(4,128)}, u32[]{:S(2)}) copy-start(f32[3,3,512]{2,1,0:T(4,128)} %param.13) | copy-start | bytes 55300
  18.1 111.3 %all-to-all-start.1 = ((bf16[32,128,768]{2,1,0:T(8,128)(2,1)}), bf16[32,128,768]{2,1,0:T(8,128)(2,1)}, u32[]{:S(2)}, u32[]{:S(2)}) async-start(bf16[32,128,768]{2,1,0:T(8,128)(2,1)} %broadcast_in_dim.5), calls=%async_computation.1 | async-start | bytes 12582912 | tf_op jit(solution)/shard_map/all_to_all | solution.py:95
  25.0 2.7 %copy-start.4 = (f32[64,256]{1,0:T(8,128)S(1)}, f32[64,256]{1,0:T(8,128)}, u32[]{:S(2)}) copy-start(f32[64,256]{1,0:T(8,128)} %constant.36.clone) | copy-start | bytes 196612
  25.0 2.7 %copy-start.5 = (f32[64,256]{1,0:T(8,128)S(1)}, f32[64,256]{1,0:T(8,128)}, u32[]{:S(2)}) copy-start(f32[64,256]{1,0:T(8,128)} %constant.37.clone) | copy-start | bytes 196612
  25.0 49.4 %all-gather.3.cloned.1.call-start = ((), (), s32[]{:S(2)}) async-start(), calls=%async_computation.5 | async-start | bytes 2359296 | tf_op jit(solution)/shard_map/all_gather | solution.py:97
  27.7 1.0 copy-start.1
  27.7 1.0 copy-start.2
  78.5 1.3 copy-start.3
  79.9 6.2 %collective-permute-start = (bf16[2,4096]{1,0:T(2,128)(2,1)S(1)}, bf16[2,4096]{1,0:T(2,128)(2,1)S(1)}, u32[]{:S(2)}, u32[]{:S(2)}) collective-permute-start(bf16[2,4096]{1,0:T(2,128)(2,1)S(1)} %slice.148), channel_id=1, source_target_pairs={{0,8},{8,16},{16,24},{24,32},{32,40},{40,48},{48,56},{56,64},{64,7... | collective-permute-start | bytes 49160 | tf_op jit(solution)/shard_map/ppermute | solution.py:16
  135.6 13.7 %all-to-all-start.2 = ((bf16[32,8,256]{2,1,0:T(8,128)(2,1)}), bf16[32,8,256]{2,1,0:T(8,128)(2,1)S(1)}, u32[]{:S(2)}, u32[]{:S(2)}) async-start(bf16[32,8,256]{2,1,0:T(8,128)(2,1)} %bitcast.19), calls=%async_computation.2 | async-start | bytes 262144 | tf_op jit(solution)/shard_map/all_to_all | solution.py:115
  153.4 5.2 %copy-start.9 = (f32[512]{0:T(512)S(1)}, f32[512]{0:T(512)}, u32[]{:S(2)}) copy-start(f32[512]{0:T(512)} %param.15) | copy-start | bytes 6148
  154.7 11.4 %all-to-all-start.3 = ((bf16[32,8,256]{2,1,0:T(8,128)(2,1)}), bf16[32,8,256]{2,1,0:T(8,128)(2,1)S(1)}, u32[]{:S(2)}, u32[]{:S(2)}) async-start(bf16[32,8,256]{2,1,0:T(8,128)(2,1)} %copy.103), calls=%async_computation.3 | async-start | bytes 262144 | tf_op jit(solution)/shard_map/all_to_all | solution.py:117
Sparse Core Ops, SparseCore 0:
  27.7 46.6 all-gather.2
